TPU v7x, 32 devices: a whole 2x2x4 slice. The times are simulated.
32 devices in a mesh: groups: 2 (over y), col: 4 (over z), aux: 2 (over x), rep: 2 (over core).
Axes of the slice: x: 2, y: 2, z: 4, core: 2. Of those that a mesh axis runs over, the one named last changes fastest.
Arguments:
- b_aux: bfloat16 [4, 4096, 2400], P(('groups', 'aux'), ('col', 'rep')), parts along dimension 0, may hold values from -0.59765625 to 0.59765625
- occ_energies: float32 [2], P('groups'), parts along dimension 0, may hold values from -2 to -0.3
- vir_energies: float32 [4800], P('groups'), parts along dimension 0, may hold values from 0.2 to 3
- owners: int32 [2], replicated, may hold values from 0 to 7
Outputs:
- gamma: float32 [4, 4096, 2400], P(('groups', 'aux'), None, ('col', 'rep')), parts along dimension 0
There are 2 independent parts, one for each index of `groups`. A program takes and returns all parts, laid end to end along the dimension named above; an argument that names none is the same for every part. Nothing has to cross between parts.
Inputs may be any that keep to these rules, and one draw needn't show every extreme that they name: owners[s] is a column shard index in the order of col+rep; owners may repeat.
All inputs are finite; a program needn't handle non-finite values.
Results may differ from a plain program's by a relative error of at most 0.003.
Values may be sent and summed in bfloat16 or wider, within the bound.
No kernel may reach another device: no remote copies, remote signals or barrier semaphores. Data moves between devices by JAX's collectives and lax.ppermute only.
A program may use at most 64 MiB of HBM per device.

v0:
```python
import jax
import jax.numpy as jnp
from jax import lax
from jax.sharding import PartitionSpec as P

os_scale = 1.3


def from_root(value, axis, source):
    kept = jnp.where(lax.axis_index(axis) == source, value, 0).astype(value.dtype)
    return lax.psum(kept, axis)


def column_energy(first, occ_energies, vir_energies, width):
    nvirt = vir_energies.shape[0]
    occ_value = lax.dynamic_index_in_dim(occ_energies, first // nvirt, 0, keepdims=False)
    vir_values = lax.dynamic_slice_in_dim(vir_energies, first % nvirt, width, 0)
    return vir_values - occ_value


def body(b_aux, occ_energies, vir_energies, owners):
    moved = lax.all_to_all(b_aux, ("col", "rep"), split_axis=2, concat_axis=1, tiled=True)
    local_cols = moved[0]
    width = local_cols.shape[1]
    shard_index = lax.axis_index(("col", "rep"))
    energy_mine = column_energy(shard_index * width, occ_energies, vir_energies, width)
    gamma_acc = jnp.zeros(local_cols.shape, jnp.float32)
    for step_index in range(owners.shape[0]):
        owner_shard = owners[step_index]
        owner_cols = from_root(local_cols, ("col", "rep"), owner_shard)
        owner_energy = column_energy(owner_shard * width, occ_energies, vir_energies, width)
        denominator = energy_mine[:, None] + owner_energy[None, :]
        partial_value = lax.dot_general(
            local_cols, owner_cols, (((0,), (0,)), ((), ())), preferred_element_type=jnp.float32
        )
        coupling = lax.psum(partial_value, "aux")
        amplitude = (os_scale * coupling / denominator).astype(jnp.bfloat16)
        gamma_acc = gamma_acc + lax.dot_general(
            owner_cols, amplitude, (((1,), (1,)), ((), ())), preferred_element_type=jnp.float32
        )
    return gamma_acc[None]


def solution(mesh):
    placed = (P(("groups", "aux"), ("col", "rep"), None), P("groups"), P("groups"), P())
    return jax.shard_map(
        body,
        mesh=mesh,
        in_specs=placed,
        out_specs=P(("groups", "aux"), None, ("col", "rep")),
        check_vma=False,
    )
```

profile of v0, /device:TPU:0, one launch (start us, length us, event | category | flops | bytes accessed | tf_op | source)
XLA Modules:
  0.0 311.1 jit_solution(7487857900732730221)
XLA Ops:
  6.5 13.4 %copy.16 = bf16[1,512,2400]{1,0,2:T(2,128)(2,1)} copy(bf16[1,512,2400]{1,2,0:T(8,128)(2,1)} %param.4) | data formatting | bytes 4915200 | tf_op args[0]
  20.0 0.6 broadcast.16
  20.6 16.3 %reduce.2 = bf16[2400,512]{1,0:T(8,128)(2,1)S(1)} reduce(bf16[2400,1,512]{2,1,0:T(2,128)(2,1)} %bitcast.32, bf16[]{:T(256)} %broadcast.16), dimensions={1}, to_apply=%bitcast.30.reduce_sub_computation | reduce | bytes 4915202
  36.9 2.4 reshape.5
  39.3 0.0 copy-start.4
  39.3 6.5 %all-to-all-start = ((bf16[8,2,76800]{2,1,0:T(2,128)(2,1)}), bf16[8,2,76800]{2,1,0:T(2,128)(2,1)S(1)}, u32[]{:S(2)}, u32[]{:S(2)}) async-start(bf16[8,2,76800]{2,1,0:T(2,128)(2,1)} %reshape.5), calls=%async_computation | async-start | bytes 4915200 | tf_op jit(solution)/shard_map/all_to_all | solution.py:22
  45.7 0.0 all-reduce.7.cloned.1.call-start
  45.8 0.0 copy-done.4
  45.8 0.6 fusion.10
  47.7 54.8 %all-to-all-done = bf16[8,2,76800]{2,1,0:T(2,128)(2,1)S(1)} async-done(((bf16[8,2,76800]{2,1,0:T(2,128)(2,1)}), bf16[8,2,76800]{2,1,0:T(2,128)(2,1)S(1)}, u32[]{:S(2)}, u32[]{:S(2)}) %all-to-all-start) | async-done | bytes 2457632 | tf_op jit(solution)/shard_map/all_to_all | solution.py:22
  102.5 4.4 %reshape.6 = bf16[2400,1,512]{2,1,0:T(2,128)(2,1)} reshape(bf16[8,2,76800]{2,1,0:T(2,128)(2,1)S(1)} %all-to-all-done) | data formatting | bytes 4915200
  107.0 17.2 %bitcast_reduce_fusion = bf16[512,2400]{0,1:T(8,128)(2,1)} fusion(bf16[2400,1,512]{2,1,0:T(2,128)(2,1)} %reshape.6), kind=kLoop, calls=%fused_computation.22 | loop fusion | bytes 4915200 | tf_op jit(solution)/shard_map/all_to_all | solution.py:22
  124.1 2.6 all_to_all.12
  126.8 1.4 copy.15
  128.1 0.2 pad
  128.3 1.1 copy.12
  129.4 2.6 broadcast_select_fusion
  132.1 0.0 all-reduce.7.cloned.1.call-update
  132.1 0.2 all-reduce.5.cloned.1.call-start
  132.3 110.6 %all-reduce.7.cloned.1.call-done = (bf16[4096,300]{0,1:T(8,128)(2,1)}, bf16[4096,300]{0,1:T(8,128)(2,1)}) async-done(((bf16[4096,300]{0,1:T(8,128)(2,1)}, bf16[4096,300]{0,1:T(8,128)(2,1)}), (bf16[4096,300]{0,1:T(8,128)(2,1)}, bf16[4096,300]{0,1:T(8,128)(2,1)})) %all-reduce.7.cloned.1.call-update) | async-done | bytes 4915216 | tf_op jit(solution)/shard_map/psum | solution.py:11
  242.9 4.1 %convolution_bitcast_fusion.1 = f32[300,300]{0,1:T(8,128)} fusion(bf16[4096,300]{0,1:T(8,128)(2,1)} %get-tuple-element.7, bf16[4096,300]{0,1:T(8,128)(2,1)S(1)} %bitcast.34), kind=kOutput, calls=%fused_computation.6 | convolution fusion | flops 737280000 | bytes 5275200 | tf_op jit(solution)/shard_map/dot_general | solution.py:33
  247.0 0.0 copy-done
  247.0 2.3 convolution_bitcast_fusion
  249.2 0.0 all-reduce.5.cloned.1.call-update
  251.2 0.0 copy-done.3
  251.2 0.1 dynamic-slice_subtract_fusion
  251.3 35.9 %all-reduce.5.cloned.1.call-done = (f32[300,300]{0,1:T(8,128)}, f32[300,300]{0,1:T(8,128)}) async-done(((f32[300,300]{0,1:T(8,128)}, f32[300,300]{0,1:T(8,128)}), (f32[300,300]{0,1:T(8,128)}, f32[300,300]{0,1:T(8,128)})) %all-reduce.5.cloned.1.call-update) | async-done | bytes 720016 | tf_op jit(solution)/shard_map/psum | solution.py:36
  287.2 3.5 %fusion.1 = f32[4096,300]{0,1:T(8,128)S(1)} fusion(bf16[4096,300]{0,1:T(8,128)(2,1)} %get-tuple-element.7, f32[300,300]{0,1:T(8,128)} %get-tuple-element.5, f32[300]{0:T(512)S(1)} %get-tuple-element.13, f32[300]{0:T(512)S(1)} %get-tuple-element.12), kind=kOutput, calls=%fused_computation.9 | convolution fusion | flops 737640000 | bytes 7735200 | tf_op jit(solution)/shard_map/dot_general | solution.py:38
  290.7 0.0 copy-done.1
  290.7 0.0 copy-done.2
  290.7 3.9 %fusion = f32[1,4096,300]{1,2,0:T(8,128)} fusion(f32[4096,300]{0,1:T(8,128)S(1)} %fusion.1, bf16[4096,300]{0,1:T(8,128)(2,1)S(1)} %copy-done.1, f32[300,300]{0,1:T(8,128)S(1)} %copy-done.2, f32[300]{0:T(512)S(1)} %get-tuple-element.11, f32[300]{0:T(512)S(1)} %get-tuple-element.12), kind=kOutput, calls=%fused_computation.1 | convolution fusion | flops 738868800 | bytes 12650400 | tf_op jit(solution)/shard_map/dot_general | solution.py:38
  294.6 9.7 %copy.10 = f32[1,4096,300]{1,0,2:T(1,128)} copy(f32[1,4096,300]{1,2,0:T(8,128)} %fusion) | data formatting | bytes 9830400 | tf_op jit(solution)/shard_map/broadcast_in_dim | solution.py:41
  (4 shorter events, 0.0 us)
Async XLA Ops:
  39.3 6.5 %copy-start.4 = (s32[2]{0:T(128)S(1)}, s32[2]{0:T(128)}, u32[]{:S(2)}) copy-start(s32[2]{0:T(128)} %param.7) | copy-start | bytes 28
  39.3 63.2 %all-to-all-start = ((bf16[8,2,76800]{2,1,0:T(2,128)(2,1)}), bf16[8,2,76800]{2,1,0:T(2,128)(2,1)S(1)}, u32[]{:S(2)}, u32[]{:S(2)}) async-start(bf16[8,2,76800]{2,1,0:T(2,128)(2,1)} %reshape.5), calls=%async_computation | async-start | bytes 4915200 | tf_op jit(solution)/shard_map/all_to_all | solution.py:22
  45.7 197.1 %all-reduce.7.cloned.1.call-start = ((), (), s32[]{:S(2)}) async-start(), calls=%async_computation.2 | async-start | bytes 9961472 | tf_op jit(solution)/shard_map/psum | solution.py:11
  132.1 155.1 %all-reduce.5.cloned.1.call-start = ((), (), s32[]{:S(2)}) async-start(), calls=%async_computation.1 | async-start | bytes 1867776 | tf_op jit(solution)/shard_map/psum | solution.py:36
  242.9 4.1 %copy-start = (bf16[4096,300]{0,1:T(8,128)(2,1)S(1)}, bf16[4096,300]{0,1:T(8,128)(2,1)}, u32[]{:S(2)}) copy-start(bf16[4096,300]{0,1:T(8,128)(2,1)} %get-tuple-element.8) | copy-start | bytes 7372804
  247.0 4.2 %copy-start.3 = (f32[2400]{0:T(1024)S(1)}, f32[2400]{0:T(1024)}, u32[]{:S(2)}) copy-start(f32[2400]{0:T(1024)} %param.6) | copy-start | bytes 28804
  287.2 3.5 %copy-start.1 = (bf16[4096,300]{0,1:T(8,128)(2,1)S(1)}, bf16[4096,300]{0,1:T(8,128)(2,1)}, u32[]{:S(2)}) copy-start(bf16[4096,300]{0,1:T(8,128)(2,1)} %get-tuple-element.8) | copy-start | bytes 7372804
  287.2 3.5 %copy-start.2 = (f32[300,300]{0,1:T(8,128)S(1)}, f32[300,300]{0,1:T(8,128)}, u32[]{:S(2)}) copy-start(f32[300,300]{0,1:T(8,128)} %get-tuple-element.6) | copy-start | bytes 1080004
Sparse Core Ops, SparseCore 0:
  132.2 110.6 all-reduce.6
  249.4 37.7 all-reduce.4
where the time goes:
time: 312 us; the launch traced here: 311 us
  waiting for transfers between devices  201 us (64%)
  local copies, waits for them, and re-layouts  53.6 us (17%)
  other arithmetic  19.1 us (6%)
  between operations  16.7 us (5%)
  matrix products  13.7 us (4%)
  starting transfers between devices  6.72 us (2%)
    psum x1, waiting for transfers between devices, from_root(): return lax.psum(kept, axis)  111 us
    all_to_all x1, waiting for transfers between devices, body(): lax.all_to_all(b_aux, ('col', 'rep'), split_axis=2, concat_axis=1, tiled=...  54.8 us
    psum x1, waiting for transfers between devices, body(): coupling = lax.psum(partial_value, 'aux')  35.9 us
    unnamed x16, local copies, waits for them, and re-layouts  22.1 us
    all_to_all x3, local copies, waits for them, and re-layouts, body(): lax.all_to_all(b_aux, ('col', 'rep'), split_axis=2, concat_axis=1, tiled=...  21.1 us
    unnamed x1, other arithmetic  16.3 us
    broadcast_in_dim x1, local copies, waits for them, and re-layouts, body(): return gamma_acc[None]  9.71 us
    dot_general x2, matrix products, body(): lax.dot_general(owner_cols, amplitude, (((1,), (1,)), ((), ())), preferre...  7.4 us
  transfers between devices with their start and end apart: 3, of which 3 were waited for; matrix products, arithmetic and copies ran while one was open for 0% of the time, Pallas kernels for 0%

commit v1 on v0

v1 whole, which is shorter than its diff:
```python
import jax
import jax.numpy as jnp
from jax import lax
from jax.sharding import PartitionSpec as P

os_scale = 1.3
COLS = ("col", "rep")
PARTIAL_BYTES_MAX = 16 * 2**20


def owner_columns(local, col_energy, owners, width):
    owned = []
    owner_energy = []
    for step_index in range(owners.shape[0]):
        first = owners[step_index] * width
        owned.append(lax.dynamic_slice_in_dim(local, first, width, 1))
        owner_energy.append(lax.dynamic_slice_in_dim(col_energy, first, width, 0))
    return jnp.concatenate(owned, axis=1), jnp.concatenate(owner_energy, axis=0)


def coupling_by_partials(local, owned, shards, width):
    rows = local.shape[0]
    blocked = local.reshape(rows, shards, width)
    partial_value = lax.dot_general(
        blocked, owned, (((0,), (0,)), ((), ())), preferred_element_type=jnp.float32
    )
    return lax.psum_scatter(partial_value, COLS, scatter_dimension=0, tiled=False)


def coupling_by_columns(b_aux, owned_all):
    moved = lax.all_to_all(b_aux, COLS, split_axis=2, concat_axis=1, tiled=True)
    return lax.dot_general(
        moved[0], owned_all, (((0,), (0,)), ((), ())), preferred_element_type=jnp.float32
    )


def body(b_aux, occ_energies, vir_energies, owners, *, shards, by_partials):
    local = b_aux[0]
    width = local.shape[1] // shards
    col_energy = (vir_energies[None, :] - occ_energies[:, None]).reshape(-1)
    shard_index = lax.axis_index(COLS)
    energy_mine = lax.dynamic_slice_in_dim(col_energy, shard_index * width, width, 0)
    owned, owner_energy = owner_columns(local, col_energy, owners, width)
    owned_all = lax.all_gather(owned, COLS, axis=0, tiled=True)
    if by_partials:
        coupling = coupling_by_partials(local, owned, shards, width)
    else:
        coupling = coupling_by_columns(b_aux, owned_all)
    coupling = lax.psum(coupling, "aux")
    denominator = energy_mine[:, None] + owner_energy[None, :]
    amplitude = (os_scale * coupling / denominator).astype(jnp.bfloat16)
    gamma = lax.dot_general(
        owned_all, amplitude, (((1,), (1,)), ((), ())), preferred_element_type=jnp.float32
    )
    return gamma[None]


def solution(mesh):
    shards = mesh.shape["col"] * mesh.shape["rep"]

    def run(b_aux, occ_energies, vir_energies, owners):
        ncol = b_aux.shape[2]
        partial_bytes = ncol * owners.shape[0] * (ncol // shards) * 4
        by_partials = partial_bytes <= PARTIAL_BYTES_MAX
        placed = (P(("groups", "aux"), COLS, None), P("groups"), P("groups"), P())
        return jax.shard_map(
            lambda *a: body(*a, shards=shards, by_partials=by_partials),
            mesh=mesh,
            in_specs=placed,
            out_specs=P(("groups", "aux"), None, COLS),
            check_vma=False,
        )(b_aux, occ_energies, vir_energies, owners)

    return run
```

time: 312 us -> 202 us (0.65)
  waiting for transfers between devices: 201 us -> 160 us
  local copies, waits for them, and re-layouts: 53.6 us -> 15.1 us
  other arithmetic: 19.1 us -> 0.16 us
  starting transfers between devices: 6.72 us -> 0.08 us
    psum x2 -> x1, waiting for transfers between devices: 146 us -> 35.4 us  [body(): coupling = lax.psum(coupling, 'aux')]
    reduce_scatter x0 -> x1, waiting for transfers between devices: none -> 71.2 us  [coupling_by_partials(): lax.psum_scatter(partial_value, COLS, scatter_dimension=0, tiled=False)]
    all_to_all x1 -> x0, waiting for transfers between devices: 54.8 us -> none  [body(): lax.all_to_all(b_aux, ('col', 'rep'), split_axis=2, concat_axis=1, tiled=...]
    all_gather x0 -> x1, waiting for transfers between devices: none -> 52.5 us  [body(): owned_all = lax.all_gather(owned, COLS, axis=0, tiled=True)]
    unnamed x16 -> x4, local copies, waits for them, and re-layouts: 22.1 us -> 0.01 us
    all_to_all x3 -> x0, local copies, waits for them, and re-layouts: 21.1 us -> none  [body(): lax.all_to_all(b_aux, ('col', 'rep'), split_axis=2, concat_axis=1, tiled=...]
    unnamed x1 -> x0, other arithmetic: 16.3 us -> none
    all_to_all x1 -> x0, starting transfers between devices: 6.46 us -> none  [body(): lax.all_to_all(b_aux, ('col', 'rep'), split_axis=2, concat_axis=1, tiled=...]
where the time goes in v1:
time: 202 us
  waiting for transfers between devices  160 us (79%)
  between operations  15.2 us (8%)
  local copies, waits for them, and re-layouts  15.1 us (7%)
  matrix products  11.8 us (6%)
    reduce_scatter x1, waiting for transfers between devices, coupling_by_partials(): lax.psum_scatter(partial_value, COLS, scatter_dimension=0, tiled=False)  71.2 us
    all_gather x1, waiting for transfers between devices, body(): owned_all = lax.all_gather(owned, COLS, axis=0, tiled=True)  52.5 us
    psum x1, waiting for transfers between devices, body(): coupling = lax.psum(coupling, 'aux')  35.4 us
    broadcast_in_dim x1, local copies, waits for them, and re-layouts, body(): return gamma[None]  9.71 us
    dot_general x1, matrix products, body(): lax.dot_general(owned_all, amplitude, (((1,), (1,)), ((), ())), preferred...  6.98 us
    dot_general x1, matrix products, coupling_by_partials(): lax.dot_general(blocked, owned, (((0,), (0,)), ((), ())), preferred_eleme...  4.78 us
  transfers between devices with their start and end apart: 3, of which 3 were waited for; matrix products, arithmetic and copies ran while one was open for 0% of the time, Pallas kernels for 0%

profile of v1, /device:TPU:0, one launch (start us, length us, event | category | flops | bytes accessed | tf_op | source)
XLA Modules:
  0.0 202.1 jit_solution(16254460932990910338)
XLA Ops:
  6.5 0.0 reduce-scatter.2.cloned.1.call-start
  6.5 1.4 fusion.6
  9.3 2.6 %reshape_squeeze.3 = bf16[512,8,300]{0,2,1:T(8,128)(2,1)S(1)} reshape(bf16[1,512,2400]{1,2,0:T(8,128)(2,1)} %param.4) | data formatting | bytes 4915200 | tf_op jit(solution)/shard_map/reshape;squeeze | solution.py:23
  11.9 1.2 dynamic-slice_bitcast_fusion.1
  13.1 0.1 pad_maximum_fusion
  13.2 0.0 copy-start
  13.2 4.8 %convolution_bitcast_fusion.1 = f32[8,300,600]{2,1,0:T(8,128)} fusion(bf16[512,8,300]{0,2,1:T(8,128)(2,1)S(1)} %reshape_squeeze.3, bf16[512,600]{0,1:T(8,128)(2,1)S(1)} %pad_maximum_fusion), kind=kOutput, calls=%fused_computation.1 | convolution fusion | flops 1474560000 | bytes 8832000 | tf_op jit(solution)/shard_map/dot_general | solution.py:24
  18.0 0.0 copy-done
  18.0 0.0 copy-start.1
  18.0 0.0 reduce-scatter.2.cloned.1.call-update
  18.1 0.0 all-gather.2.cloned.1.call-start
  18.1 0.7 all-gather.2.cloned.1.call-update
  18.8 0.0 all-reduce.2.cloned.1.call-start
  18.9 71.2 %reduce-scatter.2.cloned.1.call-done = f32[1,300,600]{2,1,0:T(8,128)} async-done(((f32[8,300,600]{2,1,0:T(8,128)}), f32[1,300,600]{2,1,0:T(8,128)}) %reduce-scatter.2.cloned.1.call-update) | async-done | bytes 720016 | tf_op jit(solution)/shard_map/reduce_scatter | solution.py:27
  90.1 0.0 all-reduce.2.cloned.1.call-update
  90.8 0.0 copy-done.1
  90.8 0.1 fusion.5
  90.9 0.1 pad_maximum_fusion.1
  91.0 52.5 %all-gather.2.cloned.1.call-done = bf16[4096,600]{0,1:T(8,128)(2,1)} async-done(((bf16[512,600]{0,1:T(8,128)(2,1)}), bf16[4096,600]{0,1:T(8,128)(2,1)}) %all-gather.2.cloned.1.call-update) | async-done | bytes 4915216 | tf_op jit(solution)/shard_map/all_gather | solution.py:44
  143.5 35.4 %all-reduce.2.cloned.1.call-done = f32[300,600]{1,0:T(8,128)} async-done(((f32[300,600]{1,0:T(8,128)}), f32[300,600]{1,0:T(8,128)}) %all-reduce.2.cloned.1.call-update) | async-done | bytes 720016 | tf_op jit(solution)/shard_map/psum | solution.py:49
  178.9 7.0 %convolution_bitcast_fusion = f32[1,4096,300]{1,2,0:T(8,128)} fusion(bf16[4096,600]{0,1:T(8,128)(2,1)} %all-gather.2.cloned.1.call-done, f32[300,600]{1,0:T(8,128)} %all-reduce.2.cloned.1.call-done, f32[600]{0:T(1024)S(1)} %pad_maximum_fusion.1, f32[300]{0:T(512)S(1)} %get-tuple-element.7), kind=kOutput, calls=%fused_computation | convolution fusion | flops 1475280000 | bytes 10554000 | tf_op jit(solution)/shard_map/dot_general | solution.py:52
  185.9 9.7 %copy.6 = f32[1,4096,300]{1,0,2:T(1,128)} copy(f32[1,4096,300]{1,2,0:T(8,128)} %convolution_bitcast_fusion) | data formatting | bytes 9830400 | tf_op jit(solution)/shard_map/broadcast_in_dim | solution.py:55
  (1 shorter events, 0.0 us)
Async XLA Ops:
  6.5 83.6 %reduce-scatter.2.cloned.1.call-start = ((), (), s32[]{:S(2)}) async-start(), calls=%async_computation.2 | async-start | bytes 7004160 | tf_op jit(solution)/shard_map/reduce_scatter | solution.py:27
  13.2 4.8 %copy-start = (bf16[512,600]{0,1:T(8,128)(2,1)}, bf16[512,600]{0,1:T(8,128)(2,1)S(1)}, u32[]{:S(2)}) copy-start(bf16[512,600]{0,1:T(8,128)(2,1)S(1)} %pad_maximum_fusion) | copy-start | bytes 1843204
  18.0 72.7 %copy-start.1 = (f32[2400]{0:T(1024)S(1)}, f32[2400]{0:T(1024)}, u32[]{:S(2)}) copy-start(f32[2400]{0:T(1024)} %param.6) | copy-start | bytes 28804
  18.1 125.4 %all-gather.2.cloned.1.call-start = ((), (), s32[]{:S(2)}) async-start(), calls=%async_computation.1 | async-start | bytes 5529600 | tf_op jit(solution)/shard_map/all_gather | solution.py:44
  18.8 160.1 %all-reduce.2.cloned.1.call-start = ((), (), s32[]{:S(2)}) async-start(), calls=%async_computation.3 | async-start | bytes 1556480 | tf_op jit(solution)/shard_map/psum | solution.py:49
Sparse Core Ops, SparseCore 0:
  18.2 71.8 reduce-scatter.1
  91.8 51.6 all-gather.1
  145.9 32.9 all-reduce.1

commit v2 on v1

--- a/solution.py
+++ b/solution.py
@@ -34,7 +34,14 @@
     )
 
 
-def body(b_aux, occ_energies, vir_energies, owners, *, shards, by_partials):
+def exchange_sum(value, axis, size):
+    total = value
+    for step in range(1, size):
+        total = total + lax.ppermute(value, axis, [(i, (i + step) % size) for i in range(size)])
+    return total
+
+
+def body(b_aux, occ_energies, vir_energies, owners, *, shards, n_aux, by_partials):
     local = b_aux[0]
     width = local.shape[1] // shards
     col_energy = (vir_energies[None, :] - occ_energies[:, None]).reshape(-1)
@@ -46,7 +53,7 @@
         coupling = coupling_by_partials(local, owned, shards, width)
     else:
         coupling = coupling_by_columns(b_aux, owned_all)
-    coupling = lax.psum(coupling, "aux")
+    coupling = exchange_sum(coupling, "aux", n_aux)
     denominator = energy_mine[:, None] + owner_energy[None, :]
     amplitude = (os_scale * coupling / denominator).astype(jnp.bfloat16)
     gamma = lax.dot_general(
@@ -64,7 +71,7 @@
         by_partials = partial_bytes <= PARTIAL_BYTES_MAX
         placed = (P(("groups", "aux"), COLS, None), P("groups"), P("groups"), P())
         return jax.shard_map(
-            lambda *a: body(*a, shards=shards, by_partials=by_partials),
+            lambda *a: body(*a, shards=shards, n_aux=mesh.shape["aux"], by_partials=by_partials),
             mesh=mesh,
             in_specs=placed,
             out_specs=P(("groups", "aux"), None, COLS),

time: 202 us -> 167 us (0.83)
  waiting for transfers between devices: 160 us -> 123 us
    psum x1 -> x0, waiting for transfers between devices: 35.4 us -> none  [body(): coupling = lax.psum(coupling, 'aux')]
  transfers between devices with their start and end apart: 3 -> 3, of which waited for: 3 -> 2; matrix products, arithmetic and copies ran while one was open for 0% -> 0% of each run, Pallas kernels for 0% -> 0%
where the time goes in v2:
time: 167 us
  waiting for transfers between devices  123 us (74%)
  between operations  15.4 us (9%)
  local copies, waits for them, and re-layouts  15 us (9%)
  matrix products  11.8 us (7%)
    reduce_scatter x1, waiting for transfers between devices, coupling_by_partials(): lax.psum_scatter(partial_value, COLS, scatter_dimension=0, tiled=False)  71.3 us
    all_gather x1, waiting for transfers between devices, body(): owned_all = lax.all_gather(owned, COLS, axis=0, tiled=True)  51.1 us
    broadcast_in_dim x1, local copies, waits for them, and re-layouts, body(): return gamma[None]  9.71 us
    dot_general x1, matrix products, body(): lax.dot_general(owned_all, amplitude, (((1,), (1,)), ((), ())), preferred...  6.99 us
    dot_general x1, matrix products, coupling_by_partials(): lax.dot_general(blocked, owned, (((0,), (0,)), ((), ())), preferred_eleme...  4.77 us
  transfers between devices with their start and end apart: 3, of which 2 were waited for; matrix products, arithmetic and copies ran while one was open for 0% of the time, Pallas kernels for 0%

profile of v2, /device:TPU:0, one launch (start us, length us, event | category | flops | bytes accessed | tf_op | source)
XLA Modules:
  0.0 166.9 jit_solution(9124298590345004235)
XLA Ops:
  6.5 0.0 reduce-scatter.2.cloned.1.call-start
  6.5 1.4 fusion.7
  9.2 2.6 %reshape_squeeze.3 = bf16[512,8,300]{0,2,1:T(8,128)(2,1)S(1)} reshape(bf16[1,512,2400]{1,2,0:T(8,128)(2,1)} %param.4) | data formatting | bytes 4915200 | tf_op jit(solution)/shard_map/reshape;squeeze | solution.py:23
  11.8 1.2 dynamic-slice_bitcast_fusion.1
  13.1 0.1 pad_maximum_fusion
  13.2 0.0 copy-start
  13.2 4.8 %convolution_bitcast_fusion.1 = f32[8,300,600]{2,1,0:T(8,128)} fusion(bf16[512,8,300]{0,2,1:T(8,128)(2,1)S(1)} %reshape_squeeze.3, bf16[512,600]{0,1:T(8,128)(2,1)S(1)} %pad_maximum_fusion), kind=kOutput, calls=%fused_computation.1 | convolution fusion | flops 1474560000 | bytes 8832000 | tf_op jit(solution)/shard_map/dot_general | solution.py:24
  17.9 0.0 copy-done
  17.9 0.0 copy-start.1
  17.9 0.0 reduce-scatter.2.cloned.1.call-update
  18.0 0.0 all-gather.2.cloned.1.call-start
  18.0 0.7 all-gather.2.cloned.1.call-update
  18.7 71.3 %reduce-scatter.2.cloned.1.call-done = f32[1,300,600]{2,1,0:T(8,128)} async-done(((f32[8,300,600]{2,1,0:T(8,128)}), f32[1,300,600]{2,1,0:T(8,128)}) %reduce-scatter.2.cloned.1.call-update) | async-done | bytes 720016 | tf_op jit(solution)/shard_map/reduce_scatter | solution.py:27
  90.0 1.5 collective-permute-start
  92.1 0.0 copy-done.1
  92.2 0.1 fusion.6
  92.2 0.1 pad_maximum_fusion.1
  92.3 51.1 %all-gather.2.cloned.1.call-done = bf16[4096,600]{0,1:T(8,128)(2,1)} async-done(((bf16[512,600]{0,1:T(8,128)(2,1)}), bf16[4096,600]{0,1:T(8,128)(2,1)}) %all-gather.2.cloned.1.call-update) | async-done | bytes 4915216 | tf_op jit(solution)/shard_map/all_gather | solution.py:51
  143.4 0.0 collective-permute-done
  143.4 7.0 %convolution_bitcast_fusion = f32[1,4096,300]{1,2,0:T(8,128)} fusion(bf16[4096,600]{0,1:T(8,128)(2,1)} %all-gather.2.cloned.1.call-done, f32[300,600]{1,0:T(8,128)S(1)} %collective-permute-done, f32[600]{0:T(1024)S(1)} %pad_maximum_fusion.1, f32[300]{0:T(512)S(1)} %get-tuple-element.7, f32[1,300,600]{2,1,0:T(8,128)} %reduce-scatter.2.cloned.1.call-done), kind=kOutput, calls=%fused_computation | convolution fusion | flops 1475459968 | bytes 11274000 | tf_op jit(solution)/shard_map/dot_general | solution.py:59
  150.4 9.7 %copy.6 = f32[1,4096,300]{1,0,2:T(1,128)} copy(f32[1,4096,300]{1,2,0:T(8,128)} %convolution_bitcast_fusion) | data formatting | bytes 9830400 | tf_op jit(solution)/shard_map/broadcast_in_dim | solution.py:62
  (1 shorter events, 0.0 us)
Async XLA Ops:
  6.5 83.5 %reduce-scatter.2.cloned.1.call-start = ((), (), s32[]{:S(2)}) async-start(), calls=%async_computation.2 | async-start | bytes 7004160 | tf_op jit(solution)/shard_map/reduce_scatter | solution.py:27
  13.2 4.8 %copy-start = (bf16[512,600]{0,1:T(8,128)(2,1)}, bf16[512,600]{0,1:T(8,128)(2,1)S(1)}, u32[]{:S(2)}) copy-start(bf16[512,600]{0,1:T(8,128)(2,1)S(1)} %pad_maximum_fusion) | copy-start | bytes 1843204
  17.9 74.2 %copy-start.1 = (f32[2400]{0:T(1024)S(1)}, f32[2400]{0:T(1024)}, u32[]{:S(2)}) copy-start(f32[2400]{0:T(1024)} %param.6) | copy-start | bytes 28804
  18.0 125.4 %all-gather.2.cloned.1.call-start = ((), (), s32[]{:S(2)}) async-start(), calls=%async_computation.1 | async-start | bytes 5529600 | tf_op jit(solution)/shard_map/all_gather | solution.py:51
  90.0 53.4 %collective-permute-start = (f32[300,600]{1,0:T(8,128)}, f32[300,600]{1,0:T(8,128)S(1)}, u32[]{:S(2)}, u32[]{:S(2)}) collective-permute-start(f32[300,600]{1,0:T(8,128)} %bitcast.24), channel_id=1, source_target_pairs={{0,2},{2,0},{1,3},{3,1},{4,6},{6,4},{5,7},{7,5},{8,10},{10,8},{9,1... | collective-permute-start | bytes 2160008 | tf_op jit(solution)/shard_map/ppermute | solution.py:40
Sparse Core Ops, SparseCore 0:
  18.1 71.8 reduce-scatter.1
  91.7 51.6 all-gather.1

commit v3 on v2

--- a/solution.py
+++ b/solution.py
@@ -6,6 +6,7 @@
 os_scale = 1.3
 COLS = ("col", "rep")
 PARTIAL_BYTES_MAX = 16 * 2**20
+LINE_MAX = 8
 
 
 def owner_columns(local, col_energy, owners, width):
@@ -18,13 +19,70 @@
     return jnp.concatenate(owned, axis=1), jnp.concatenate(owner_energy, axis=0)
 
 
-def coupling_by_partials(local, owned, shards, width):
+def pick(stack, index):
+    return lax.dynamic_index_in_dim(stack, index, 0, keepdims=False)
+
+
+def line_reduce_scatter(partial_value, n_col, n_rep):
+    me = lax.axis_index("col")
+    rep = lax.axis_index("rep")
+    summed = pick(partial_value, rep)
+    for step in range(1, n_rep):
+        pairs = [(i, (i + step) % n_rep) for i in range(n_rep)]
+        summed = summed + lax.ppermute(pick(partial_value, (rep + step) % n_rep), "rep", pairs)
+    right = None
+    left = None
+    for step in range(1, n_col):
+        far = jnp.minimum(me + n_col - step, n_col - 1)
+        message = pick(summed, far) if right is None else pick(summed, far) + right
+        right = lax.ppermute(message, "col", [(c, c + 1) for c in range(step)])
+        near = jnp.maximum(me - n_col + step, 0)
+        message = pick(summed, near) if left is None else pick(summed, near) + left
+        left = lax.ppermute(message, "col", [(c, c - 1) for c in range(n_col - step, n_col)])
+    total = pick(summed, me)
+    if right is not None:
+        total = total + right + left
+    return total
+
+
+def line_all_gather(owned, n_col, n_rep):
+    me = lax.axis_index("col")
+    rep = lax.axis_index("rep")
+    from_right = [None]
+    from_left = [None]
+    right = owned
+    left = owned
+    for step in range(1, n_col):
+        right = lax.ppermute(right, "col", [(c, c + 1) for c in range(step - 1, n_col - 1)])
+        left = lax.ppermute(left, "col", [(c, c - 1) for c in range(1, n_col - step + 1)])
+        from_right.append(right)
+        from_left.append(left)
+    relative = [owned]
+    for step in range(1, n_col):
+        relative.append(jnp.where(me + step < n_col, from_left[step], from_right[n_col - step]))
+    relative = jnp.stack(relative + relative)
+    mine = lax.dynamic_slice_in_dim(relative, (n_col - me) % n_col, n_col, 0)
+    by_offset = [mine]
+    for step in range(1, n_rep):
+        pairs = [(i, (i - step) % n_rep) for i in range(n_rep)]
+        by_offset.append(lax.ppermute(mine, "rep", pairs))
+    slots = []
+    for slot in range(n_rep):
+        value = by_offset[0]
+        for step in range(1, n_rep):
+            value = jnp.where((rep + step) % n_rep == slot, by_offset[step], value)
+        slots.append(value)
+    full = jnp.stack(slots, axis=1)
+    return full.reshape((-1,) + owned.shape[1:])
+
+
+def coupling_by_partials(local, owned, n_col, n_rep, width):
     rows = local.shape[0]
-    blocked = local.reshape(rows, shards, width)
+    blocked = local.reshape(rows, n_col, n_rep, width).transpose(0, 2, 1, 3)
     partial_value = lax.dot_general(
         blocked, owned, (((0,), (0,)), ((), ())), preferred_element_type=jnp.float32
     )
-    return lax.psum_scatter(partial_value, COLS, scatter_dimension=0, tiled=False)
+    return line_reduce_scatter(partial_value, n_col, n_rep)
 
 
 def coupling_by_columns(b_aux, owned_all):
@@ -41,16 +99,20 @@
     return total
 
 
-def body(b_aux, occ_energies, vir_energies, owners, *, shards, n_aux, by_partials):
+def body(b_aux, occ_energies, vir_energies, owners, *, n_col, n_rep, n_aux, by_partials):
+    shards = n_col * n_rep
     local = b_aux[0]
     width = local.shape[1] // shards
     col_energy = (vir_energies[None, :] - occ_energies[:, None]).reshape(-1)
     shard_index = lax.axis_index(COLS)
     energy_mine = lax.dynamic_slice_in_dim(col_energy, shard_index * width, width, 0)
     owned, owner_energy = owner_columns(local, col_energy, owners, width)
-    owned_all = lax.all_gather(owned, COLS, axis=0, tiled=True)
+    if n_col <= LINE_MAX:
+        owned_all = line_all_gather(owned, n_col, n_rep)
+    else:
+        owned_all = lax.all_gather(owned, COLS, axis=0, tiled=True)
     if by_partials:
-        coupling = coupling_by_partials(local, owned, shards, width)
+        coupling = coupling_by_partials(local, owned, n_col, n_rep, width)
     else:
         coupling = coupling_by_columns(b_aux, owned_all)
     coupling = exchange_sum(coupling, "aux", n_aux)
@@ -63,7 +125,8 @@
 
 
 def solution(mesh):
-    shards = mesh.shape["col"] * mesh.shape["rep"]
+    n_col, n_rep = mesh.shape["col"], mesh.shape["rep"]
+    shards = n_col * n_rep
 
     def run(b_aux, occ_energies, vir_energies, owners):
         ncol = b_aux.shape[2]
@@ -71,7 +134,7 @@
         by_partials = partial_bytes <= PARTIAL_BYTES_MAX
         placed = (P(("groups", "aux"), COLS, None), P("groups"), P("groups"), P())
         return jax.shard_map(
-            lambda *a: body(*a, shards=shards, n_aux=mesh.shape["aux"], by_partials=by_partials),
+            lambda *a: body(*a, n_col=n_col, n_rep=n_rep, n_aux=mesh.shape["aux"], by_partials=by_partials),
             mesh=mesh,
             in_specs=placed,
             out_specs=P(("groups", "aux"), None, COLS),

time: 167 us -> 195 us (1.17)
  waiting for transfers between devices: 123 us -> 79.8 us
  local copies, waits for them, and re-layouts: 15 us -> 46.5 us
  starting transfers between devices: 1.52 us -> 31.2 us
  other arithmetic: 0.16 us -> 22.8 us
  between operations: 15.4 us -> 2.27 us
    ppermute x0 -> x14, waiting for transfers between devices: none -> 79.8 us  [the longest x3 27 us: line_reduce_scatter(): right = lax.ppermute(message, 'col', [(c, c + 1) for c in range(step)])]
    reduce_scatter x1 -> x0, waiting for transfers between devices: 71.3 us -> none  [coupling_by_partials(): lax.psum_scatter(partial_value, COLS, scatter_dimension=0, tiled=False)]
    all_gather x1 -> x0, waiting for transfers between devices: 51.1 us -> none  [body(): owned_all = lax.all_gather(owned, COLS, axis=0, tiled=True)]
    ppermute x0 -> x14, starting transfers between devices: none -> 29.7 us  [the longest x3 14.8 us: line_reduce_scatter(): right = lax.ppermute(message, 'col', [(c, c + 1) for c in range(step)])]
    reshape x0 -> x1, local copies, waits for them, and re-layouts: none -> 12 us  [line_all_gather(): return full.reshape((-1,) + owned.shape[1:])]
    add x0 -> x5, other arithmetic: none -> 11.5 us  [the longest x2 3.82 us: line_reduce_scatter(): message = pick(summed, far) if right is None else pick(summed, far) + right]
    another operation x2 -> x3, local copies, waits for them, and re-layouts: 2.73 us -> 12.4 us  [the longest x1 9.66 us: line_all_gather(): full = jnp.stack(slots, axis=1)]
    squeeze x0 -> x3, local copies, waits for them, and re-layouts: none -> 5.93 us  [pick(): return lax.dynamic_index_in_dim(stack, index, 0, keepdims=False)]
  transfers between devices with their start and end apart: 3 -> 15, of which waited for: 2 -> 8; matrix products, arithmetic and copies ran while one was open for 0% -> 24% of each run, Pallas kernels for 0% -> 0%
where the time goes in v3:
time: 195 us; the launch traced here: 194 us
  waiting for transfers between devices  79.8 us (41%)
  local copies, waits for them, and re-layouts  46.5 us (24%)
  starting transfers between devices  31.2 us (16%)
  other arithmetic  22.8 us (12%)
  matrix products  11.8 us (6%)
  between operations  2.27 us (1%)
    ppermute x3, waiting for transfers between devices, line_reduce_scatter(): right = lax.ppermute(message, 'col', [(c, c + 1) for c in range(step)])  27 us
    ppermute x3, waiting for transfers between devices, line_all_gather(): lax.ppermute(left, 'col', [(c, c - 1) for c in range(1, n_col - step + 1)])  21.7 us
    ppermute x3, waiting for transfers between devices, line_reduce_scatter(): lax.ppermute(message, 'col', [(c, c - 1) for c in range(n_col - step, n_c...  18.6 us
    ppermute x3, starting transfers between devices, line_reduce_scatter(): right = lax.ppermute(message, 'col', [(c, c + 1) for c in range(step)])  14.8 us
    ppermute x3, waiting for transfers between devices, line_all_gather(): lax.ppermute(right, 'col', [(c, c + 1) for c in range(step - 1, n_col - 1)])  12.4 us
    reshape x1, local copies, waits for them, and re-layouts, line_all_gather(): return full.reshape((-1,) + owned.shape[1:])  12 us
    broadcast_in_dim x1, local copies, waits for them, and re-layouts, body(): return gamma[None]  9.71 us
    another operation x1, local copies, waits for them, and re-layouts, line_all_gather(): full = jnp.stack(slots, axis=1)  9.66 us
  transfers between devices with their start and end apart: 15, of which 8 were waited for; matrix products, arithmetic and copies ran while one was open for 24% of the time, Pallas kernels for 0%

profile of v3, /device:TPU:0, one launch (start us, length us, event | category | flops | bytes accessed | tf_op | source)
XLA Modules:
  0.0 194.3 jit_solution(481184186687748308)
XLA Ops:
  2.6 2.6 %reshape_squeeze.3 = bf16[512,4,2,300]{0,3,2,1:T(8,128)(2,1)S(1)} reshape(bf16[1,512,2400]{1,2,0:T(8,128)(2,1)} %param.4) | data formatting | bytes 4915200 | tf_op jit(solution)/shard_map/reshape;squeeze | solution.py:81
  7.4 4.8 %fusion = f32[600,2,4,300]{0,3,2,1:T(8,128)} fusion(bf16[512,600]{0,1:T(8,128)(2,1)S(1)} %get-tuple-element.6, bf16[512,4,2,300]{0,3,2,1:T(8,128)(2,1)S(1)} %reshape_squeeze.3), kind=kOutput, calls=%fused_computation.4 | convolution fusion | flops 1474560000 | bytes 8832000 | tf_op jit(solution)/shard_map/dot_general | solution.py:82
  12.2 2.1 %dynamic-slice_bitcast_fusion = f32[4,300,600]{2,1,0:T(8,128)S(1)} fusion(f32[600,2,4,300]{0,3,2,1:T(8,128)} %fusion, s32[]{:T(128)S(6)} %select_n.102), kind=kLoop, calls=%fused_computation.3 | loop fusion | bytes 5760004 | tf_op jit(solution)/shard_map/jit(dynamic_index_in_dim)/squeeze | solution.py:23
  14.3 2.8 %copy.12 = f32[4,300,600]{2,0,1:T(4,128)} copy(f32[4,300,600]{2,1,0:T(8,128)S(1)} %dynamic-slice_bitcast_fusion) | data formatting | bytes 5760000 | tf_op jit(solution)/shard_map/jit(dynamic_index_in_dim)/squeeze | solution.py:23
  17.5 4.5 %collective-permute-start.1 = (bf16[512,600]{0,1:T(8,128)(2,1)S(1)}, bf16[512,600]{0,1:T(8,128)(2,1)S(1)}, u32[]{:S(2)}, u32[]{:S(2)}) collective-permute-start(bf16[512,600]{0,1:T(8,128)(2,1)S(1)} %get-tuple-element.6), channel_id=1, source_target_pairs={{0,4},{4,8},{8,12},{1,5},{5,9},{9,13},{2,6},{6,10},{10,14},{3,7},{... | collective-permute-start | bytes 1843208 | tf_op jit(solution)/shard_map/ppermute | solution.py:56
  23.4 12.4 %collective-permute-done.1 = bf16[512,600]{0,1:T(8,128)(2,1)S(1)} collective-permute-done((bf16[512,600]{0,1:T(8,128)(2,1)S(1)}, bf16[512,600]{0,1:T(8,128)(2,1)S(1)}, u32[]{:S(2)}, u32[]{:S(2)}) %collective-permute-start.1) | collective-permute-done | bytes 614432 | tf_op jit(solution)/shard_map/ppermute | solution.py:56
  36.5 3.5 %collective-permute-done = bf16[512,600]{0,1:T(8,128)(2,1)S(1)} collective-permute-done((bf16[512,600]{0,1:T(8,128)(2,1)S(1)}, bf16[512,600]{0,1:T(8,128)(2,1)S(1)}, u32[]{:S(2)}, u32[]{:S(2)}) %collective-permute-start) | collective-permute-done | bytes 614432 | tf_op jit(solution)/shard_map/ppermute | solution.py:57
  42.0 15.3 %collective-permute-done.4 = bf16[512,600]{0,1:T(8,128)(2,1)} collective-permute-done((bf16[512,600]{0,1:T(8,128)(2,1)S(1)}, bf16[512,600]{0,1:T(8,128)(2,1)}, u32[]{:S(2)}, u32[]{:S(2)}) %collective-permute-start.4) | collective-permute-done | bytes 614432 | tf_op jit(solution)/shard_map/ppermute | solution.py:57
  59.6 2.1 %bitcast_dynamic-update-slice_fusion.2 = bf16[8,512,600]{1,2,0:T(8,128)(2,1)} fusion(bf16[8,512,600]{1,2,0:T(8,128)(2,1)} %bitcast_dynamic-update-slice_fusion.4, bf16[512,600]{0,1:T(8,128)(2,1)} %collective-permute-done.4, bf16[512,600]{0,1:T(8,128)(2,1)S(1)} %collective-permute-done.2, pred[]{:T(512)S(6)} %lt.64), kind=kLoop, calls=%fused_computation.21 | loop fusion | flops 307200 | bytes 1843201
  61.7 3.3 %bitcast_add_fusion = f32[4,300,600]{2,1,0:T(8,128)S(1)} fusion(f32[4,300,600]{2,0,1:T(4,128)} %collective-permute-done.7, f32[600,2,4,300]{0,3,2,1:T(8,128)} %fusion, s32[]{:T(128)S(6)} %select_n.101), kind=kLoop, calls=%fused_computation.2 | loop fusion | flops 720000 | bytes 8640004 | tf_op jit(solution)/shard_map/add | solution.py:32
  66.1 4.7 %collective-permute-start.8 = (f32[300,600]{1,0:T(8,128)S(1)}, f32[300,600]{1,0:T(8,128)S(1)}, u32[]{:S(2)}, u32[]{:S(2)}) collective-permute-start(f32[300,600]{1,0:T(8,128)S(1)} %get-tuple-element.11), channel_id=1, source_target_pairs={{0,4},{1,5},{2,6},{3,7},{16,20},{17,21},{18,22},{19,23}} | collective-permute-start | bytes 2160008 | tf_op jit(solution)/shard_map/ppermute | solution.py:38
  70.8 3.0 %collective-permute-done.5 = bf16[512,600]{0,1:T(8,128)(2,1)S(1)} collective-permute-done((bf16[512,600]{0,1:T(8,128)(2,1)}, bf16[512,600]{0,1:T(8,128)(2,1)S(1)}, u32[]{:S(2)}, u32[]{:S(2)}) %collective-permute-start.5) | collective-permute-done | bytes 614432 | tf_op jit(solution)/shard_map/ppermute | solution.py:57
  74.2 1.5 collective-permute-start.11
  75.8 10.2 %collective-permute-done.8 = f32[300,600]{1,0:T(8,128)S(1)} collective-permute-done((f32[300,600]{1,0:T(8,128)S(1)}, f32[300,600]{1,0:T(8,128)S(1)}, u32[]{:S(2)}, u32[]{:S(2)}) %collective-permute-start.8) | collective-permute-done | bytes 720032 | tf_op jit(solution)/shard_map/ppermute | solution.py:38
  87.0 5.2 %collective-permute-start.9 = (f32[300,600]{1,0:T(8,128)}, f32[300,600]{1,0:T(8,128)}, u32[]{:S(2)}, u32[]{:S(2)}) collective-permute-start(f32[300,600]{1,0:T(8,128)} %bitcast_add_fusion.3), channel_id=1, source_target_pairs={{0,4},{4,8},{1,5},{5,9},{2,6},{6,10},{3,7},{7,11},{16,20},{20,24},... | collective-permute-start | bytes 2160008 | tf_op jit(solution)/shard_map/ppermute | solution.py:38
  93.6 2.2 %copy-done.1 = bf16[8,512,600]{1,2,0:T(8,128)(2,1)} copy-done((bf16[8,512,600]{1,2,0:T(8,128)(2,1)}, bf16[8,512,600]{1,2,0:T(8,128)(2,1)S(1)}, u32[]{:S(2)}) %copy-start.1) | copy-done | bytes 4915224
  95.9 1.6 constant_dynamic-slice_fusion
  97.5 8.4 %collective-permute-done.9 = f32[300,600]{1,0:T(8,128)} collective-permute-done((f32[300,600]{1,0:T(8,128)}, f32[300,600]{1,0:T(8,128)}, u32[]{:S(2)}, u32[]{:S(2)}) %collective-permute-start.9) | collective-permute-done | bytes 720032 | tf_op jit(solution)/shard_map/ppermute | solution.py:38
  105.9 2.8 %bitcast_add_fusion.4 = (f32[300,600]{1,0:T(8,128)}, f32[300,600]{1,0:T(8,128)}) fusion(f32[300,600]{1,0:T(8,128)} %collective-permute-done.9, f32[4,300,600]{2,1,0:T(8,128)S(1)} %bitcast_add_fusion, s32[]{:T(128)S(6)} %select_n.104, f32[300,600]{1,0:T(8,128)} %collective-permute-done.11, s32[]{:T(128)S(6)} %max.10), kind=kLoop, calls=%fused_computation.11 | loop fusion | flops 360000 | bytes 4320008 | tf_op jit(solution)/shard_map/add | solution.py:37
  108.7 1.6 collective-permute-start.12
  110.3 4.9 %collective-permute-start.10 = (f32[300,600]{1,0:T(8,128)}, f32[300,600]{1,0:T(8,128)}, u32[]{:S(2)}, u32[]{:S(2)}) collective-permute-start(f32[300,600]{1,0:T(8,128)} %get-tuple-element.9), channel_id=1, source_target_pairs={{0,4},{4,8},{8,12},{1,5},{5,9},{9,13},{2,6},{6,10},{10,14},{3,7},{... | collective-permute-start | bytes 2160008 | tf_op jit(solution)/shard_map/ppermute | solution.py:38
  115.2 2.1 %bitcast_add_fusion.2 = f32[300,600]{1,0:T(8,128)} fusion(f32[300,600]{1,0:T(8,128)} %collective-permute-done.12, f32[4,300,600]{2,1,0:T(8,128)S(1)} %bitcast_add_fusion, s32[]{:T(128)S(6)} %max.9), kind=kLoop, calls=%fused_computation.9 | loop fusion | flops 180000 | bytes 2160004 | tf_op jit(solution)/shard_map/add | solution.py:40
  119.5 8.4 %collective-permute-done.10 = f32[300,600]{1,0:T(8,128)} collective-permute-done((f32[300,600]{1,0:T(8,128)}, f32[300,600]{1,0:T(8,128)}, u32[]{:S(2)}, u32[]{:S(2)}) %collective-permute-start.10) | collective-permute-done | bytes 720032 | tf_op jit(solution)/shard_map/ppermute | solution.py:38
  128.0 18.6 %collective-permute-done.13 = f32[300,600]{1,0:T(8,128)} collective-permute-done((f32[300,600]{1,0:T(8,128)}, f32[300,600]{1,0:T(8,128)}, u32[]{:S(2)}, u32[]{:S(2)}) %collective-permute-start.13) | collective-permute-done | bytes 720032 | tf_op jit(solution)/shard_map/ppermute | solution.py:41
  146.6 2.3 %fusion.2 = f32[300,600]{1,0:T(8,128)} fusion(f32[300,600]{1,0:T(8,128)} %collective-permute-done.13, f32[300,600]{1,0:T(8,128)} %collective-permute-done.10, f32[4,300,600]{2,1,0:T(8,128)S(1)} %bitcast_add_fusion, s32[]{:T(128)S(6)} %select_n.103), kind=kLoop, calls=%fused_computation.13 | loop fusion | flops 360000 | bytes 2880004 | tf_op jit(solution)/shard_map/add | solution.py:44
  148.9 1.5 collective-permute-start.14
  150.5 2.8 %select_bitcast_fusion.1 = (bf16[4,1,512,600]{2,3,0,1:T(8,128)(2,1)S(1)}, bf16[4,1,512,600]{2,3,0,1:T(8,128)(2,1)S(1)}) fusion(bf16[4,512,600]{1,2,0:T(8,128)(2,1)} %collective-permute-done.6, pred[]{:T(512)S(6)} %eq.11, pred[]{:T(512)S(6)} %eq.12, bf16[8,512,600]{1,2,0:T(8,128)(2,1)} %copy-done.1, s32[]{:T(128)S(6)} %select_n.97), kind=kLoop, calls=%fused_computation.7 | loop fusion | flops 2457600 | bytes 9830406 | tf_op jit(solution)/shard_map/stack | solution.py:75
  153.3 2.7 %pad_maximum_fusion = bf16[4,2,512,600]{2,3,0,1:T(8,128)(2,1)} fusion(bf16[4,1,512,600]{2,3,0,1:T(8,128)(2,1)S(1)} %get-tuple-element.8, bf16[4,1,512,600]{2,3,0,1:T(8,128)(2,1)S(1)} %get-tuple-element.7), kind=kLoop, calls=%fused_computation.1 | loop fusion | flops 2457600 | bytes 9830400 | tf_op jit(solution)/shard_map/stack | solution.py:75
  155.9 9.7 %copy.10 = bf16[4,2,512,600]{2,1,0,3:T(2,128)(2,1)} copy(bf16[4,2,512,600]{2,3,0,1:T(8,128)(2,1)} %pad_maximum_fusion) | data formatting | bytes 9830400 | tf_op jit(solution)/shard_map/stack | solution.py:75
  165.6 12.0 %reshape.26 = bf16[4096,600]{0,1:T(8,128)(2,1)} reshape(bf16[4,2,512,600]{2,1,0,3:T(2,128)(2,1)} %copy.10) | data formatting | bytes 9830400 | tf_op jit(solution)/shard_map/reshape | solution.py:76
  177.6 7.0 %convolution_bitcast_fusion = f32[1,4096,300]{1,2,0:T(8,128)} fusion(bf16[4096,600]{0,1:T(8,128)(2,1)} %reshape.26, f32[300,600]{1,0:T(8,128)} %fusion.2, f32[300,600]{1,0:T(8,128)S(1)} %collective-permute-done.14, f32[600]{0:T(1024)S(1)} %pad_maximum_fusion.2, f32[300]{0:T(512)S(1)} %get-tuple-element.15), kind=kOutput, calls=%fused_computation | convolution fusion | flops 1475459968 | bytes 11274000 | tf_op jit(solution)/shard_map/dot_general | solution.py:121
  184.6 9.7 %copy.14 = f32[1,4096,300]{1,0,2:T(1,128)} copy(f32[1,4096,300]{1,2,0:T(8,128)} %convolution_bitcast_fusion) | data formatting | bytes 9830400 | tf_op jit(solution)/shard_map/broadcast_in_dim | solution.py:124
  (54 shorter events, 15.7 us)
Async XLA Ops:
  7.4 14.6 %copy-start.2 = (bf16[512,600]{0,1:T(8,128)(2,1)}, bf16[512,600]{0,1:T(8,128)(2,1)S(1)}, u32[]{:S(2)}) copy-start(bf16[512,600]{0,1:T(8,128)(2,1)S(1)} %get-tuple-element.6) | copy-start | bytes 1843204
  17.1 44.6 %collective-permute-start.7 = (f32[4,300,600]{2,0,1:T(4,128)}, f32[4,300,600]{2,0,1:T(4,128)}, u32[]{:S(2)}, u32[]{:S(2)}) collective-permute-start(f32[4,300,600]{2,0,1:T(4,128)} %copy.12), channel_id=1, source_target_pairs={{0,1},{1,0},{2,3},{3,2},{4,5},{5,4},{6,7},{7,6},{8,9},{9,8},{10,11... | collective-permute-start | bytes 8640008 | tf_op jit(solution)/shard_map/ppermute | solution.py:32
  17.5 18.2 %collective-permute-start.1 = (bf16[512,600]{0,1:T(8,128)(2,1)S(1)}, bf16[512,600]{0,1:T(8,128)(2,1)S(1)}, u32[]{:S(2)}, u32[]{:S(2)}) collective-permute-start(bf16[512,600]{0,1:T(8,128)(2,1)S(1)} %get-tuple-element.6), channel_id=1, source_target_pairs={{0,4},{4,8},{8,12},{1,5},{5,9},{9,13},{2,6},{6,10},{10,14},{3,7},{... | collective-permute-start | bytes 1843208 | tf_op jit(solution)/shard_map/ppermute | solution.py:56
  22.1 17.9 %collective-permute-start = (bf16[512,600]{0,1:T(8,128)(2,1)S(1)}, bf16[512,600]{0,1:T(8,128)(2,1)S(1)}, u32[]{:S(2)}, u32[]{:S(2)}) collective-permute-start(bf16[512,600]{0,1:T(8,128)(2,1)S(1)} %get-tuple-element.6), channel_id=1, source_target_pairs={{4,0},{8,4},{12,8},{5,1},{9,5},{13,9},{6,2},{10,6},{14,10},{7,3},{... | collective-permute-start | bytes 1843208 | tf_op jit(solution)/shard_map/ppermute | solution.py:57
  35.8 4.2 %copy-start.4 = (bf16[512,600]{0,1:T(8,128)(2,1)}, bf16[512,600]{0,1:T(8,128)(2,1)S(1)}, u32[]{:S(2)}) copy-start(bf16[512,600]{0,1:T(8,128)(2,1)S(1)} %collective-permute-done.1) | copy-start | bytes 1843204
  35.8 5.5 %collective-permute-start.2 = (bf16[512,600]{0,1:T(8,128)(2,1)S(1)}, bf16[512,600]{0,1:T(8,128)(2,1)S(1)}, u32[]{:S(2)}, u32[]{:S(2)}) collective-permute-start(bf16[512,600]{0,1:T(8,128)(2,1)S(1)} %collective-permute-done.1), channel_id=1, source_target_pairs={{4,8},{8,12},{5,9},{9,13},{6,10},{10,14},{7,11},{11,15},{20,24},{2... | collective-permute-start | bytes 1843208 | tf_op jit(solution)/shard_map/ppermute | solution.py:56
  39.9 21.7 %copy-start.8 = (bf16[512,600]{0,1:T(8,128)(2,1)}, bf16[512,600]{0,1:T(8,128)(2,1)S(1)}, u32[]{:S(2)}) copy-start(bf16[512,600]{0,1:T(8,128)(2,1)S(1)} %collective-permute-done) | copy-start | bytes 1843204
  39.9 17.3 %collective-permute-start.4 = (bf16[512,600]{0,1:T(8,128)(2,1)S(1)}, bf16[512,600]{0,1:T(8,128)(2,1)}, u32[]{:S(2)}, u32[]{:S(2)}) collective-permute-start(bf16[512,600]{0,1:T(8,128)(2,1)S(1)} %collective-permute-done), channel_id=1, source_target_pairs={{4,0},{8,4},{5,1},{9,5},{6,2},{10,6},{7,3},{11,7},{20,16},{24,20},... | collective-permute-start | bytes 1843208 | tf_op jit(solution)/shard_map/ppermute | solution.py:57
  41.2 20.4 %copy-start.6 = (bf16[512,600]{0,1:T(8,128)(2,1)}, bf16[512,600]{0,1:T(8,128)(2,1)S(1)}, u32[]{:S(2)}) copy-start(bf16[512,600]{0,1:T(8,128)(2,1)S(1)} %collective-permute-done.2) | copy-start | bytes 1843204
  41.3 17.3 %collective-permute-start.3 = (bf16[512,600]{0,1:T(8,128)(2,1)S(1)}, bf16[512,600]{0,1:T(8,128)(2,1)S(1)}, u32[]{:S(2)}, u32[]{:S(2)}) collective-permute-start(bf16[512,600]{0,1:T(8,128)(2,1)S(1)} %collective-permute-done.2), channel_id=1, source_target_pairs={{8,12},{9,13},{10,14},{11,15},{24,28},{25,29},{26,30},{27,31}} | collective-permute-start | bytes 1843208 | tf_op jit(solution)/shard_map/ppermute | solution.py:56
  57.3 16.5 %collective-permute-start.5 = (bf16[512,600]{0,1:T(8,128)(2,1)}, bf16[512,600]{0,1:T(8,128)(2,1)S(1)}, u32[]{:S(2)}, u32[]{:S(2)}) collective-permute-start(bf16[512,600]{0,1:T(8,128)(2,1)} %collective-permute-done.4), channel_id=1, source_target_pairs={{4,0},{5,1},{6,2},{7,3},{20,16},{21,17},{22,18},{23,19}} | collective-permute-start | bytes 1843208 | tf_op jit(solution)/shard_map/ppermute | solution.py:57
  58.6 3.1 %copy-start.10 = (bf16[512,600]{0,1:T(8,128)(2,1)}, bf16[512,600]{0,1:T(8,128)(2,1)S(1)}, u32[]{:S(2)}) copy-start(bf16[512,600]{0,1:T(8,128)(2,1)S(1)} %collective-permute-done.3) | copy-start | bytes 1843204
  61.7 12.1 %copy-start = (bf16[8,512,600]{1,2,0:T(8,128)(2,1)S(1)}, bf16[8,512,600]{1,2,0:T(8,128)(2,1)}, u32[]{:S(2)}) copy-start(bf16[8,512,600]{1,2,0:T(8,128)(2,1)} %bitcast_dynamic-update-slice_fusion.2) | copy-start | bytes 14745604
  61.7 12.1 %copy-start.5 = (bf16[512,600]{0,1:T(8,128)(2,1)S(1)}, bf16[512,600]{0,1:T(8,128)(2,1)}, u32[]{:S(2)}) copy-start(bf16[512,600]{0,1:T(8,128)(2,1)} %copy-done.4) | copy-start | bytes 1843204
  61.7 12.3 %copy-start.3 = (bf16[512,600]{0,1:T(8,128)(2,1)S(1)}, bf16[512,600]{0,1:T(8,128)(2,1)}, u32[]{:S(2)}) copy-start(bf16[512,600]{0,1:T(8,128)(2,1)} %copy-done.2) | copy-start | bytes 1843204
  65.0 9.0 %copy-start.9 = (bf16[512,600]{0,1:T(8,128)(2,1)S(1)}, bf16[512,600]{0,1:T(8,128)(2,1)}, u32[]{:S(2)}) copy-start(bf16[512,600]{0,1:T(8,128)(2,1)} %copy-done.8) | copy-start | bytes 1843204
  65.0 9.0 %copy-start.11 = (bf16[512,600]{0,1:T(8,128)(2,1)S(1)}, bf16[512,600]{0,1:T(8,128)(2,1)}, u32[]{:S(2)}) copy-start(bf16[512,600]{0,1:T(8,128)(2,1)} %copy-done.10) | copy-start | bytes 1843204
  65.0 27.2 %copy-start.7 = (bf16[512,600]{0,1:T(8,128)(2,1)S(1)}, bf16[512,600]{0,1:T(8,128)(2,1)}, u32[]{:S(2)}) copy-start(bf16[512,600]{0,1:T(8,128)(2,1)} %copy-done.6) | copy-start | bytes 1843204
  66.1 19.9 %collective-permute-start.8 = (f32[300,600]{1,0:T(8,128)S(1)}, f32[300,600]{1,0:T(8,128)S(1)}, u32[]{:S(2)}, u32[]{:S(2)}) collective-permute-start(f32[300,600]{1,0:T(8,128)S(1)} %get-tuple-element.11), channel_id=1, source_target_pairs={{0,4},{1,5},{2,6},{3,7},{16,20},{17,21},{18,22},{19,23}} | collective-permute-start | bytes 2160008 | tf_op jit(solution)/shard_map/ppermute | solution.py:38
  74.2 23.3 %collective-permute-start.11 = (f32[300,600]{1,0:T(8,128)}, f32[300,600]{1,0:T(8,128)}, u32[]{:S(2)}, u32[]{:S(2)}) collective-permute-start(f32[300,600]{1,0:T(8,128)} %get-tuple-element.12), channel_id=1, source_target_pairs={{12,8},{13,9},{14,10},{15,11},{28,24},{29,25},{30,26},{31,27}} | collective-permute-start | bytes 2160008 | tf_op jit(solution)/shard_map/ppermute | solution.py:41
  87.0 18.9 %collective-permute-start.9 = (f32[300,600]{1,0:T(8,128)}, f32[300,600]{1,0:T(8,128)}, u32[]{:S(2)}, u32[]{:S(2)}) collective-permute-start(f32[300,600]{1,0:T(8,128)} %bitcast_add_fusion.3), channel_id=1, source_target_pairs={{0,4},{4,8},{1,5},{5,9},{2,6},{6,10},{3,7},{7,11},{16,20},{20,24},... | collective-permute-start | bytes 2160008 | tf_op jit(solution)/shard_map/ppermute | solution.py:38
  93.6 2.3 %copy-start.1 = (bf16[8,512,600]{1,2,0:T(8,128)(2,1)}, bf16[8,512,600]{1,2,0:T(8,128)(2,1)S(1)}, u32[]{:S(2)}) copy-start(bf16[8,512,600]{1,2,0:T(8,128)(2,1)S(1)} %bitcast_dynamic-update-slice_fusion.1) | copy-start | bytes 14745604
  95.9 23.5 %copy-start.12 = (f32[2400]{0:T(1024)S(1)}, f32[2400]{0:T(1024)}, u32[]{:S(2)}) copy-start(f32[2400]{0:T(1024)} %param.6) | copy-start | bytes 28804
  97.5 53.0 %collective-permute-start.6 = (bf16[4,512,600]{1,2,0:T(8,128)(2,1)}, bf16[4,512,600]{1,2,0:T(8,128)(2,1)}, u32[]{:S(2)}, u32[]{:S(2)}) collective-permute-start(bf16[4,512,600]{1,2,0:T(8,128)(2,1)} %constant_dynamic-slice_fusion), channel_id=1, source_target_pairs={{0,1},{1,0},{2,3},{3,2},{4,5},{5,4},{6,7},{7,6},{8,9},{9,8},{10,11... | collective-permute-start | bytes 7372808 | tf_op jit(solution)/shard_map/ppermute | solution.py:68
  108.7 6.5 %collective-permute-start.12 = (f32[300,600]{1,0:T(8,128)}, f32[300,600]{1,0:T(8,128)}, u32[]{:S(2)}, u32[]{:S(2)}) collective-permute-start(f32[300,600]{1,0:T(8,128)} %get-tuple-element.10), channel_id=1, source_target_pairs={{8,4},{12,8},{9,5},{13,9},{10,6},{14,10},{11,7},{15,11},{24,20},{2... | collective-permute-start | bytes 2160008 | tf_op jit(solution)/shard_map/ppermute | solution.py:41
  110.3 17.6 %collective-permute-start.10 = (f32[300,600]{1,0:T(8,128)}, f32[300,600]{1,0:T(8,128)}, u32[]{:S(2)}, u32[]{:S(2)}) collective-permute-start(f32[300,600]{1,0:T(8,128)} %get-tuple-element.9), channel_id=1, source_target_pairs={{0,4},{4,8},{8,12},{1,5},{5,9},{9,13},{2,6},{6,10},{10,14},{3,7},{... | collective-permute-start | bytes 2160008 | tf_op jit(solution)/shard_map/ppermute | solution.py:38
  117.3 29.3 %collective-permute-start.13 = (f32[300,600]{1,0:T(8,128)}, f32[300,600]{1,0:T(8,128)}, u32[]{:S(2)}, u32[]{:S(2)}) collective-permute-start(f32[300,600]{1,0:T(8,128)} %bitcast_add_fusion.2), channel_id=1, source_target_pairs={{4,0},{8,4},{12,8},{5,1},{9,5},{13,9},{6,2},{10,6},{14,10},{7,3},{... | collective-permute-start | bytes 2160008 | tf_op jit(solution)/shard_map/ppermute | solution.py:41
  148.9 28.6 %collective-permute-start.14 = (f32[300,600]{1,0:T(8,128)}, f32[300,600]{1,0:T(8,128)S(1)}, u32[]{:S(2)}, u32[]{:S(2)}) collective-permute-start(f32[300,600]{1,0:T(8,128)} %fusion.2), channel_id=1, source_target_pairs={{0,2},{2,0},{1,3},{3,1},{4,6},{6,4},{5,7},{7,5},{8,10},{10,8},{9,1... | collective-permute-start | bytes 2160008 | tf_op jit(solution)/shard_map/ppermute | solution.py:98

commit v4 on v2

--- a/solution.py
+++ b/solution.py
@@ -18,13 +18,20 @@
     return jnp.concatenate(owned, axis=1), jnp.concatenate(owner_energy, axis=0)
 
 
-def coupling_by_partials(local, owned, shards, width):
+def coupling_by_partials(local, owned, n_col, n_rep, width):
     rows = local.shape[0]
-    blocked = local.reshape(rows, shards, width)
+    blocked = local.reshape(rows, n_col, n_rep, width).transpose(0, 2, 1, 3)
     partial_value = lax.dot_general(
         blocked, owned, (((0,), (0,)), ((), ())), preferred_element_type=jnp.float32
     )
-    return lax.psum_scatter(partial_value, COLS, scatter_dimension=0, tiled=False)
+    partial_value = lax.psum_scatter(partial_value, "rep", scatter_dimension=0, tiled=False)
+    return lax.psum_scatter(partial_value, "col", scatter_dimension=0, tiled=False)
+
+
+def gather_by_chip(owned):
+    gathered = lax.all_gather(owned, "col", axis=0, tiled=False)
+    gathered = lax.all_gather(gathered, "rep", axis=1, tiled=False)
+    return gathered.reshape((-1,) + owned.shape[1:])
 
 
 def coupling_by_columns(b_aux, owned_all):
@@ -41,16 +48,17 @@
     return total
 
 
-def body(b_aux, occ_energies, vir_energies, owners, *, shards, n_aux, by_partials):
+def body(b_aux, occ_energies, vir_energies, owners, *, n_col, n_rep, n_aux, by_partials):
+    shards = n_col * n_rep
     local = b_aux[0]
     width = local.shape[1] // shards
     col_energy = (vir_energies[None, :] - occ_energies[:, None]).reshape(-1)
     shard_index = lax.axis_index(COLS)
     energy_mine = lax.dynamic_slice_in_dim(col_energy, shard_index * width, width, 0)
     owned, owner_energy = owner_columns(local, col_energy, owners, width)
-    owned_all = lax.all_gather(owned, COLS, axis=0, tiled=True)
+    owned_all = gather_by_chip(owned)
     if by_partials:
-        coupling = coupling_by_partials(local, owned, shards, width)
+        coupling = coupling_by_partials(local, owned, n_col, n_rep, width)
     else:
         coupling = coupling_by_columns(b_aux, owned_all)
     coupling = exchange_sum(coupling, "aux", n_aux)
@@ -63,7 +71,8 @@
 
 
 def solution(mesh):
-    shards = mesh.shape["col"] * mesh.shape["rep"]
+    n_col, n_rep = mesh.shape["col"], mesh.shape["rep"]
+    shards = n_col * n_rep
 
     def run(b_aux, occ_energies, vir_energies, owners):
         ncol = b_aux.shape[2]
@@ -71,7 +80,7 @@
         by_partials = partial_bytes <= PARTIAL_BYTES_MAX
         placed = (P(("groups", "aux"), COLS, None), P("groups"), P("groups"), P())
         return jax.shard_map(
-            lambda *a: body(*a, shards=shards, n_aux=mesh.shape["aux"], by_partials=by_partials),
+            lambda *a: body(*a, n_col=n_col, n_rep=n_rep, n_aux=mesh.shape["aux"], by_partials=by_partials),
             mesh=mesh,
             in_specs=placed,
             out_specs=P(("groups", "aux"), None, COLS),

time: 167 us -> 177 us (1.060)
  local copies, waits for them, and re-layouts: 15 us -> 27 us
  matrix products: 11.8 us -> 9.18 us
    all_gather x1 -> x2, waiting for transfers between devices: 51.1 us -> 39.3 us  [the longest x1 39.3 us: gather_by_chip(): gathered = lax.all_gather(owned, 'col', axis=0, tiled=False)]
    ppermute x1, waiting for transfers between devices: 0.01 us -> 11 us  [exchange_sum(): lax.ppermute(value, axis, [(i, (i + step) % size) for i in range(size)])]
    all_gather x0 -> x1, local copies, waits for them, and re-layouts: none -> 6.37 us  [gather_by_chip(): gathered = lax.all_gather(owned, 'col', axis=0, tiled=False)]
    unnamed x4 -> x7, local copies, waits for them, and re-layouts: 0.01 us -> 5.67 us
    dot_general x1, matrix products: 6.99 us -> 4.39 us  [body(): lax.dot_general(owned_all, amplitude, (((1,), (1,)), ((), ())), preferred...]
    reduce_scatter x1 -> x2, waiting for transfers between devices: 71.3 us -> 70.9 us  [the longest x1 54.2 us: coupling_by_partials(): lax.psum_scatter(partial_value, 'col', scatter_dimension=0, tiled=False)]
  transfers between devices with their start and end apart: 3 -> 5, of which waited for: 2 -> 4; matrix products, arithmetic and copies ran while one was open for 0% -> 7% of each run, Pallas kernels for 0% -> 0%
where the time goes in v4:
time: 177 us; the launch traced here: 176 us
  waiting for transfers between devices  122 us (69%)
  local copies, waits for them, and re-layouts  27 us (15%)
  between operations  16.8 us (9%)
  matrix products  9.18 us (5%)
    reduce_scatter x1, waiting for transfers between devices, coupling_by_partials(): lax.psum_scatter(partial_value, 'col', scatter_dimension=0, tiled=False)  54.2 us
    all_gather x1, waiting for transfers between devices, gather_by_chip(): gathered = lax.all_gather(owned, 'col', axis=0, tiled=False)  39.3 us
    reduce_scatter x1, waiting for transfers between devices, coupling_by_partials(): lax.psum_scatter(partial_value, 'rep', scatter_dimension=0, tiled=False)  16.6 us
    ppermute x1, waiting for transfers between devices, exchange_sum(): lax.ppermute(value, axis, [(i, (i + step) % size) for i in range(size)])  11 us
    broadcast_in_dim x1, local copies, waits for them, and re-layouts, body(): return gamma[None]  9.71 us
    all_gather x1, local copies, waits for them, and re-layouts, gather_by_chip(): gathered = lax.all_gather(owned, 'col', axis=0, tiled=False)  6.37 us
    unnamed x7, local copies, waits for them, and re-layouts  5.67 us
    dot_general x1, matrix products, coupling_by_partials(): lax.dot_general(blocked, owned, (((0,), (0,)), ((), ())), preferred_eleme...  4.79 us
  transfers between devices with their start and end apart: 5, of which 4 were waited for; matrix products, arithmetic and copies ran while one was open for 7% of the time, Pallas kernels for 0%

profile of v4, /device:TPU:0, one launch (start us, length us, event | category | flops | bytes accessed | tf_op | source)
XLA Modules:
  0.0 176.5 jit_solution(2716274532426126214)
XLA Ops:
  7.4 0.0 reduce-scatter.3.cloned.1.call-start
  7.4 1.3 fusion.8
  9.9 2.6 %reshape_squeeze.3 = bf16[512,4,2,300]{0,3,2,1:T(8,128)(2,1)S(1)} reshape(bf16[1,512,2400]{1,2,0:T(8,128)(2,1)} %param.4) | data formatting | bytes 4915200 | tf_op jit(solution)/shard_map/reshape;squeeze | solution.py:23
  12.6 1.2 dynamic-slice_bitcast_fusion.1
  13.8 0.1 pad_maximum_fusion
  13.9 0.0 copy-start
  13.9 4.8 %convolution_bitcast_fusion.1 = f32[2,4,300,600]{3,2,1,0:T(8,128)} fusion(bf16[512,600]{0,1:T(8,128)(2,1)S(1)} %pad_maximum_fusion, bf16[512,4,2,300]{0,3,2,1:T(8,128)(2,1)S(1)} %reshape_squeeze.3), kind=kOutput, calls=%fused_computation.1 | convolution fusion | flops 1474560000 | bytes 8832000 | tf_op jit(solution)/shard_map/dot_general | solution.py:24
  18.7 0.0 copy-done
  18.7 0.0 reduce-scatter.3.cloned.1.call-update
  18.7 0.0 all-gather.5.cloned.1.call-start
  18.8 0.5 all-gather.5.cloned.1.call-update
  19.3 0.0 reduce-scatter.5.cloned.1.call-start
  19.3 16.6 %reduce-scatter.3.cloned.1.call-done = f32[1,4,300,600]{3,2,1,0:T(8,128)} async-done(((f32[2,4,300,600]{3,2,1,0:T(8,128)}), f32[1,4,300,600]{3,2,1,0:T(8,128)}) %reduce-scatter.3.cloned.1.call-update) | async-done | bytes 2880016 | tf_op jit(solution)/shard_map/reduce_scatter | solution.py:27
  36.0 0.0 reduce-scatter.5.cloned.1.call-update
  36.0 0.0 copy-start.2
  36.0 0.0 all-gather.7.cloned.1.call-start
  36.1 39.3 %all-gather.5.cloned.1.call-done = bf16[2048,600]{0,1:T(8,128)(2,1)} async-done(((bf16[512,600]{0,1:T(8,128)(2,1)}), bf16[2048,600]{0,1:T(8,128)(2,1)}) %all-gather.5.cloned.1.call-update) | async-done | bytes 2457616 | tf_op jit(solution)/shard_map/all_gather | solution.py:32
  75.4 6.4 %reshape.27 = bf16[4,512,600]{1,0,2:T(4,128)(2,1)} reshape(bf16[2048,600]{0,1:T(8,128)(2,1)} %all-gather.5.cloned.1.call-done) | data formatting | bytes 4915200 | tf_op jit(solution)/shard_map/all_gather | solution.py:32
  81.8 0.0 all-gather.7.cloned.1.call-update
  81.8 54.2 %reduce-scatter.5.cloned.1.call-done = f32[1,300,600]{2,1,0:T(8,128)} async-done(((f32[4,300,600]{2,1,0:T(8,128)}), f32[1,300,600]{2,1,0:T(8,128)}) %reduce-scatter.5.cloned.1.call-update) | async-done | bytes 720016 | tf_op jit(solution)/shard_map/reduce_scatter | solution.py:28
  136.0 1.5 collective-permute-start
  138.1 0.0 copy-done.2
  138.1 0.1 fusion.7
  138.2 0.1 pad_maximum_fusion.1
  138.3 0.0 all-gather.7.cloned.1.call-done
  138.3 0.0 copy-start.1
  138.3 5.7 %copy.10 = bf16[75,8,4,1024]{3,1,2,0:T(8,128)(2,1)S(1)} copy(bf16[75,8,4,1024]{3,2,1,0:T(4,128)(2,1)} %bitcast.37) | data formatting | bytes 9830400
  144.0 11.0 %collective-permute-done = f32[300,600]{1,0:T(8,128)S(1)} collective-permute-done((f32[300,600]{1,0:T(8,128)}, f32[300,600]{1,0:T(8,128)S(1)}, u32[]{:S(2)}, u32[]{:S(2)}) %collective-permute-start) | collective-permute-done | bytes 720032 | tf_op jit(solution)/shard_map/ppermute | solution.py:47
  155.0 0.0 copy-done.1
  155.0 4.4 %convolution_bitcast_fusion = f32[1,4096,300]{1,2,0:T(8,128)} fusion(bf16[4096,600]{0,1:T(8,128)(2,1)S(1)} %bitcast.36, f32[300,600]{1,0:T(8,128)S(1)} %collective-permute-done, f32[600]{0:T(1024)S(1)} %pad_maximum_fusion.1, f32[300]{0:T(512)S(1)} %get-tuple-element.7, f32[1,300,600]{2,1,0:T(8,128)S(1)} %copy-done.1), kind=kOutput, calls=%fused_computation | convolution fusion | flops 1475459968 | bytes 11274000 | tf_op jit(solution)/shard_map/dot_general | solution.py:67
  159.4 9.7 %copy.8 = f32[1,4096,300]{1,0,2:T(1,128)} copy(f32[1,4096,300]{1,2,0:T(8,128)} %convolution_bitcast_fusion) | data formatting | bytes 9830400 | tf_op jit(solution)/shard_map/broadcast_in_dim | solution.py:70
  (1 shorter events, 0.0 us)
Async XLA Ops:
  7.4 28.6 %reduce-scatter.3.cloned.1.call-start = ((), (), s32[]{:S(2)}) async-start(), calls=%async_computation.2 | async-start | bytes 9338880 | tf_op jit(solution)/shard_map/reduce_scatter | solution.py:27
  13.9 4.8 %copy-start = (bf16[512,600]{0,1:T(8,128)(2,1)}, bf16[512,600]{0,1:T(8,128)(2,1)S(1)}, u32[]{:S(2)}) copy-start(bf16[512,600]{0,1:T(8,128)(2,1)S(1)} %pad_maximum_fusion) | copy-start | bytes 1843204
  18.7 56.7 %all-gather.5.cloned.1.call-start = ((), (), s32[]{:S(2)}) async-start(), calls=%async_computation.4 | async-start | bytes 3072000 | tf_op jit(solution)/shard_map/all_gather | solution.py:32
  19.3 116.7 %reduce-scatter.5.cloned.1.call-start = ((), (), s32[]{:S(2)}) async-start(), calls=%async_computation.3 | async-start | bytes 3891200 | tf_op jit(solution)/shard_map/reduce_scatter | solution.py:28
  36.0 102.1 %copy-start.2 = (f32[2400]{0:T(1024)S(1)}, f32[2400]{0:T(1024)}, u32[]{:S(2)}) copy-start(f32[2400]{0:T(1024)} %param.6) | copy-start | bytes 28804
  36.0 102.3 %all-gather.7.cloned.1.call-start = ((), (), s32[]{:S(2)}) async-start(), calls=%async_computation.5 | async-start | bytes 7372800 | tf_op jit(solution)/shard_map/all_gather | solution.py:33
  136.0 19.0 %collective-permute-start = (f32[300,600]{1,0:T(8,128)}, f32[300,600]{1,0:T(8,128)S(1)}, u32[]{:S(2)}, u32[]{:S(2)}) collective-permute-start(f32[300,600]{1,0:T(8,128)} %bitcast.39), channel_id=1, source_target_pairs={{0,2},{2,0},{1,3},{3,1},{4,6},{6,4},{5,7},{7,5},{8,10},{10,8},{9,1... | collective-permute-start | bytes 2160008 | tf_op jit(solution)/shard_map/ppermute | solution.py:47
  138.3 16.6 %copy-start.1 = (f32[1,300,600]{2,1,0:T(8,128)S(1)}, f32[1,300,600]{2,1,0:T(8,128)}, u32[]{:S(2)}) copy-start(f32[1,300,600]{2,1,0:T(8,128)} %reduce-scatter.5.cloned.1.call-done) | copy-start | bytes 2160004
Sparse Core Ops, SparseCore 0:
  18.8 17.1 reduce-scatter.2
  81.9 12.5 all-gather.6
Sparse Core Ops, SparseCore 1:
  20.8 54.6 all-gather.4
  77.6 58.4 reduce-scatter.4

commit v5 on v2

--- a/solution.py
+++ b/solution.py
@@ -41,6 +41,12 @@
     return total
 
 
+def gather_by_chip(owned):
+    gathered = lax.all_gather(owned, "col", axis=0, tiled=False)
+    gathered = lax.all_gather(gathered, "rep", axis=1, tiled=False)
+    return gathered.reshape((-1,) + owned.shape[1:])
+
+
 def body(b_aux, occ_energies, vir_energies, owners, *, shards, n_aux, by_partials):
     local = b_aux[0]
     width = local.shape[1] // shards
@@ -48,7 +54,7 @@
     shard_index = lax.axis_index(COLS)
     energy_mine = lax.dynamic_slice_in_dim(col_energy, shard_index * width, width, 0)
     owned, owner_energy = owner_columns(local, col_energy, owners, width)
-    owned_all = lax.all_gather(owned, COLS, axis=0, tiled=True)
+    owned_all = gather_by_chip(owned)
     if by_partials:
         coupling = coupling_by_partials(local, owned, shards, width)
     else:

time: 167 us -> 165 us (0.988)
  waiting for transfers between devices: 123 us -> 108 us
  local copies, waits for them, and re-layouts: 15 us -> 27.2 us
  matrix products: 11.8 us -> 9.18 us
    reduce_scatter x1, waiting for transfers between devices: 71.3 us -> 33.7 us  [coupling_by_partials(): lax.psum_scatter(partial_value, COLS, scatter_dimension=0, tiled=False)]
    all_gather x1 -> x2, waiting for transfers between devices: 51.1 us -> 66.7 us  [the longest x1 66.7 us: gather_by_chip(): gathered = lax.all_gather(owned, 'col', axis=0, tiled=False)]
    ppermute x1, waiting for transfers between devices: 0.01 us -> 7.75 us  [exchange_sum(): lax.ppermute(value, axis, [(i, (i + step) % size) for i in range(size)])]
    all_gather x0 -> x1, local copies, waits for them, and re-layouts: none -> 6.39 us  [gather_by_chip(): gathered = lax.all_gather(owned, 'col', axis=0, tiled=False)]
    unnamed x4 -> x7, local copies, waits for them, and re-layouts: 0.01 us -> 5.67 us
    dot_general x1, matrix products: 6.99 us -> 4.39 us  [body(): lax.dot_general(owned_all, amplitude, (((1,), (1,)), ((), ())), preferred...]
  transfers between devices with their start and end apart: 3 -> 4, of which waited for: 2 -> 3; matrix products, arithmetic and copies ran while one was open for 0% -> 12% of each run, Pallas kernels for 0% -> 0%
where the time goes in v5:
time: 165 us; the launch traced here: 164 us
  waiting for transfers between devices  108 us (65%)
  local copies, waits for them, and re-layouts  27.2 us (16%)
  between operations  16.8 us (10%)
  matrix products  9.18 us (6%)
    all_gather x1, waiting for transfers between devices, gather_by_chip(): gathered = lax.all_gather(owned, 'col', axis=0, tiled=False)  66.7 us
    reduce_scatter x1, waiting for transfers between devices, coupling_by_partials(): lax.psum_scatter(partial_value, COLS, scatter_dimension=0, tiled=False)  33.7 us
    broadcast_in_dim x1, local copies, waits for them, and re-layouts, body(): return gamma[None]  9.71 us
    ppermute x1, waiting for transfers between devices, exchange_sum(): lax.ppermute(value, axis, [(i, (i + step) % size) for i in range(size)])  7.75 us
    all_gather x1, local copies, waits for them, and re-layouts, gather_by_chip(): gathered = lax.all_gather(owned, 'col', axis=0, tiled=False)  6.39 us
    unnamed x7, local copies, waits for them, and re-layouts  5.67 us
    dot_general x1, matrix products, coupling_by_partials(): lax.dot_general(blocked, owned, (((0,), (0,)), ((), ())), preferred_eleme...  4.78 us
    dot_general x1, matrix products, body(): lax.dot_general(owned_all, amplitude, (((1,), (1,)), ((), ())), preferred...  4.39 us
  transfers between devices with their start and end apart: 4, of which 3 were waited for; matrix products, arithmetic and copies ran while one was open for 12% of the time, Pallas kernels for 0%

profile of v5, /device:TPU:0, one launch (start us, length us, event | category | flops | bytes accessed | tf_op | source)
XLA Modules:
  0.0 163.9 jit_solution(11857170951768703688)
XLA Ops:
  7.4 0.0 all-gather.5.cloned.1.call-start
  7.4 1.3 fusion.7
  9.9 1.3 dynamic-slice_bitcast_fusion.1
  11.2 0.9 pad_maximum_fusion
  12.1 0.0 all-gather.5.cloned.1.call-update
  12.2 0.0 copy-start
  12.2 0.0 reduce-scatter.2.cloned.1.call-start
  12.2 2.7 %reshape_squeeze.3 = bf16[512,8,300]{0,2,1:T(8,128)(2,1)S(1)} reshape(bf16[1,512,2400]{1,2,0:T(8,128)(2,1)} %param.4) | data formatting | bytes 4915200 | tf_op jit(solution)/shard_map/reshape;squeeze | solution.py:23
  14.9 0.0 copy-done
  14.9 4.8 %convolution_bitcast_fusion.1 = f32[8,300,600]{2,1,0:T(8,128)} fusion(bf16[512,8,300]{0,2,1:T(8,128)(2,1)S(1)} %reshape_squeeze.3, bf16[512,600]{0,1:T(8,128)(2,1)S(1)} %copy-done), kind=kOutput, calls=%fused_computation.1 | convolution fusion | flops 1474560000 | bytes 8832000 | tf_op jit(solution)/shard_map/dot_general | solution.py:24
  19.7 0.0 reduce-scatter.2.cloned.1.call-update
  19.7 0.0 copy-start.2
  19.7 0.0 all-gather.7.cloned.1.call-start
  19.8 66.7 %all-gather.5.cloned.1.call-done = bf16[2048,600]{0,1:T(8,128)(2,1)} async-done(((bf16[512,600]{0,1:T(8,128)(2,1)}), bf16[2048,600]{0,1:T(8,128)(2,1)}) %all-gather.5.cloned.1.call-update) | async-done | bytes 2457616 | tf_op jit(solution)/shard_map/all_gather | solution.py:45
  86.5 6.4 %reshape.27 = bf16[4,512,600]{1,0,2:T(4,128)(2,1)} reshape(bf16[2048,600]{0,1:T(8,128)(2,1)} %all-gather.5.cloned.1.call-done) | data formatting | bytes 4915200 | tf_op jit(solution)/shard_map/all_gather | solution.py:45
  92.9 0.0 all-gather.7.cloned.1.call-update
  92.9 33.7 %reduce-scatter.2.cloned.1.call-done = f32[1,300,600]{2,1,0:T(8,128)} async-done(((f32[8,300,600]{2,1,0:T(8,128)}), f32[1,300,600]{2,1,0:T(8,128)}) %reduce-scatter.2.cloned.1.call-update) | async-done | bytes 720016 | tf_op jit(solution)/shard_map/reduce_scatter | solution.py:27
  126.6 1.5 collective-permute-start
  128.7 0.0 copy-done.2
  128.7 0.1 fusion.6
  128.8 0.1 pad_maximum_fusion.1
  128.9 0.0 all-gather.7.cloned.1.call-done
  128.9 0.0 copy-start.1
  128.9 5.7 %copy.7 = bf16[75,8,4,1024]{3,1,2,0:T(8,128)(2,1)S(1)} copy(bf16[75,8,4,1024]{3,2,1,0:T(4,128)(2,1)} %bitcast.31) | data formatting | bytes 9830400
  134.6 7.8 %collective-permute-done = f32[300,600]{1,0:T(8,128)S(1)} collective-permute-done((f32[300,600]{1,0:T(8,128)}, f32[300,600]{1,0:T(8,128)S(1)}, u32[]{:S(2)}, u32[]{:S(2)}) %collective-permute-start) | collective-permute-done | bytes 720032 | tf_op jit(solution)/shard_map/ppermute | solution.py:40
  142.3 0.0 copy-done.1
  142.3 4.4 %convolution_bitcast_fusion = f32[1,4096,300]{1,2,0:T(8,128)} fusion(bf16[4096,600]{0,1:T(8,128)(2,1)S(1)} %bitcast.30, f32[300,600]{1,0:T(8,128)S(1)} %collective-permute-done, f32[600]{0:T(1024)S(1)} %pad_maximum_fusion.1, f32[300]{0:T(512)S(1)} %get-tuple-element.7, f32[1,300,600]{2,1,0:T(8,128)S(1)} %copy-done.1), kind=kOutput, calls=%fused_computation | convolution fusion | flops 1475459968 | bytes 11274000 | tf_op jit(solution)/shard_map/dot_general | solution.py:65
  146.7 9.7 %copy.6 = f32[1,4096,300]{1,0,2:T(1,128)} copy(f32[1,4096,300]{1,2,0:T(8,128)} %convolution_bitcast_fusion) | data formatting | bytes 9830400 | tf_op jit(solution)/shard_map/broadcast_in_dim | solution.py:68
  (1 shorter events, 0.0 us)
Async XLA Ops:
  7.4 79.1 %all-gather.5.cloned.1.call-start = ((), (), s32[]{:S(2)}) async-start(), calls=%async_computation.2 | async-start | bytes 3072000 | tf_op jit(solution)/shard_map/all_gather | solution.py:45
  12.2 2.8 %copy-start = (bf16[512,600]{0,1:T(8,128)(2,1)S(1)}, bf16[512,600]{0,1:T(8,128)(2,1)}, u32[]{:S(2)}) copy-start(bf16[512,600]{0,1:T(8,128)(2,1)} %pad_maximum_fusion) | copy-start | bytes 1843204
  12.2 114.4 %reduce-scatter.2.cloned.1.call-start = ((), (), s32[]{:S(2)}) async-start(), calls=%async_computation.1 | async-start | bytes 7004160 | tf_op jit(solution)/shard_map/reduce_scatter | solution.py:27
  19.7 109.0 %copy-start.2 = (f32[2400]{0:T(1024)S(1)}, f32[2400]{0:T(1024)}, u32[]{:S(2)}) copy-start(f32[2400]{0:T(1024)} %param.6) | copy-start | bytes 28804
  19.7 109.2 %all-gather.7.cloned.1.call-start = ((), (), s32[]{:S(2)}) async-start(), calls=%async_computation.3 | async-start | bytes 7372800 | tf_op jit(solution)/shard_map/all_gather | solution.py:46
  126.6 15.8 %collective-permute-start = (f32[300,600]{1,0:T(8,128)}, f32[300,600]{1,0:T(8,128)S(1)}, u32[]{:S(2)}, u32[]{:S(2)}) collective-permute-start(f32[300,600]{1,0:T(8,128)} %bitcast.32), channel_id=1, source_target_pairs={{0,2},{2,0},{1,3},{3,1},{4,6},{6,4},{5,7},{7,5},{8,10},{10,8},{9,1... | collective-permute-start | bytes 2160008 | tf_op jit(solution)/shard_map/ppermute | solution.py:40
  128.9 13.4 %copy-start.1 = (f32[1,300,600]{2,1,0:T(8,128)S(1)}, f32[1,300,600]{2,1,0:T(8,128)}, u32[]{:S(2)}) copy-start(f32[1,300,600]{2,1,0:T(8,128)} %reduce-scatter.2.cloned.1.call-done) | copy-start | bytes 2160004
Sparse Core Ops, SparseCore 0:
  12.3 74.1 all-gather.4
  93.0 17.8 all-gather.6
Sparse Core Ops, SparseCore 1:
  19.8 106.7 reduce-scatter.1

commit v6 on v2

--- a/solution.py
+++ b/solution.py
@@ -1,6 +1,8 @@
 import jax
 import jax.numpy as jnp
 from jax import lax
+from jax.experimental import pallas as pl
+from jax.experimental.pallas import tpu as pltpu
 from jax.sharding import PartitionSpec as P
 
 os_scale = 1.3
@@ -41,6 +43,25 @@
     return total
 
 
+def gamma_kernel(amp_ref, owned_ref, out_ref):
+    out_ref[:, 0, :] = lax.dot_general(
+        amp_ref[...], owned_ref[...], (((1,), (1,)), ((), ())), preferred_element_type=jnp.float32
+    )
+
+
+def gamma_rows_last(amplitude, owned_all):
+    width = amplitude.shape[0]
+    rows = owned_all.shape[0]
+    out = pl.pallas_call(
+        gamma_kernel,
+        out_shape=jax.ShapeDtypeStruct((width, 1, rows), jnp.float32),
+        in_specs=[pl.BlockSpec(memory_space=pltpu.VMEM)] * 2,
+        out_specs=pl.BlockSpec(memory_space=pltpu.VMEM),
+        compiler_params=pltpu.CompilerParams(vmem_limit_bytes=48 * 2**20),
+    )(amplitude, owned_all)
+    return out.transpose(1, 2, 0)
+
+
 def body(b_aux, occ_energies, vir_energies, owners, *, shards, n_aux, by_partials):
     local = b_aux[0]
     width = local.shape[1] // shards
@@ -56,10 +77,7 @@
     coupling = exchange_sum(coupling, "aux", n_aux)
     denominator = energy_mine[:, None] + owner_energy[None, :]
     amplitude = (os_scale * coupling / denominator).astype(jnp.bfloat16)
-    gamma = lax.dot_general(
-        owned_all, amplitude, (((1,), (1,)), ((), ())), preferred_element_type=jnp.float32
-    )
-    return gamma[None]
+    return gamma_rows_last(amplitude, owned_all)
 
 
 def solution(mesh):

time: 167 us -> 163 us (0.976)
  matrix products: 11.8 us -> 4.74 us
  local copies, waits for them, and re-layouts: 15 us -> 8.92 us
  Pallas kernels: 0 us -> 4.93 us
  other arithmetic: 0.16 us -> 2.7 us
    ppermute x1, waiting for transfers between devices: 0.01 us -> 14.9 us  [exchange_sum(): lax.ppermute(value, axis, [(i, (i + step) % size) for i in range(size)])]
    all_gather x1, waiting for transfers between devices: 51.1 us -> 37.6 us  [body(): owned_all = lax.all_gather(owned, COLS, axis=0, tiled=True)]
    broadcast_in_dim x1 -> x0, local copies, waits for them, and re-layouts: 9.71 us -> none  [body(): return gamma[None]]
    dot_general x1 -> x0, matrix products: 6.99 us -> none  [body(): lax.dot_general(owned_all, amplitude, (((1,), (1,)), ((), ())), preferred...]
    pallas_call x0 -> x1, Pallas kernels: none -> 4.93 us  [gamma_rows_last(): pl.pallas_call(gamma_kernel, out_shape=jax.ShapeDtypeStruct((width, 1, ro...]
    unnamed x4 -> x6, local copies, waits for them, and re-layouts: 0.01 us -> 2.5 us
  transfers between devices with their start and end apart: 3 -> 3, of which waited for: 2 -> 3; matrix products, arithmetic and copies ran while one was open for 0% -> 1% of each run, Pallas kernels for 0% -> 0%
where the time goes in v6:
time: 163 us
  waiting for transfers between devices  124 us (76%)
  between operations  15.4 us (9%)
  local copies, waits for them, and re-layouts  8.92 us (5%)
  Pallas kernels  4.93 us (3%)
  matrix products  4.74 us (3%)
  other arithmetic  2.7 us (2%)
    reduce_scatter x1, waiting for transfers between devices, coupling_by_partials(): lax.psum_scatter(partial_value, COLS, scatter_dimension=0, tiled=False)  71.3 us
    all_gather x1, waiting for transfers between devices, body(): owned_all = lax.all_gather(owned, COLS, axis=0, tiled=True)  37.6 us
    ppermute x1, waiting for transfers between devices, exchange_sum(): lax.ppermute(value, axis, [(i, (i + step) % size) for i in range(size)])  14.9 us
    pallas_call x1, Pallas kernels, gamma_rows_last(): pl.pallas_call(gamma_kernel, out_shape=jax.ShapeDtypeStruct((width, 1, ro...  4.93 us
    dot_general x1, matrix products, coupling_by_partials(): lax.dot_general(blocked, owned, (((0,), (0,)), ((), ())), preferred_eleme...  4.74 us
  transfers between devices with their start and end apart: 3, of which 3 were waited for; matrix products, arithmetic and copies ran while one was open for 1% of the time, Pallas kernels for 0%

profile of v6, /device:TPU:0, one launch (start us, length us, event | category | flops | bytes accessed | tf_op | source)
XLA Modules:
  0.0 162.6 jit_solution(1243917131729593134)
XLA Ops:
  6.5 0.0 reduce-scatter.2.cloned.1.call-start
  6.5 1.3 fusion.2
  9.2 2.6 %reshape_squeeze.3 = bf16[512,8,300]{0,2,1:T(8,128)(2,1)S(1)} reshape(bf16[1,512,2400]{1,2,0:T(8,128)(2,1)} %param.4) | data formatting | bytes 4915200 | tf_op jit(solution)/shard_map/reshape;squeeze | solution.py:25
  11.8 1.2 constant_dynamic-slice_fusion.1
  13.1 0.2 copy.8
  13.3 0.9 copy.9
  14.2 1.2 pad_maximum_fusion
  15.4 0.0 copy-start.1
  15.4 4.7 %convolution_bitcast_fusion = f32[8,300,600]{2,1,0:T(8,128)} fusion(bf16[512,8,300]{0,2,1:T(8,128)(2,1)S(1)} %reshape_squeeze.3, bf16[512,600]{1,0:T(8,128)(2,1)S(1)} %pad_maximum_fusion), kind=kOutput, calls=%fused_computation | convolution fusion | flops 1474560000 | bytes 8832000 | tf_op jit(solution)/shard_map/dot_general | solution.py:26
  20.1 0.0 copy-done.1
  20.1 0.0 copy-start.2
  20.2 0.0 reduce-scatter.2.cloned.1.call-update
  20.2 0.0 all-gather.2.cloned.1.call-start
  20.2 0.7 all-gather.2.cloned.1.call-update
  20.9 71.3 %reduce-scatter.2.cloned.1.call-done = f32[1,300,600]{2,1,0:T(8,128)} async-done(((f32[8,300,600]{2,1,0:T(8,128)}), f32[1,300,600]{2,1,0:T(8,128)}) %reduce-scatter.2.cloned.1.call-update) | async-done | bytes 720016 | tf_op jit(solution)/shard_map/reduce_scatter | solution.py:29
  92.2 1.5 collective-permute-start
  94.3 0.0 copy-done.2
  94.4 0.1 fusion.1
  94.5 0.1 pad_maximum_fusion.1
  94.5 14.9 %collective-permute-done = f32[300,600]{1,0:T(8,128)S(1)} collective-permute-done((f32[300,600]{1,0:T(8,128)}, f32[300,600]{1,0:T(8,128)S(1)}, u32[]{:S(2)}, u32[]{:S(2)}) %collective-permute-start) | collective-permute-done | bytes 720032 | tf_op jit(solution)/shard_map/ppermute | solution.py:42
  109.4 1.4 divide_convert_fusion.amp_ref
  110.8 37.6 %all-gather.2.cloned.1.call-done.owned_ref = bf16[4096,600]{1,0:T(8,128)(2,1)} async-done(((bf16[512,600]{1,0:T(8,128)(2,1)}), bf16[4096,600]{1,0:T(8,128)(2,1)}) %all-gather.2.cloned.1.call-update) | async-done | bytes 4915216 | tf_op jit(solution)/shard_map/all_gather | solution.py:72
  148.4 0.0 copy-start
  148.4 2.5 %copy-done = bf16[4096,600]{1,0:T(8,128)(2,1)S(1)} copy-done((bf16[4096,600]{1,0:T(8,128)(2,1)S(1)}, bf16[4096,600]{1,0:T(8,128)(2,1)}, u32[]{:S(2)}) %copy-start) | copy-done | bytes 4915224
  150.9 4.9 %shard_map.46 = f32[300,1,4096]{2,1,0:T(1,128)} custom-call(bf16[300,600]{1,0:T(8,128)(2,1)S(1)} %divide_convert_fusion.amp_ref, bf16[4096,600]{1,0:T(8,128)(2,1)S(1)} %copy-done), custom_call_target="tpu_custom_call" | custom-call | tf_op jit(solution)/shard_map/pallas_call | solution.py:55
  (1 shorter events, 0.0 us)
Async XLA Ops:
  6.5 85.7 %reduce-scatter.2.cloned.1.call-start = ((), (), s32[]{:S(2)}) async-start(), calls=%async_computation.1 | async-start | bytes 7004160 | tf_op jit(solution)/shard_map/reduce_scatter | solution.py:29
  15.4 4.8 %copy-start.1 = (bf16[512,600]{1,0:T(8,128)(2,1)}, bf16[512,600]{1,0:T(8,128)(2,1)S(1)}, u32[]{:S(2)}) copy-start(bf16[512,600]{1,0:T(8,128)(2,1)S(1)} %pad_maximum_fusion) | copy-start | bytes 1843204
  20.1 74.2 %copy-start.2 = (f32[2400]{0:T(1024)S(1)}, f32[2400]{0:T(1024)}, u32[]{:S(2)}) copy-start(f32[2400]{0:T(1024)} %param.6) | copy-start | bytes 28804
  20.2 128.2 %all-gather.2.cloned.1.call-start = ((), (), s32[]{:S(2)}) async-start(), calls=%async_computation.2 | async-start | bytes 5898240 | tf_op jit(solution)/shard_map/all_gather | solution.py:72
  92.2 17.2 %collective-permute-start = (f32[300,600]{1,0:T(8,128)}, f32[300,600]{1,0:T(8,128)S(1)}, u32[]{:S(2)}, u32[]{:S(2)}) collective-permute-start(f32[300,600]{1,0:T(8,128)} %bitcast.19), channel_id=1, source_target_pairs={{0,2},{2,0},{1,3},{3,1},{4,6},{6,4},{5,7},{7,5},{8,10},{10,8},{9,1... | collective-permute-start | bytes 2160008 | tf_op jit(solution)/shard_map/ppermute | solution.py:42
  148.4 2.5 %copy-start = (bf16[4096,600]{1,0:T(8,128)(2,1)S(1)}, bf16[4096,600]{1,0:T(8,128)(2,1)}, u32[]{:S(2)}) copy-start(bf16[4096,600]{1,0:T(8,128)(2,1)} %all-gather.2.cloned.1.call-done.owned_ref) | copy-start | bytes 14745604
Sparse Core Ops, SparseCore 0:
  20.3 71.8 reduce-scatter.1
  93.9 54.3 all-gather.1

commit v7 on v6

--- a/solution.py
+++ b/solution.py
@@ -7,7 +7,7 @@
 
 os_scale = 1.3
 COLS = ("col", "rep")
-PARTIAL_BYTES_MAX = 16 * 2**20
+PARTIAL_BYTES_MAX = 0
 
 
 def owner_columns(local, col_energy, owners, width):

time: 163 us -> 188 us (1.15)
  waiting for transfers between devices: 124 us -> 17.1 us
  blocking collectives: 0 us -> 69.1 us
  local copies, waits for them, and re-layouts: 8.92 us -> 57.1 us
  other arithmetic: 2.7 us -> 17.7 us
    reduce_scatter x1 -> x0, waiting for transfers between devices: 71.3 us -> none  [coupling_by_partials(): lax.psum_scatter(partial_value, COLS, scatter_dimension=0, tiled=False)]
    all_to_all x0 -> x1, blocking collectives: none -> 69.1 us  [coupling_by_columns(): moved = lax.all_to_all(b_aux, COLS, split_axis=2, concat_axis=1, tiled=True)]
    all_gather x1, waiting for transfers between devices: 37.6 us -> 0.02 us  [body(): owned_all = lax.all_gather(owned, COLS, axis=0, tiled=True)]
    unnamed x6 -> x12, local copies, waits for them, and re-layouts: 2.5 us -> 32.8 us
    all_to_all x0 -> x3, local copies, waits for them, and re-layouts: none -> 21.2 us  [coupling_by_columns(): moved = lax.all_to_all(b_aux, COLS, split_axis=2, concat_axis=1, tiled=True)]
    unnamed x0 -> x1, other arithmetic: none -> 16.3 us
    another operation x1 -> x0, local copies, waits for them, and re-layouts: 2.64 us -> none  [coupling_by_partials(): blocked = local.reshape(rows, shards, width)]
    ppermute x1, waiting for transfers between devices: 14.9 us -> 17.1 us  [exchange_sum(): lax.ppermute(value, axis, [(i, (i + step) % size) for i in range(size)])]
  transfers between devices with their start and end apart: 3 -> 2, of which waited for: 3 -> 1; matrix products, arithmetic and copies ran while one was open for 1% -> 35% of each run, Pallas kernels for 0% -> 0%
where the time goes in v7:
time: 188 us
  blocking collectives  69.1 us (37%)
  local copies, waits for them, and re-layouts  57.1 us (30%)
  other arithmetic  17.7 us (9%)
  waiting for transfers between devices  17.1 us (9%)
  between operations  15.4 us (8%)
  Pallas kernels  4.98 us (3%)
  matrix products  4.58 us (2%)
    all_to_all x1, blocking collectives, coupling_by_columns(): moved = lax.all_to_all(b_aux, COLS, split_axis=2, concat_axis=1, tiled=True)  69.1 us
    unnamed x12, local copies, waits for them, and re-layouts  32.8 us
    all_to_all x3, local copies, waits for them, and re-layouts, coupling_by_columns(): moved = lax.all_to_all(b_aux, COLS, split_axis=2, concat_axis=1, tiled=True)  21.2 us
    ppermute x1, waiting for transfers between devices, exchange_sum(): lax.ppermute(value, axis, [(i, (i + step) % size) for i in range(size)])  17.1 us
    unnamed x1, other arithmetic  16.3 us
    pallas_call x1, Pallas kernels, gamma_rows_last(): pl.pallas_call(gamma_kernel, out_shape=jax.ShapeDtypeStruct((width, 1, ro...  4.98 us
    dot_general x1, matrix products, coupling_by_columns(): lax.dot_general(moved[0], owned_all, (((0,), (0,)), ((), ())), preferred_...  4.58 us
  transfers between devices with their start and end apart: 2, of which 1 were waited for; matrix products, arithmetic and copies ran while one was open for 35% of the time, Pallas kernels for 0%

profile of v7, /device:TPU:0, one launch (start us, length us, event | category | flops | bytes accessed | tf_op | source)
XLA Modules:
  0.0 187.5 jit_solution(14700639447211360055)
XLA Ops:
  6.5 0.0 copy-start.1
  6.5 0.0 all-gather.2.cloned.1.call-start
  6.5 1.4 fusion.1
  9.2 1.2 constant_dynamic-slice_fusion.1
  10.5 0.2 copy.11
  10.7 0.2 copy.10
  10.9 1.1 pad_maximum_fusion
  12.0 0.0 all-gather.2.cloned.1.call-update
  12.0 0.0 copy-done.1
  12.0 21.7 %copy.19 = bf16[1,512,2400]{1,0,2:T(2,128)(2,1)} copy(bf16[1,512,2400]{1,2,0:T(8,128)(2,1)S(1)} %copy-done.1) | data formatting | bytes 4915200 | tf_op args[0]
  33.7 0.5 broadcast.5
  34.2 16.3 %reduce.2 = bf16[2400,512]{1,0:T(8,128)(2,1)S(1)} reduce(bf16[2400,1,512]{2,1,0:T(2,128)(2,1)} %bitcast.27, bf16[]{:T(256)} %broadcast.5), dimensions={1}, to_apply=%bitcast.25.reduce_sub_computation | reduce | bytes 4915202
  50.5 2.4 %reshape.25 = bf16[8,2,76800]{2,1,0:T(2,128)(2,1)} reshape(bf16[2400,512]{1,0:T(8,128)(2,1)S(1)} %reduce.2) | data formatting | bytes 4915200
  52.9 69.1 %all_to_all.15 = bf16[8,2,76800]{2,1,0:T(2,128)(2,1)S(1)} all-to-all(bf16[8,2,76800]{2,1,0:T(2,128)(2,1)} %reshape.25), channel_id=1, replica_groups=mesh['groups'=2,'col'=4,'aux'=2,'rep'=2] {'col','rep'}, dimensions={0} | all-to-all | bytes 4915200 | tf_op jit(solution)/shard_map/all_to_all | solution.py:33
  122.0 4.4 %reshape.26 = bf16[2400,1,512]{2,1,0:T(2,128)(2,1)} reshape(bf16[8,2,76800]{2,1,0:T(2,128)(2,1)S(1)} %all_to_all.15) | data formatting | bytes 4915200
  126.4 17.2 %bitcast_reduce_fusion = bf16[512,2400]{0,1:T(8,128)(2,1)} fusion(bf16[2400,1,512]{2,1,0:T(2,128)(2,1)} %reshape.26), kind=kLoop, calls=%fused_computation.10 | loop fusion | bytes 4915200 | tf_op jit(solution)/shard_map/all_to_all | solution.py:33
  143.6 2.6 %all_to_all.12 = bf16[1,512,8,300]{1,3,2,0:T(8,128)(2,1)S(1)} reshape(bf16[512,2400]{0,1:T(8,128)(2,1)} %bitcast_reduce_fusion) | data formatting | bytes 4915200 | tf_op jit(solution)/shard_map/all_to_all | solution.py:33
  146.2 1.4 copy.18
  147.6 0.2 pad.4
  147.8 1.1 copy.15
  148.9 0.0 all-gather.2.cloned.1.call-done.owned_ref
  148.9 0.0 copy-start.2
  148.9 4.6 %convolution_bitcast_fusion = f32[300,600]{1,0:T(8,128)S(1)} fusion(bf16[4096,600]{1,0:T(8,128)(2,1)} %all-gather.2.cloned.1.call-done.owned_ref, bf16[4096,300]{0,1:T(8,128)(2,1)S(1)} %bitcast.31), kind=kOutput, calls=%fused_computation.1 | convolution fusion | flops 1474560000 | bytes 8092800 | tf_op jit(solution)/shard_map/dot_general | solution.py:34
  153.5 1.5 collective-permute-start
  155.7 0.0 copy-done.2
  155.7 0.1 fusion
  155.8 0.1 pad_maximum_fusion.1
  155.9 17.1 %collective-permute-done = f32[300,600]{1,0:T(8,128)S(1)} collective-permute-done((f32[300,600]{1,0:T(8,128)S(1)}, f32[300,600]{1,0:T(8,128)S(1)}, u32[]{:S(2)}, u32[]{:S(2)}) %collective-permute-start) | collective-permute-done | bytes 720032 | tf_op jit(solution)/shard_map/ppermute | solution.py:42
  173.0 0.2 divide_convert_fusion.amp_ref
  173.2 0.0 copy-start
  173.2 2.5 %copy-done = bf16[4096,600]{1,0:T(8,128)(2,1)S(1)} copy-done((bf16[4096,600]{1,0:T(8,128)(2,1)S(1)}, bf16[4096,600]{1,0:T(8,128)(2,1)}, u32[]{:S(2)}) %copy-start) | copy-done | bytes 4915224
  175.7 5.0 %shard_map.46 = f32[300,1,4096]{2,1,0:T(1,128)} custom-call(bf16[300,600]{1,0:T(8,128)(2,1)S(1)} %divide_convert_fusion.amp_ref, bf16[4096,600]{1,0:T(8,128)(2,1)S(1)} %copy-done), custom_call_target="tpu_custom_call" | custom-call | tf_op jit(solution)/shard_map/pallas_call | solution.py:55
  (1 shorter events, 0.0 us)
Async XLA Ops:
  6.5 5.5 %copy-start.1 = (bf16[1,512,2400]{1,2,0:T(8,128)(2,1)S(1)}, bf16[1,512,2400]{1,2,0:T(8,128)(2,1)}, u32[]{:S(2)}) copy-start(bf16[1,512,2400]{1,2,0:T(8,128)(2,1)} %param.4) | copy-start | bytes 7372804
  6.5 142.4 %all-gather.2.cloned.1.call-start = ((), (), s32[]{:S(2)}) async-start(), calls=%async_computation.1 | async-start | bytes 5898240 | tf_op jit(solution)/shard_map/all_gather | solution.py:72
  148.9 6.8 %copy-start.2 = (f32[2400]{0:T(1024)S(1)}, f32[2400]{0:T(1024)}, u32[]{:S(2)}) copy-start(f32[2400]{0:T(1024)} %param.6) | copy-start | bytes 28804
  153.5 19.5 %collective-permute-start = (f32[300,600]{1,0:T(8,128)S(1)}, f32[300,600]{1,0:T(8,128)S(1)}, u32[]{:S(2)}, u32[]{:S(2)}) collective-permute-start(f32[300,600]{1,0:T(8,128)S(1)} %convolution_bitcast_fusion), channel_id=1, source_target_pairs={{0,2},{2,0},{1,3},{3,1},{4,6},{6,4},{5,7},{7,5},{8,10},{10,8},{9,1... | collective-permute-start | bytes 2160008 | tf_op jit(solution)/shard_map/ppermute | solution.py:42
  173.2 2.5 %copy-start = (bf16[4096,600]{1,0:T(8,128)(2,1)S(1)}, bf16[4096,600]{1,0:T(8,128)(2,1)}, u32[]{:S(2)}) copy-start(bf16[4096,600]{1,0:T(8,128)(2,1)} %all-gather.2.cloned.1.call-done.owned_ref) | copy-start | bytes 14745604
Sparse Core Ops, SparseCore 0:
  12.1 65.7 all-gather.1

commit v8 on v7

--- a/solution.py
+++ b/solution.py
@@ -29,10 +29,13 @@
     return lax.psum_scatter(partial_value, COLS, scatter_dimension=0, tiled=False)
 
 
-def coupling_by_columns(b_aux, owned_all):
-    moved = lax.all_to_all(b_aux, COLS, split_axis=2, concat_axis=1, tiled=True)
+def coupling_by_columns(local, owned_all, shards, width):
+    rows = local.shape[0]
+    blocked = local.reshape(rows, shards, width).transpose(1, 0, 2)
+    moved = lax.all_to_all(blocked, COLS, split_axis=0, concat_axis=0, tiled=True)
     return lax.dot_general(
-        moved[0], owned_all, (((0,), (0,)), ((), ())), preferred_element_type=jnp.float32
+        moved.reshape(shards * rows, width), owned_all, (((0,), (0,)), ((), ())),
+        preferred_element_type=jnp.float32,
     )
 
 
@@ -73,7 +76,7 @@
     if by_partials:
         coupling = coupling_by_partials(local, owned, shards, width)
     else:
-        coupling = coupling_by_columns(b_aux, owned_all)
+        coupling = coupling_by_columns(local, owned_all, shards, width)
     coupling = exchange_sum(coupling, "aux", n_aux)
     denominator = energy_mine[:, None] + owner_energy[None, :]
     amplitude = (os_scale * coupling / denominator).astype(jnp.bfloat16)

time: 188 us -> 162 us (0.86)
  local copies, waits for them, and re-layouts: 57.1 us -> 10.9 us
  blocking collectives: 69.1 us -> 106 us
  other arithmetic: 17.7 us -> 1.37 us
    all_to_all x1, blocking collectives: 69.1 us -> 106 us  [coupling_by_columns(): lax.all_to_all(blocked, COLS, split_axis=0, concat_axis=0, tiled=True)]
    unnamed x12 -> x6, local copies, waits for them, and re-layouts: 32.8 us -> 3.78 us
    all_to_all x3 -> x1, local copies, waits for them, and re-layouts: 21.2 us -> 1.37 us  [coupling_by_columns(): lax.all_to_all(blocked, COLS, split_axis=0, concat_axis=0, tiled=True)]
    unnamed x1 -> x0, other arithmetic: 16.3 us -> none
    another operation x0 -> x1, local copies, waits for them, and re-layouts: none -> 2.64 us  [coupling_by_columns(): blocked = local.reshape(rows, shards, width).transpose(1, 0, 2)]
  transfers between devices with their start and end apart: 2 -> 2, of which waited for: 1 -> 1; matrix products, arithmetic and copies ran while one was open for 35% -> 3% of each run, Pallas kernels for 0% -> 0%
where the time goes in v8:
time: 162 us; the launch traced here: 161 us
  blocking collectives  106 us (65%)
  waiting for transfers between devices  16.6 us (10%)
  between operations  15.5 us (10%)
  local copies, waits for them, and re-layouts  10.9 us (7%)
  Pallas kernels  4.99 us (3%)
  matrix products  4.59 us (3%)
    all_to_all x1, blocking collectives, coupling_by_columns(): lax.all_to_all(blocked, COLS, split_axis=0, concat_axis=0, tiled=True)  106 us
    ppermute x1, waiting for transfers between devices, exchange_sum(): lax.ppermute(value, axis, [(i, (i + step) % size) for i in range(size)])  16.6 us
    pallas_call x1, Pallas kernels, gamma_rows_last(): pl.pallas_call(gamma_kernel, out_shape=jax.ShapeDtypeStruct((width, 1, ro...  4.99 us
    dot_general x1, matrix products, coupling_by_columns(): lax.dot_general(moved.reshape(shards * rows, width), owned_all, (((0,), (...  4.59 us
    unnamed x6, local copies, waits for them, and re-layouts  3.78 us
  transfers between devices with their start and end apart: 2, of which 1 were waited for; matrix products, arithmetic and copies ran while one was open for 3% of the time, Pallas kernels for 0%

profile of v8, /device:TPU:0, one launch (start us, length us, event | category | flops | bytes accessed | tf_op | source)
XLA Modules:
  0.0 161.3 jit_solution(4810374962115206833)
XLA Ops:
  6.5 0.0 all-gather.2.cloned.1.call-start
  6.5 1.4 fusion.1
  9.3 1.2 constant_dynamic-slice_fusion.1
  10.5 0.2 copy.7
  10.7 0.2 copy.8
  10.9 1.1 pad_maximum_fusion
  12.0 0.0 all-gather.2.cloned.1.call-update
  12.0 2.6 %reshape_squeeze.3 = bf16[512,8,300]{0,2,1:T(8,128)(2,1)S(1)} reshape(bf16[1,512,2400]{1,2,0:T(8,128)(2,1)} %param.4) | data formatting | bytes 4915200 | tf_op jit(solution)/shard_map/reshape;squeeze | solution.py:34
  14.7 105.7 %all_to_all.5 = bf16[8,512,300]{1,2,0:T(8,128)(2,1)S(1)} all-to-all(bf16[8,512,300]{1,2,0:T(8,128)(2,1)S(1)} %bitcast.22), channel_id=1, replica_groups=mesh['groups'=2,'col'=4,'aux'=2,'rep'=2] {'col','rep'}, dimensions={0} | all-to-all | bytes 4915200 | tf_op jit(solution)/shard_map/all_to_all | solution.py:35
  120.4 1.4 copy.12
  121.8 0.2 pad.4
  121.9 1.1 copy.10
  123.1 0.0 all-gather.2.cloned.1.call-done.owned_ref
  123.1 0.0 copy-start.1
  123.1 4.6 %convolution_bitcast_fusion = f32[300,600]{1,0:T(8,128)S(1)} fusion(bf16[4096,600]{1,0:T(8,128)(2,1)} %all-gather.2.cloned.1.call-done.owned_ref, bf16[4096,300]{0,1:T(8,128)(2,1)S(1)} %bitcast.24), kind=kOutput, calls=%fused_computation.1 | convolution fusion | flops 1474560000 | bytes 8092800 | tf_op jit(solution)/shard_map/dot_general | solution.py:36
  127.7 1.6 collective-permute-start
  129.9 0.0 copy-done.1
  129.9 0.1 fusion
  130.0 0.1 pad_maximum_fusion.1
  130.1 16.6 %collective-permute-done = f32[300,600]{1,0:T(8,128)S(1)} collective-permute-done((f32[300,600]{1,0:T(8,128)S(1)}, f32[300,600]{1,0:T(8,128)S(1)}, u32[]{:S(2)}, u32[]{:S(2)}) %collective-permute-start) | collective-permute-done | bytes 720032 | tf_op jit(solution)/shard_map/ppermute | solution.py:45
  146.7 0.2 divide_convert_fusion.amp_ref
  146.9 0.0 copy-start
  146.9 2.5 %copy-done = bf16[4096,600]{1,0:T(8,128)(2,1)S(1)} copy-done((bf16[4096,600]{1,0:T(8,128)(2,1)S(1)}, bf16[4096,600]{1,0:T(8,128)(2,1)}, u32[]{:S(2)}) %copy-start) | copy-done | bytes 4915224
  149.4 5.0 %shard_map.46 = f32[300,1,4096]{2,1,0:T(1,128)} custom-call(bf16[300,600]{1,0:T(8,128)(2,1)S(1)} %divide_convert_fusion.amp_ref, bf16[4096,600]{1,0:T(8,128)(2,1)S(1)} %copy-done), custom_call_target="tpu_custom_call" | custom-call | tf_op jit(solution)/shard_map/pallas_call | solution.py:58
  (1 shorter events, 0.0 us)
Async XLA Ops:
  6.5 116.6 %all-gather.2.cloned.1.call-start = ((), (), s32[]{:S(2)}) async-start(), calls=%async_computation.1 | async-start | bytes 5898240 | tf_op jit(solution)/shard_map/all_gather | solution.py:75
  123.1 6.8 %copy-start.1 = (f32[2400]{0:T(1024)S(1)}, f32[2400]{0:T(1024)}, u32[]{:S(2)}) copy-start(f32[2400]{0:T(1024)} %param.6) | copy-start | bytes 28804
  127.7 19.0 %collective-permute-start = (f32[300,600]{1,0:T(8,128)S(1)}, f32[300,600]{1,0:T(8,128)S(1)}, u32[]{:S(2)}, u32[]{:S(2)}) collective-permute-start(f32[300,600]{1,0:T(8,128)S(1)} %convolution_bitcast_fusion), channel_id=1, source_target_pairs={{0,2},{2,0},{1,3},{3,1},{4,6},{6,4},{5,7},{7,5},{8,10},{10,8},{9,1... | collective-permute-start | bytes 2160008 | tf_op jit(solution)/shard_map/ppermute | solution.py:45
  146.9 2.5 %copy-start = (bf16[4096,600]{1,0:T(8,128)(2,1)S(1)}, bf16[4096,600]{1,0:T(8,128)(2,1)}, u32[]{:S(2)}) copy-start(bf16[4096,600]{1,0:T(8,128)(2,1)} %all-gather.2.cloned.1.call-done.owned_ref) | copy-start | bytes 14745604
Sparse Core Ops, SparseCore 0:
  12.1 105.7 all-gather.1

commit v9 on v8

--- a/solution.py
+++ b/solution.py
@@ -8,6 +8,7 @@
 os_scale = 1.3
 COLS = ("col", "rep")
 PARTIAL_BYTES_MAX = 0
+LANES = 128
 
 
 def owner_columns(local, col_energy, owners, width):
@@ -29,14 +30,24 @@
     return lax.psum_scatter(partial_value, COLS, scatter_dimension=0, tiled=False)
 
 
-def coupling_by_columns(local, owned_all, shards, width):
+def coupling_by_columns(local, owned_all, shards, width, n_aux):
     rows = local.shape[0]
     blocked = local.reshape(rows, shards, width).transpose(1, 0, 2)
-    moved = lax.all_to_all(blocked, COLS, split_axis=0, concat_axis=0, tiled=True)
-    return lax.dot_general(
-        moved.reshape(shards * rows, width), owned_all, (((0,), (0,)), ((), ())),
-        preferred_element_type=jnp.float32,
-    )
+    edges = sorted(set([0, min(LANES, width), width]))
+    pieces = {}
+    previous = None
+    for first, last in list(zip(edges[:-1], edges[1:]))[::-1]:
+        chunk = blocked[:, :, first:last]
+        if previous is not None:
+            chunk, _ = lax.optimization_barrier((chunk, previous))
+        moved = lax.all_to_all(chunk, COLS, split_axis=0, concat_axis=0, tiled=True)
+        piece = lax.dot_general(
+            moved.reshape(shards * rows, last - first), owned_all, (((0,), (0,)), ((), ())),
+            preferred_element_type=jnp.float32,
+        )
+        previous = piece
+        pieces[first] = exchange_sum(piece, "aux", n_aux)
+    return jnp.concatenate([pieces[first] for first in sorted(pieces)], axis=0)
 
 
 def exchange_sum(value, axis, size):
@@ -75,9 +86,9 @@
     owned_all = lax.all_gather(owned, COLS, axis=0, tiled=True)
     if by_partials:
         coupling = coupling_by_partials(local, owned, shards, width)
+        coupling = exchange_sum(coupling, "aux", n_aux)
     else:
-        coupling = coupling_by_columns(local, owned_all, shards, width)
-    coupling = exchange_sum(coupling, "aux", n_aux)
+        coupling = coupling_by_columns(local, owned_all, shards, width, n_aux)
     denominator = energy_mine[:, None] + owner_energy[None, :]
     amplitude = (os_scale * coupling / denominator).astype(jnp.bfloat16)
     return gamma_rows_last(amplitude, owned_all)

time: 162 us -> 163 us (level)
  blocking collectives: 106 us -> 0 us
  waiting for transfers between devices: 16.6 us -> 107 us
  starting transfers between devices: 1.56 us -> 13 us
  local copies, waits for them, and re-layouts: 10.9 us -> 13.9 us
  matrix products: 4.59 us -> 7.28 us
    all_to_all x1 -> x0, blocking collectives: 106 us -> none  [coupling_by_columns(): lax.all_to_all(blocked, COLS, split_axis=0, concat_axis=0, tiled=True)]
    all_to_all x0 -> x2, waiting for transfers between devices: none -> 94.9 us  [coupling_by_columns(): moved = lax.all_to_all(chunk, COLS, split_axis=0, concat_axis=0, tiled=True)]
    all_to_all x0 -> x2, starting transfers between devices: none -> 9.89 us  [coupling_by_columns(): moved = lax.all_to_all(chunk, COLS, split_axis=0, concat_axis=0, tiled=True)]
    ppermute x1 -> x2, waiting for transfers between devices: 16.6 us -> 7.53 us  [exchange_sum(): lax.ppermute(value, axis, [(i, (i + step) % size) for i in range(size)])]
    all_gather x1, waiting for transfers between devices: 0.02 us -> 4.29 us  [body(): owned_all = lax.all_gather(owned, COLS, axis=0, tiled=True)]
    dot_general x1 -> x2, matrix products: 4.59 us -> 7.28 us  [coupling_by_columns(): lax.dot_general(moved.reshape(shards * rows, last - first), owned_all, ((...]
    slice x0 -> x2, local copies, waits for them, and re-layouts: none -> 2.25 us  [coupling_by_columns(): chunk = blocked[:, :, first:last]]
  transfers between devices with their start and end apart: 2 -> 5, of which waited for: 1 -> 4; matrix products, arithmetic and copies ran while one was open for 3% -> 7% of each run, Pallas kernels for 0% -> 0%
where the time goes in v9:
time: 163 us
  waiting for transfers between devices  107 us (66%)
  between operations  15.4 us (9%)
  local copies, waits for them, and re-layouts  13.9 us (9%)
  starting transfers between devices  13 us (8%)
  matrix products  7.28 us (4%)
  Pallas kernels  4.99 us (3%)
    all_to_all x2, waiting for transfers between devices, coupling_by_columns(): moved = lax.all_to_all(chunk, COLS, split_axis=0, concat_axis=0, tiled=True)  94.9 us
    all_to_all x2, starting transfers between devices, coupling_by_columns(): moved = lax.all_to_all(chunk, COLS, split_axis=0, concat_axis=0, tiled=True)  9.89 us
    ppermute x2, waiting for transfers between devices, exchange_sum(): lax.ppermute(value, axis, [(i, (i + step) % size) for i in range(size)])  7.53 us
    dot_general x2, matrix products, coupling_by_columns(): lax.dot_general(moved.reshape(shards * rows, last - first), owned_all, ((...  7.28 us
    pallas_call x1, Pallas kernels, gamma_rows_last(): pl.pallas_call(gamma_kernel, out_shape=jax.ShapeDtypeStruct((width, 1, ro...  4.99 us
    all_gather x1, waiting for transfers between devices, body(): owned_all = lax.all_gather(owned, COLS, axis=0, tiled=True)  4.29 us
  transfers between devices with their start and end apart: 5, of which 4 were waited for; matrix products, arithmetic and copies ran while one was open for 7% of the time, Pallas kernels for 0%

profile of v9, /device:TPU:0, one launch (start us, length us, event | category | flops | bytes accessed | tf_op | source)
XLA Modules:
  0.0 162.8 jit_solution(9327889066807295462)
XLA Ops:
  6.5 0.0 all-gather.2.cloned.1.call-start
  6.5 1.3 fusion.3
  9.1 1.2 constant_dynamic-slice_fusion.1
  10.3 0.2 copy.9
  10.5 0.2 copy.10
  10.7 1.1 pad_maximum_fusion
  11.9 0.0 all-gather.2.cloned.1.call-update
  11.9 2.6 %reshape_squeeze.3 = bf16[512,8,300]{0,2,1:T(8,128)(2,1)S(1)} reshape(bf16[1,512,2400]{1,2,0:T(8,128)(2,1)} %param.4) | data formatting | bytes 4915200 | tf_op jit(solution)/shard_map/reshape;squeeze | solution.py:35
  14.5 1.2 slice.17
  15.7 6.3 %all-to-all-start = ((bf16[8,512,172]{1,2,0:T(8,128)(2,1)}), bf16[8,512,172]{1,2,0:T(8,128)(2,1)}, u32[]{:S(2)}, u32[]{:S(2)}) async-start(bf16[8,512,172]{1,2,0:T(8,128)(2,1)} %slice.17), calls=%async_computation | async-start | bytes 2883584 | tf_op jit(solution)/shard_map/all_to_all | solution.py:43
  22.1 1.0 slice.16
  23.1 70.6 %all-to-all-done = bf16[8,512,172]{1,2,0:T(8,128)(2,1)} async-done(((bf16[8,512,172]{1,2,0:T(8,128)(2,1)}), bf16[8,512,172]{1,2,0:T(8,128)(2,1)}, u32[]{:S(2)}, u32[]{:S(2)}) %all-to-all-start) | async-done | bytes 1409056 | tf_op jit(solution)/shard_map/all_to_all | solution.py:43
  93.7 2.1 %copy.18 = bf16[8,512,172]{1,0,2:T(8,128)(2,1)S(1)} copy(bf16[8,512,172]{1,2,0:T(8,128)(2,1)} %all-to-all-done) | data formatting | bytes 2818048 | tf_op jit(solution)/shard_map/all_to_all | solution.py:43
  95.8 0.1 pad.6
  95.9 0.6 copy.16
  96.5 4.3 %all-gather.2.cloned.1.call-done.owned_ref = bf16[4096,600]{1,0:T(8,128)(2,1)} async-done(((bf16[512,600]{1,0:T(8,128)(2,1)}), bf16[4096,600]{1,0:T(8,128)(2,1)}) %all-gather.2.cloned.1.call-update) | async-done | bytes 4915216 | tf_op jit(solution)/shard_map/all_gather | solution.py:86
  100.8 3.8 %convolution_bitcast_fusion = f32[172,600]{1,0:T(8,128)S(1)} fusion(bf16[4096,600]{1,0:T(8,128)(2,1)} %all-gather.2.cloned.1.call-done.owned_ref, bf16[4096,172]{0,1:T(8,128)(2,1)S(1)} %bitcast.31), kind=kOutput, calls=%fused_computation.1 | convolution fusion | flops 845414400 | bytes 6737024 | tf_op jit(solution)/shard_map/dot_general | solution.py:44
  104.6 3.6 %all-to-all-start.1 = ((bf16[8,512,128]{1,2,0:T(8,128)(2,1)}), bf16[8,512,128]{1,2,0:T(8,128)(2,1)S(1)}, u32[]{:S(2)}, u32[]{:S(2)}) async-start(bf16[8,512,128]{1,2,0:T(8,128)(2,1)} %slice.16), calls=%async_computation.1 | async-start | bytes 2097152 | tf_op jit(solution)/shard_map/all_to_all | solution.py:43
  108.8 1.6 collective-permute-start.1
  110.4 24.3 %all-to-all-done.1 = bf16[8,512,128]{1,2,0:T(8,128)(2,1)S(1)} async-done(((bf16[8,512,128]{1,2,0:T(8,128)(2,1)}), bf16[8,512,128]{1,2,0:T(8,128)(2,1)S(1)}, u32[]{:S(2)}, u32[]{:S(2)}) %all-to-all-start.1) | async-done | bytes 1048608 | tf_op jit(solution)/shard_map/all_to_all | solution.py:43
  134.7 0.7 copy.12
  135.4 0.0 copy-start.1
  135.4 3.5 %fusion.4 = f32[128,600]{1,0:T(8,128)S(1)} fusion(bf16[4096,128]{1,0:T(8,128)(2,1)S(1)} %bitcast.28, bf16[4096,600]{1,0:T(8,128)(2,1)} %all-gather.2.cloned.1.call-done.owned_ref), kind=kOutput, calls=%fused_computation.12 | convolution fusion | flops 629145600 | bytes 6270976 | tf_op jit(solution)/shard_map/dot_general | solution.py:44
  138.9 1.6 collective-permute-start
  140.4 0.1 fusion.2
  140.5 0.1 pad_maximum_fusion.1
  140.6 0.0 collective-permute-done.1
  140.6 0.1 add.36
  140.7 7.5 %collective-permute-done = f32[128,600]{1,0:T(8,128)S(1)} collective-permute-done((f32[128,600]{1,0:T(8,128)S(1)}, f32[128,600]{1,0:T(8,128)S(1)}, u32[]{:S(2)}, u32[]{:S(2)}) %collective-permute-start) | collective-permute-done | bytes 307232 | tf_op jit(solution)/shard_map/ppermute | solution.py:56
  148.2 0.2 fusion.1.amp_ref
  148.5 2.5 %copy-done = bf16[4096,600]{1,0:T(8,128)(2,1)S(1)} copy-done((bf16[4096,600]{1,0:T(8,128)(2,1)S(1)}, bf16[4096,600]{1,0:T(8,128)(2,1)}, u32[]{:S(2)}) %copy-start) | copy-done | bytes 4915224
  151.0 5.0 %shard_map.46 = f32[300,1,4096]{2,1,0:T(1,128)} custom-call(bf16[300,600]{1,0:T(8,128)(2,1)S(1)} %fusion.1.amp_ref, bf16[4096,600]{1,0:T(8,128)(2,1)S(1)} %copy-done), custom_call_target="tpu_custom_call" | custom-call | tf_op jit(solution)/shard_map/pallas_call | solution.py:69
  (4 shorter events, 0.0 us)
Async XLA Ops:
  6.5 94.3 %all-gather.2.cloned.1.call-start = ((), (), s32[]{:S(2)}) async-start(), calls=%async_computation.2 | async-start | bytes 5898240 | tf_op jit(solution)/shard_map/all_gather | solution.py:86
  15.7 78.0 %all-to-all-start = ((bf16[8,512,172]{1,2,0:T(8,128)(2,1)}), bf16[8,512,172]{1,2,0:T(8,128)(2,1)}, u32[]{:S(2)}, u32[]{:S(2)}) async-start(bf16[8,512,172]{1,2,0:T(8,128)(2,1)} %slice.17), calls=%async_computation | async-start | bytes 2883584 | tf_op jit(solution)/shard_map/all_to_all | solution.py:43
  104.6 30.1 %all-to-all-start.1 = ((bf16[8,512,128]{1,2,0:T(8,128)(2,1)}), bf16[8,512,128]{1,2,0:T(8,128)(2,1)S(1)}, u32[]{:S(2)}, u32[]{:S(2)}) async-start(bf16[8,512,128]{1,2,0:T(8,128)(2,1)} %slice.16), calls=%async_computation.1 | async-start | bytes 2097152 | tf_op jit(solution)/shard_map/all_to_all | solution.py:43
  108.8 31.8 %collective-permute-start.1 = (f32[172,600]{1,0:T(8,128)S(1)}, f32[172,600]{1,0:T(8,128)S(1)}, u32[]{:S(2)}, u32[]{:S(2)}) collective-permute-start(f32[172,600]{1,0:T(8,128)S(1)} %convolution_bitcast_fusion), channel_id=1, source_target_pairs={{0,2},{2,0},{1,3},{3,1},{4,6},{6,4},{5,7},{7,5},{8,10},{10,8},{9,1... | collective-permute-start | bytes 1238408 | tf_op jit(solution)/shard_map/ppermute | solution.py:56
  135.4 5.1 %copy-start.1 = (f32[2400]{0:T(1024)S(1)}, f32[2400]{0:T(1024)}, u32[]{:S(2)}) copy-start(f32[2400]{0:T(1024)} %param.6) | copy-start | bytes 28804
  138.9 9.3 %collective-permute-start = (f32[128,600]{1,0:T(8,128)S(1)}, f32[128,600]{1,0:T(8,128)S(1)}, u32[]{:S(2)}, u32[]{:S(2)}) collective-permute-start(f32[128,600]{1,0:T(8,128)S(1)} %fusion.4), channel_id=1, source_target_pairs={{0,2},{2,0},{1,3},{3,1},{4,6},{6,4},{5,7},{7,5},{8,10},{10,8},{9,1... | collective-permute-start | bytes 921608 | tf_op jit(solution)/shard_map/ppermute | solution.py:56
  148.5 2.5 %copy-start = (bf16[4096,600]{1,0:T(8,128)(2,1)S(1)}, bf16[4096,600]{1,0:T(8,128)(2,1)}, u32[]{:S(2)}) copy-start(bf16[4096,600]{1,0:T(8,128)(2,1)} %all-gather.2.cloned.1.call-done.owned_ref) | copy-start | bytes 14745604
Sparse Core Ops, SparseCore 0:
  12.0 88.7 all-gather.1

commit v10 on v8

v10 whole, which is shorter than its diff:
```python
import functools

import jax
import jax.numpy as jnp
from jax import lax
from jax.experimental import pallas as pl
from jax.experimental.pallas import tpu as pltpu
from jax.experimental.layout import Layout, with_layout_constraint
from jax.sharding import PartitionSpec as P

os_scale = 1.3
COLS = ("col", "rep")
PARTIAL_BYTES_MAX = 0
LINE_MAX = 8


def owner_columns(local, col_energy, owners, width):
    owned = []
    owner_energy = []
    for step_index in range(owners.shape[0]):
        first = owners[step_index] * width
        owned.append(lax.dynamic_slice_in_dim(local, first, width, 1))
        owner_energy.append(lax.dynamic_slice_in_dim(col_energy, first, width, 0))
    return jnp.concatenate(owned, axis=1), jnp.concatenate(owner_energy, axis=0)


def coupling_by_partials(local, owned, shards, width):
    rows = local.shape[0]
    blocked = local.reshape(rows, shards, width)
    partial_value = lax.dot_general(
        blocked, owned, (((0,), (0,)), ((), ())), preferred_element_type=jnp.float32
    )
    return lax.psum_scatter(partial_value, COLS, scatter_dimension=0, tiled=False)


def move_columns(local, shards, width):
    rows = local.shape[0]
    blocked = local.reshape(rows, shards, width).transpose(1, 0, 2)
    return lax.all_to_all(blocked, COLS, split_axis=0, concat_axis=0, tiled=True)


def coupling_by_columns(moved, owned_blocks, n_col, n_rep, width, by_chip):
    rows = moved.shape[1]
    shards = n_col * n_rep
    if by_chip:
        moved = moved.reshape(n_col, n_rep, rows, width).transpose(1, 0, 2, 3)
    return lax.dot_general(
        moved.reshape(shards * rows, width),
        owned_blocks.reshape(shards * rows, owned_blocks.shape[-1]),
        (((0,), (0,)), ((), ())),
        preferred_element_type=jnp.float32,
    )


def exchange_sum(value, axis, size):
    total = value
    for step in range(1, size):
        total = total + lax.ppermute(value, axis, [(i, (i + step) % size) for i in range(size)])
    return total


def gamma_kernel(amp_ref, owned_ref, out_ref, *, order):
    outer, inner, rows = owned_ref.shape[:3]
    for a in range(outer):
        for b in range(inner):
            start = order(a, b) * rows
            out_ref[:, 0, start : start + rows] = lax.dot_general(
                amp_ref[...], owned_ref[a, b], (((1,), (1,)), ((), ())),
                preferred_element_type=jnp.float32,
            )


def gamma_rows_last(amplitude, owned_blocks, order):
    width = amplitude.shape[0]
    rows = owned_blocks.shape[0] * owned_blocks.shape[1] * owned_blocks.shape[2]
    out = pl.pallas_call(
        functools.partial(gamma_kernel, order=order),
        out_shape=jax.ShapeDtypeStruct((width, 1, rows), jnp.float32),
        in_specs=[pl.BlockSpec(memory_space=pltpu.VMEM)] * 2,
        out_specs=pl.BlockSpec(memory_space=pltpu.VMEM),
        compiler_params=pltpu.CompilerParams(vmem_limit_bytes=48 * 2**20),
    )(amplitude, owned_blocks)
    return out.transpose(1, 2, 0)


def gather_by_chip(owned, after):
    owned = with_layout_constraint(owned, Layout((0, 1)))
    gathered = lax.all_gather(owned, "col", axis=0, tiled=False)
    gathered, _ = lax.optimization_barrier((gathered, after))
    return lax.all_gather(gathered, "rep", axis=0, tiled=False)


def body(b_aux, occ_energies, vir_energies, owners, *, n_col, n_rep, n_aux, by_partials):
    shards = n_col * n_rep
    local = b_aux[0]
    width = local.shape[1] // shards
    col_energy = (vir_energies[None, :] - occ_energies[:, None]).reshape(-1)
    shard_index = lax.axis_index(COLS)
    energy_mine = lax.dynamic_slice_in_dim(col_energy, shard_index * width, width, 0)
    owned, owner_energy = owner_columns(local, col_energy, owners, width)
    by_chip = n_col <= LINE_MAX and not by_partials
    moved = None if by_partials else move_columns(local, shards, width)
    if by_chip:
        owned_blocks = gather_by_chip(owned, moved)
        order = lambda a, b: b * n_rep + a
    else:
        owned_blocks = lax.all_gather(owned, COLS, axis=0, tiled=True)[None, None]
        order = lambda a, b: 0
    if by_partials:
        coupling = coupling_by_partials(local, owned, shards, width)
    else:
        coupling = coupling_by_columns(moved, owned_blocks, n_col, n_rep, width, by_chip)
    coupling = exchange_sum(coupling, "aux", n_aux)
    denominator = energy_mine[:, None] + owner_energy[None, :]
    amplitude = (os_scale * coupling / denominator).astype(jnp.bfloat16)
    return gamma_rows_last(amplitude, owned_blocks, order)


def solution(mesh):
    n_col, n_rep = mesh.shape["col"], mesh.shape["rep"]
    shards = n_col * n_rep

    def run(b_aux, occ_energies, vir_energies, owners):
        ncol = b_aux.shape[2]
        partial_bytes = ncol * owners.shape[0] * (ncol // shards) * 4
        by_partials = partial_bytes <= PARTIAL_BYTES_MAX
        placed = (P(("groups", "aux"), COLS, None), P("groups"), P("groups"), P())
        return jax.shard_map(
            lambda *a: body(*a, n_col=n_col, n_rep=n_rep, n_aux=mesh.shape["aux"], by_partials=by_partials),
            mesh=mesh,
            in_specs=placed,
            out_specs=P(("groups", "aux"), None, COLS),
            check_vma=False,
        )(b_aux, occ_energies, vir_energies, owners)

    return run
```

time: 162 us -> 174 us (1.074)
  blocking collectives: 106 us -> 0 us
  waiting for transfers between devices: 16.6 us -> 116 us
  local copies, waits for them, and re-layouts: 10.9 us -> 22.6 us
  starting transfers between devices: 1.56 us -> 8.33 us
    all_gather x1 -> x2, waiting for transfers between devices: 0.02 us -> 107 us  [the longest x1 93.6 us: gather_by_chip(): gathered = lax.all_gather(owned, 'col', axis=0, tiled=False)]
    all_to_all x1 -> x0, blocking collectives: 106 us -> none  [coupling_by_columns(): lax.all_to_all(blocked, COLS, split_axis=0, concat_axis=0, tiled=True)]
    all_gather x0 -> x1, local copies, waits for them, and re-layouts: none -> 7.72 us  [gather_by_chip(): return lax.all_gather(gathered, 'rep', axis=0, tiled=False)]
    ppermute x1, waiting for transfers between devices: 16.6 us -> 9.26 us  [exchange_sum(): lax.ppermute(value, axis, [(i, (i + step) % size) for i in range(size)])]
    all_to_all x0 -> x1, starting transfers between devices: none -> 6.46 us  [move_columns(): lax.all_to_all(blocked, COLS, split_axis=0, concat_axis=0, tiled=True)]
    optimization_barrier x0 -> x1, local copies, waits for them, and re-layouts: none -> 4.33 us  [gather_by_chip(): gathered, _ = lax.optimization_barrier((gathered, after))]
  transfers between devices with their start and end apart: 2 -> 4, of which waited for: 1 -> 3; matrix products, arithmetic and copies ran while one was open for 3% -> 7% of each run, Pallas kernels for 0% -> 0%
where the time goes in v10:
time: 174 us
  waiting for transfers between devices  116 us (67%)
  local copies, waits for them, and re-layouts  22.6 us (13%)
  between operations  15.4 us (9%)
  starting transfers between devices  8.33 us (5%)
  Pallas kernels  5.04 us (3%)
  matrix products  4.52 us (3%)
    all_gather x1, waiting for transfers between devices, gather_by_chip(): gathered = lax.all_gather(owned, 'col', axis=0, tiled=False)  93.6 us
    all_gather x1, waiting for transfers between devices, gather_by_chip(): return lax.all_gather(gathered, 'rep', axis=0, tiled=False)  13.4 us
    ppermute x1, waiting for transfers between devices, exchange_sum(): lax.ppermute(value, axis, [(i, (i + step) % size) for i in range(size)])  9.26 us
    all_gather x1, local copies, waits for them, and re-layouts, gather_by_chip(): return lax.all_gather(gathered, 'rep', axis=0, tiled=False)  7.72 us
    all_to_all x1, starting transfers between devices, move_columns(): lax.all_to_all(blocked, COLS, split_axis=0, concat_axis=0, tiled=True)  6.46 us
    pallas_call x1, Pallas kernels, gamma_rows_last(): pl.pallas_call(functools.partial(gamma_kernel, order=order), out_shape=ja...  5.04 us
    dot_general x1, matrix products, coupling_by_columns(): lax.dot_general(moved.reshape(shards * rows, width), owned_blocks.reshape...  4.52 us
    optimization_barrier x1, local copies, waits for them, and re-layouts, gather_by_chip(): gathered, _ = lax.optimization_barrier((gathered, after))  4.33 us
  transfers between devices with their start and end apart: 4, of which 3 were waited for; matrix products, arithmetic and copies ran while one was open for 7% of the time, Pallas kernels for 0%

profile of v10, /device:TPU:0, one launch (start us, length us, event | category | flops | bytes accessed | tf_op | source)
XLA Modules:
  0.0 173.6 jit_solution(12478842687197524910)
XLA Ops:
  6.5 4.1 %reshape_squeeze.3 = bf16[512,8,300]{0,2,1:T(8,128)(2,1)} reshape(bf16[1,512,2400]{1,2,0:T(8,128)(2,1)} %param.4) | data formatting | bytes 4915200 | tf_op jit(solution)/shard_map/reshape;squeeze | solution.py:38
  10.6 0.0 copy-start.2
  10.6 6.5 %all-to-all-start = ((bf16[8,512,300]{1,2,0:T(8,128)(2,1)}), bf16[8,512,300]{1,2,0:T(8,128)(2,1)S(1)}, u32[]{:S(2)}, u32[]{:S(2)}) async-start(bf16[8,512,300]{1,2,0:T(8,128)(2,1)} %bitcast.5), calls=%async_computation | async-start | bytes 4980736 | tf_op jit(solution)/shard_map/all_to_all | solution.py:39
  17.1 0.0 all-gather.5.cloned.1.call-start
  17.1 0.0 copy-done.2
  17.1 0.6 fusion.7
  19.0 1.9 %constant_dynamic-slice_fusion.1 = (bf16[1,512,300]{1,2,0:T(8,128)(2,1)S(1)}, bf16[1,512,300]{1,2,0:T(8,128)(2,1)}) fusion(bf16[1,512,2400]{1,2,0:T(8,128)(2,1)} %param.4, s32[]{:T(128)S(6)} %select_n.11, s32[]{:T(128)S(6)} %select_n.12), kind=kLoop, calls=%fused_computation.9 | loop fusion | bytes 1228808 | tf_op jit(solution)/shard_map/dynamic_slice | solution.py:22
  20.9 0.2 copy.12
  21.2 1.2 copy.13
  22.3 1.1 pad_maximum_fusion
  23.4 0.0 all-gather.5.cloned.1.call-update
  23.4 0.0 all-gather.7.cloned.1.call-start
  23.5 93.6 %all-gather.5.cloned.1.call-done = bf16[2048,600]{1,0:T(8,128)(2,1)} async-done(((bf16[512,600]{1,0:T(8,128)(2,1)}), bf16[2048,600]{1,0:T(8,128)(2,1)}) %all-gather.5.cloned.1.call-update) | async-done | bytes 2457616 | tf_op jit(solution)/shard_map/all_gather | solution.py:88
  117.1 0.0 all-to-all-done
  117.1 4.3 %copy.14 = bf16[4,512,600]{1,2,0:T(8,128)(2,1)} copy(bf16[4,512,600]{2,1,0:T(8,128)(2,1)} %bitcast.28) | data formatting | bytes 4915200 | tf_op jit(solution)/shard_map/optimization_barrier | solution.py:89
  121.4 0.0 all-gather.7.cloned.1.call-update
  121.4 13.4 %all-gather.7.cloned.1.call-done = bf16[8,512,600]{1,2,0:T(8,128)(2,1)} async-done(((bf16[4,512,600]{1,2,0:T(8,128)(2,1)}), bf16[8,512,600]{1,2,0:T(8,128)(2,1)}) %all-gather.7.cloned.1.call-update) | async-done | bytes 4915216 | tf_op jit(solution)/shard_map/all_gather | solution.py:90
  134.9 0.0 copy-start.1
  134.9 4.5 %fusion.3 = f32[300,600]{1,0:T(8,128)S(1)} fusion(bf16[2,4,512,600]{2,3,1,0:T(8,128)(2,1)} %bitcast.27, bf16[4,2,512,300]{2,3,1,0:T(8,128)(2,1)S(1)} %bitcast.29), kind=kOutput, calls=%fused_computation.3 | convolution fusion | flops 1474560000 | bytes 8092800 | tf_op jit(solution)/shard_map/dot_general | solution.py:47
  139.4 1.8 %collective-permute-start = (f32[300,600]{1,0:T(8,128)S(1)}, f32[300,600]{1,0:T(8,128)S(1)}, u32[]{:S(2)}, u32[]{:S(2)}) collective-permute-start(f32[300,600]{1,0:T(8,128)S(1)} %fusion.3), channel_id=1, source_target_pairs={{0,2},{2,0},{1,3},{3,1},{4,6},{6,4},{5,7},{7,5},{8,10},{10,8},{9,1... | collective-permute-start | bytes 2160008 | tf_op jit(solution)/shard_map/ppermute | solution.py:58
  141.8 0.0 copy-done.1
  141.9 0.1 fusion.6
  141.9 0.1 pad_maximum_fusion.1
  142.0 7.7 %copy.15 = bf16[8,512,600]{2,1,0:T(8,128)(2,1)} copy(bf16[8,512,600]{1,2,0:T(8,128)(2,1)} %all-gather.7.cloned.1.call-done) | data formatting | bytes 9830400 | tf_op jit(solution)/shard_map/all_gather | solution.py:90
  149.7 9.3 %collective-permute-done = f32[300,600]{1,0:T(8,128)S(1)} collective-permute-done((f32[300,600]{1,0:T(8,128)S(1)}, f32[300,600]{1,0:T(8,128)S(1)}, u32[]{:S(2)}, u32[]{:S(2)}) %collective-permute-start) | collective-permute-done | bytes 720032 | tf_op jit(solution)/shard_map/ppermute | solution.py:58
  159.0 0.3 divide_convert_fusion.amp_ref
  159.3 0.0 copy-start
  159.3 2.5 %copy-done = bf16[8,512,600]{2,1,0:T(8,128)(2,1)S(1)} copy-done((bf16[8,512,600]{2,1,0:T(8,128)(2,1)S(1)}, bf16[8,512,600]{2,1,0:T(8,128)(2,1)}, u32[]{:S(2)}) %copy-start) | copy-done | bytes 4915224
  161.8 5.0 %shard_map.46 = f32[300,1,4096]{2,1,0:T(1,128)} custom-call(bf16[300,600]{1,0:T(8,128)(2,1)S(1)} %divide_convert_fusion.amp_ref, bf16[2,4,512,600]{3,2,1,0:T(8,128)(2,1)S(1)} %bitcast.26), custom_call_target="tpu_custom_call" | custom-call | tf_op jit(solution)/shard_map/pallas_call | solution.py:76
  (1 shorter events, 0.0 us)
Async XLA Ops:
  10.6 6.5 %copy-start.2 = (s32[2]{0:T(128)S(1)}, s32[2]{0:T(128)}, u32[]{:S(2)}) copy-start(s32[2]{0:T(128)} %param.7) | copy-start | bytes 28
  10.6 106.5 %all-to-all-start = ((bf16[8,512,300]{1,2,0:T(8,128)(2,1)}), bf16[8,512,300]{1,2,0:T(8,128)(2,1)S(1)}, u32[]{:S(2)}, u32[]{:S(2)}) async-start(bf16[8,512,300]{1,2,0:T(8,128)(2,1)} %bitcast.5), calls=%async_computation | async-start | bytes 4980736 | tf_op jit(solution)/shard_map/all_to_all | solution.py:39
  17.1 100.0 %all-gather.5.cloned.1.call-start = ((), (), s32[]{:S(2)}) async-start(), calls=%async_computation.1 | async-start | bytes 3276800 | tf_op jit(solution)/shard_map/all_gather | solution.py:88
  23.4 111.4 %all-gather.7.cloned.1.call-start = ((), (), s32[]{:S(2)}) async-start(), calls=%async_computation.2 | async-start | bytes 7372800 | tf_op jit(solution)/shard_map/all_gather | solution.py:90
  134.9 7.0 %copy-start.1 = (f32[2400]{0:T(1024)S(1)}, f32[2400]{0:T(1024)}, u32[]{:S(2)}) copy-start(f32[2400]{0:T(1024)} %param.6) | copy-start | bytes 28804
  139.4 19.6 %collective-permute-start = (f32[300,600]{1,0:T(8,128)S(1)}, f32[300,600]{1,0:T(8,128)S(1)}, u32[]{:S(2)}, u32[]{:S(2)}) collective-permute-start(f32[300,600]{1,0:T(8,128)S(1)} %fusion.3), channel_id=1, source_target_pairs={{0,2},{2,0},{1,3},{3,1},{4,6},{6,4},{5,7},{7,5},{8,10},{10,8},{9,1... | collective-permute-start | bytes 2160008 | tf_op jit(solution)/shard_map/ppermute | solution.py:58
  159.3 2.5 %copy-start = (bf16[8,512,600]{2,1,0:T(8,128)(2,1)S(1)}, bf16[8,512,600]{2,1,0:T(8,128)(2,1)}, u32[]{:S(2)}) copy-start(bf16[8,512,600]{2,1,0:T(8,128)(2,1)} %copy.15) | copy-start | bytes 14745604
Sparse Core Ops, SparseCore 0:
  23.6 93.4 all-gather.4
  121.6 13.2 all-gather.6

commit v11 on v9

--- a/solution.py
+++ b/solution.py
@@ -33,21 +33,21 @@
 def coupling_by_columns(local, owned_all, shards, width, n_aux):
     rows = local.shape[0]
     blocked = local.reshape(rows, shards, width).transpose(1, 0, 2)
-    edges = sorted(set([0, min(LANES, width), width]))
-    pieces = {}
+    split = (width // LANES) * LANES
+    edges = [0, split, width] if 0 < split < width else [0, width]
+    pieces = []
     previous = None
-    for first, last in list(zip(edges[:-1], edges[1:]))[::-1]:
+    for first, last in zip(edges[:-1], edges[1:]):
         chunk = blocked[:, :, first:last]
         if previous is not None:
             chunk, _ = lax.optimization_barrier((chunk, previous))
         moved = lax.all_to_all(chunk, COLS, split_axis=0, concat_axis=0, tiled=True)
-        piece = lax.dot_general(
+        previous = lax.dot_general(
             moved.reshape(shards * rows, last - first), owned_all, (((0,), (0,)), ((), ())),
             preferred_element_type=jnp.float32,
         )
-        previous = piece
-        pieces[first] = exchange_sum(piece, "aux", n_aux)
-    return jnp.concatenate([pieces[first] for first in sorted(pieces)], axis=0)
+        pieces.append(exchange_sum(previous, "aux", n_aux))
+    return jnp.concatenate(pieces, axis=0)
 
 
 def exchange_sum(value, axis, size):

time: 163 us -> 161 us (0.988)
  waiting for transfers between devices: 107 us -> 103 us
    all_to_all x2, waiting for transfers between devices: 94.9 us -> 100 us  [coupling_by_columns(): moved = lax.all_to_all(chunk, COLS, split_axis=0, concat_axis=0, tiled=True)]
    ppermute x2, waiting for transfers between devices: 7.53 us -> 3 us  [exchange_sum(): lax.ppermute(value, axis, [(i, (i + step) % size) for i in range(size)])]
    all_gather x1, waiting for transfers between devices: 4.29 us -> 0.02 us  [body(): owned_all = lax.all_gather(owned, COLS, axis=0, tiled=True)]
  transfers between devices with their start and end apart: 5 -> 5, of which waited for: 4 -> 3; matrix products, arithmetic and copies ran while one was open for 7% -> 8% of each run, Pallas kernels for 0% -> 0%
where the time goes in v11:
time: 161 us; the launch traced here: 160 us
  waiting for transfers between devices  103 us (64%)
  between operations  15.4 us (10%)
  local copies, waits for them, and re-layouts  14.1 us (9%)
  starting transfers between devices  12.9 us (8%)
  matrix products  7.73 us (5%)
  Pallas kernels  4.98 us (3%)
    all_to_all x2, waiting for transfers between devices, coupling_by_columns(): moved = lax.all_to_all(chunk, COLS, split_axis=0, concat_axis=0, tiled=True)  100 us
    all_to_all x2, starting transfers between devices, coupling_by_columns(): moved = lax.all_to_all(chunk, COLS, split_axis=0, concat_axis=0, tiled=True)  9.79 us
    dot_general x2, matrix products, coupling_by_columns(): lax.dot_general(moved.reshape(shards * rows, last - first), owned_all, ((...  7.73 us
    pallas_call x1, Pallas kernels, gamma_rows_last(): pl.pallas_call(gamma_kernel, out_shape=jax.ShapeDtypeStruct((width, 1, ro...  4.98 us
  transfers between devices with their start and end apart: 5, of which 3 were waited for; matrix products, arithmetic and copies ran while one was open for 8% of the time, Pallas kernels for 0%

profile of v11, /device:TPU:0, one launch (start us, length us, event | category | flops | bytes accessed | tf_op | source)
XLA Modules:
  0.0 160.1 jit_solution(11220557501945859637)
XLA Ops:
  6.5 1.3 fusion.3
  9.1 1.2 constant_dynamic-slice_fusion.1
  10.3 0.2 copy.13
  10.5 0.2 copy.14
  10.7 1.1 pad_maximum_fusion
  11.8 0.0 all-gather.2.cloned.1.call-update
  11.8 2.6 %reshape_squeeze.3 = bf16[512,8,300]{0,2,1:T(8,128)(2,1)S(1)} reshape(bf16[1,512,2400]{1,2,0:T(8,128)(2,1)} %param.4) | data formatting | bytes 4915200 | tf_op jit(solution)/shard_map/reshape;squeeze | solution.py:35
  14.5 1.5 slice.16
  16.0 6.3 %all-to-all-start = ((bf16[8,512,256]{1,2,0:T(8,128)(2,1)}), bf16[8,512,256]{1,2,0:T(8,128)(2,1)}, u32[]{:S(2)}, u32[]{:S(2)}) async-start(bf16[8,512,256]{1,2,0:T(8,128)(2,1)} %slice.16), calls=%async_computation | async-start | bytes 4194304 | tf_op jit(solution)/shard_map/all_to_all | solution.py:44
  22.3 0.8 slice.17
  23.1 90.5 %all-to-all-done = bf16[8,512,256]{1,2,0:T(8,128)(2,1)} async-done(((bf16[8,512,256]{1,2,0:T(8,128)(2,1)}), bf16[8,512,256]{1,2,0:T(8,128)(2,1)}, u32[]{:S(2)}, u32[]{:S(2)}) %all-to-all-start) | async-done | bytes 2097184 | tf_op jit(solution)/shard_map/all_to_all | solution.py:44
  113.6 2.8 %copy.15 = bf16[8,512,256]{2,1,0:T(8,128)(2,1)S(1)} copy(bf16[8,512,256]{1,2,0:T(8,128)(2,1)} %all-to-all-done) | data formatting | bytes 4194304 | tf_op jit(solution)/shard_map/all_to_all | solution.py:44
  116.5 0.0 all-gather.2.cloned.1.call-done.owned_ref
  116.5 0.0 copy-start.1
  116.5 4.3 %convolution_bitcast_fusion = f32[256,600]{1,0:T(8,128)S(1)} fusion(bf16[4096,600]{1,0:T(8,128)(2,1)} %all-gather.2.cloned.1.call-done.owned_ref, bf16[4096,256]{1,0:T(8,128)(2,1)S(1)} %bitcast.26), kind=kOutput, calls=%fused_computation | convolution fusion | flops 1258291200 | bytes 7626752 | tf_op jit(solution)/shard_map/dot_general | solution.py:45
  120.8 3.5 %all-to-all-start.1 = ((bf16[8,512,44]{1,2,0:T(8,128)(2,1)}), bf16[8,512,44]{1,2,0:T(8,128)(2,1)S(1)}, u32[]{:S(2)}, u32[]{:S(2)}) async-start(bf16[8,512,44]{1,2,0:T(8,128)(2,1)} %slice.17), calls=%async_computation.1 | async-start | bytes 786432 | tf_op jit(solution)/shard_map/all_to_all | solution.py:44
  125.0 0.2 copy.17
  125.2 1.6 collective-permute-start
  126.8 0.1 fusion.2
  126.9 9.9 %all-to-all-done.1 = bf16[8,512,44]{1,2,0:T(8,128)(2,1)S(1)} async-done(((bf16[8,512,44]{1,2,0:T(8,128)(2,1)}), bf16[8,512,44]{1,2,0:T(8,128)(2,1)S(1)}, u32[]{:S(2)}, u32[]{:S(2)}) %all-to-all-start.1) | async-done | bytes 360480 | tf_op jit(solution)/shard_map/all_to_all | solution.py:44
  136.8 0.2 copy.23
  137.0 0.1 copy.21
  137.2 3.4 %fusion.4 = f32[44,600]{1,0:T(8,128)S(1)} fusion(bf16[4096,44]{0,1:T(8,128)(2,1)S(1)} %bitcast.28, bf16[4096,600]{1,0:T(8,128)(2,1)} %all-gather.2.cloned.1.call-done.owned_ref), kind=kOutput, calls=%fused_computation.12 | convolution fusion | flops 216268800 | bytes 5381248 | tf_op jit(solution)/shard_map/dot_general | solution.py:45
  140.6 1.6 collective-permute-start.1
  142.1 0.1 pad_maximum_fusion.1
  142.2 0.0 collective-permute-done
  142.2 0.2 copy.18
  142.4 0.1 add.35
  142.5 3.0 %collective-permute-done.1 = f32[44,600]{1,0:T(8,128)S(1)} collective-permute-done((f32[44,600]{1,0:T(8,128)S(1)}, f32[44,600]{1,0:T(8,128)S(1)}, u32[]{:S(2)}, u32[]{:S(2)}) %collective-permute-start.1) | collective-permute-done | bytes 105632 | tf_op jit(solution)/shard_map/ppermute | solution.py:56
  145.5 0.2 fusion.1.amp_ref
  145.8 2.5 %copy-done = bf16[4096,600]{1,0:T(8,128)(2,1)S(1)} copy-done((bf16[4096,600]{1,0:T(8,128)(2,1)S(1)}, bf16[4096,600]{1,0:T(8,128)(2,1)}, u32[]{:S(2)}) %copy-start) | copy-done | bytes 4915224
  148.3 5.0 %shard_map.46 = f32[300,1,4096]{2,1,0:T(1,128)} custom-call(bf16[300,600]{1,0:T(8,128)(2,1)S(1)} %fusion.1.amp_ref, bf16[4096,600]{1,0:T(8,128)(2,1)S(1)} %copy-done), custom_call_target="tpu_custom_call" | custom-call | tf_op jit(solution)/shard_map/pallas_call | solution.py:69
  (6 shorter events, 0.1 us)
Async XLA Ops:
  6.5 110.0 %all-gather.2.cloned.1.call-start = ((), (), s32[]{:S(2)}) async-start(), calls=%async_computation.2 | async-start | bytes 5898240 | tf_op jit(solution)/shard_map/all_gather | solution.py:86
  16.0 97.6 %all-to-all-start = ((bf16[8,512,256]{1,2,0:T(8,128)(2,1)}), bf16[8,512,256]{1,2,0:T(8,128)(2,1)}, u32[]{:S(2)}, u32[]{:S(2)}) async-start(bf16[8,512,256]{1,2,0:T(8,128)(2,1)} %slice.16), calls=%async_computation | async-start | bytes 4194304 | tf_op jit(solution)/shard_map/all_to_all | solution.py:44
  116.5 8.5 %copy-start.1 = (f32[2400]{0:T(1024)S(1)}, f32[2400]{0:T(1024)}, u32[]{:S(2)}) copy-start(f32[2400]{0:T(1024)} %param.6) | copy-start | bytes 28804
  120.8 15.9 %all-to-all-start.1 = ((bf16[8,512,44]{1,2,0:T(8,128)(2,1)}), bf16[8,512,44]{1,2,0:T(8,128)(2,1)S(1)}, u32[]{:S(2)}, u32[]{:S(2)}) async-start(bf16[8,512,44]{1,2,0:T(8,128)(2,1)} %slice.17), calls=%async_computation.1 | async-start | bytes 786432 | tf_op jit(solution)/shard_map/all_to_all | solution.py:44
  125.2 17.0 %collective-permute-start = (f32[256,600]{0,1:T(8,128)S(1)}, f32[256,600]{0,1:T(8,128)S(1)}, u32[]{:S(2)}, u32[]{:S(2)}) collective-permute-start(f32[256,600]{0,1:T(8,128)S(1)} %copy.17), channel_id=1, source_target_pairs={{0,2},{2,0},{1,3},{3,1},{4,6},{6,4},{5,7},{7,5},{8,10},{10,8},{9,1... | collective-permute-start | bytes 1843208 | tf_op jit(solution)/shard_map/ppermute | solution.py:56
  140.6 4.9 %collective-permute-start.1 = (f32[44,600]{1,0:T(8,128)S(1)}, f32[44,600]{1,0:T(8,128)S(1)}, u32[]{:S(2)}, u32[]{:S(2)}) collective-permute-start(f32[44,600]{1,0:T(8,128)S(1)} %fusion.4), channel_id=1, source_target_pairs={{0,2},{2,0},{1,3},{3,1},{4,6},{6,4},{5,7},{7,5},{8,10},{10,8},{9,1... | collective-permute-start | bytes 316808 | tf_op jit(solution)/shard_map/ppermute | solution.py:56
  145.8 2.5 %copy-start = (bf16[4096,600]{1,0:T(8,128)(2,1)S(1)}, bf16[4096,600]{1,0:T(8,128)(2,1)}, u32[]{:S(2)}) copy-start(bf16[4096,600]{1,0:T(8,128)(2,1)} %all-gather.2.cloned.1.call-done.owned_ref) | copy-start | bytes 14745604
Sparse Core Ops, SparseCore 0:
  12.0 101.8 all-gather.1

commit v12 on v11

--- a/solution.py
+++ b/solution.py
@@ -9,6 +9,7 @@
 COLS = ("col", "rep")
 PARTIAL_BYTES_MAX = 0
 LANES = 128
+ROW_BLOCK = 1024
 
 
 def owner_columns(local, col_energy, owners, width):
@@ -64,14 +65,18 @@
 
 
 def gamma_rows_last(amplitude, owned_all):
-    width = amplitude.shape[0]
+    width, depth = amplitude.shape
     rows = owned_all.shape[0]
+    block = ROW_BLOCK if rows % ROW_BLOCK == 0 else rows
     out = pl.pallas_call(
         gamma_kernel,
         out_shape=jax.ShapeDtypeStruct((width, 1, rows), jnp.float32),
-        in_specs=[pl.BlockSpec(memory_space=pltpu.VMEM)] * 2,
-        out_specs=pl.BlockSpec(memory_space=pltpu.VMEM),
-        compiler_params=pltpu.CompilerParams(vmem_limit_bytes=48 * 2**20),
+        grid=(rows // block,),
+        in_specs=[
+            pl.BlockSpec((width, depth), lambda i: (0, 0)),
+            pl.BlockSpec((block, depth), lambda i: (i, 0)),
+        ],
+        out_specs=pl.BlockSpec((width, 1, block), lambda i: (0, 0, i)),
     )(amplitude, owned_all)
     return out.transpose(1, 2, 0)
 

time: 161 us -> 161 us (level)
  local copies, waits for them, and re-layouts: 14.1 us -> 11.7 us
  Pallas kernels: 4.98 us -> 6.68 us
    unnamed x6 -> x4, local copies, waits for them, and re-layouts: 2.64 us -> 0.16 us
    pallas_call x1, Pallas kernels: 4.98 us -> 6.68 us  [gamma_rows_last(): pl.pallas_call(gamma_kernel, out_shape=jax.ShapeDtypeStruct((width, 1, ro...]
where the time goes in v12:
time: 161 us; the launch traced here: 160 us
  waiting for transfers between devices  103 us (64%)
  between operations  15.5 us (10%)
  starting transfers between devices  12.9 us (8%)
  local copies, waits for them, and re-layouts  11.7 us (7%)
  matrix products  7.73 us (5%)
  Pallas kernels  6.68 us (4%)
  other arithmetic  2.23 us (1%)
    all_to_all x2, waiting for transfers between devices, coupling_by_columns(): moved = lax.all_to_all(chunk, COLS, split_axis=0, concat_axis=0, tiled=True)  100 us
    all_to_all x2, starting transfers between devices, coupling_by_columns(): moved = lax.all_to_all(chunk, COLS, split_axis=0, concat_axis=0, tiled=True)  9.79 us
    dot_general x2, matrix products, coupling_by_columns(): lax.dot_general(moved.reshape(shards * rows, last - first), owned_all, ((...  7.73 us
    pallas_call x1, Pallas kernels, gamma_rows_last(): pl.pallas_call(gamma_kernel, out_shape=jax.ShapeDtypeStruct((width, 1, ro...  6.68 us
  transfers between devices with their start and end apart: 5, of which 3 were waited for; matrix products, arithmetic and copies ran while one was open for 8% of the time, Pallas kernels for 0%

profile of v12, /device:TPU:0, one launch (start us, length us, event | category | flops | bytes accessed | tf_op | source)
XLA Modules:
  0.0 160.1 jit_solution(9960242425953462022)
XLA Ops:
  6.5 0.0 all-gather.2.cloned.1.call-start
  6.5 1.3 fusion.3
  9.2 1.2 constant_dynamic-slice_fusion.1
  10.4 0.2 copy.13
  10.6 0.2 copy.14
  10.8 1.1 pad_maximum_fusion
  11.9 0.0 all-gather.2.cloned.1.call-update
  11.9 2.6 %reshape_squeeze.3 = bf16[512,8,300]{0,2,1:T(8,128)(2,1)S(1)} reshape(bf16[1,512,2400]{1,2,0:T(8,128)(2,1)} %param.4) | data formatting | bytes 4915200 | tf_op jit(solution)/shard_map/reshape;squeeze | solution.py:36
  14.6 1.5 slice.16
  16.1 6.3 %all-to-all-start = ((bf16[8,512,256]{1,2,0:T(8,128)(2,1)}), bf16[8,512,256]{1,2,0:T(8,128)(2,1)}, u32[]{:S(2)}, u32[]{:S(2)}) async-start(bf16[8,512,256]{1,2,0:T(8,128)(2,1)} %slice.16), calls=%async_computation | async-start | bytes 4194304 | tf_op jit(solution)/shard_map/all_to_all | solution.py:45
  22.4 0.8 slice.17
  23.2 90.5 %all-to-all-done = bf16[8,512,256]{1,2,0:T(8,128)(2,1)} async-done(((bf16[8,512,256]{1,2,0:T(8,128)(2,1)}), bf16[8,512,256]{1,2,0:T(8,128)(2,1)}, u32[]{:S(2)}, u32[]{:S(2)}) %all-to-all-start) | async-done | bytes 2097184 | tf_op jit(solution)/shard_map/all_to_all | solution.py:45
  113.7 2.8 %copy.15 = bf16[8,512,256]{2,1,0:T(8,128)(2,1)S(1)} copy(bf16[8,512,256]{1,2,0:T(8,128)(2,1)} %all-to-all-done) | data formatting | bytes 4194304 | tf_op jit(solution)/shard_map/all_to_all | solution.py:45
  116.6 0.0 all-gather.2.cloned.1.call-done.owned_ref
  116.6 0.0 copy-start
  116.6 4.3 %convolution_bitcast_fusion = f32[256,600]{1,0:T(8,128)S(1)} fusion(bf16[4096,600]{1,0:T(8,128)(2,1)} %all-gather.2.cloned.1.call-done.owned_ref, bf16[4096,256]{1,0:T(8,128)(2,1)S(1)} %bitcast.26), kind=kOutput, calls=%fused_computation | convolution fusion | flops 1258291200 | bytes 7626752 | tf_op jit(solution)/shard_map/dot_general | solution.py:46
  120.9 3.5 %all-to-all-start.1 = ((bf16[8,512,44]{1,2,0:T(8,128)(2,1)}), bf16[8,512,44]{1,2,0:T(8,128)(2,1)S(1)}, u32[]{:S(2)}, u32[]{:S(2)}) async-start(bf16[8,512,44]{1,2,0:T(8,128)(2,1)} %slice.17), calls=%async_computation.1 | async-start | bytes 786432 | tf_op jit(solution)/shard_map/all_to_all | solution.py:45
  125.1 0.2 copy.17
  125.3 1.6 collective-permute-start
  126.9 0.1 fusion.2
  127.0 9.9 %all-to-all-done.1 = bf16[8,512,44]{1,2,0:T(8,128)(2,1)S(1)} async-done(((bf16[8,512,44]{1,2,0:T(8,128)(2,1)}), bf16[8,512,44]{1,2,0:T(8,128)(2,1)S(1)}, u32[]{:S(2)}, u32[]{:S(2)}) %all-to-all-start.1) | async-done | bytes 360480 | tf_op jit(solution)/shard_map/all_to_all | solution.py:45
  136.9 0.2 copy.23
  137.1 0.1 copy.21
  137.3 3.4 %fusion.4 = f32[44,600]{1,0:T(8,128)S(1)} fusion(bf16[4096,44]{0,1:T(8,128)(2,1)S(1)} %bitcast.28, bf16[4096,600]{1,0:T(8,128)(2,1)} %all-gather.2.cloned.1.call-done.owned_ref), kind=kOutput, calls=%fused_computation.12 | convolution fusion | flops 216268800 | bytes 5381248 | tf_op jit(solution)/shard_map/dot_general | solution.py:46
  140.7 1.6 collective-permute-start.1
  142.2 0.1 pad_maximum_fusion.1
  142.3 0.0 collective-permute-done
  142.3 0.2 copy.18
  142.5 0.1 add.35
  142.6 3.0 %collective-permute-done.1 = f32[44,600]{1,0:T(8,128)S(1)} collective-permute-done((f32[44,600]{1,0:T(8,128)S(1)}, f32[44,600]{1,0:T(8,128)S(1)}, u32[]{:S(2)}, u32[]{:S(2)}) %collective-permute-start.1) | collective-permute-done | bytes 105632 | tf_op jit(solution)/shard_map/ppermute | solution.py:57
  145.6 1.0 fusion.1.amp_ref
  146.6 6.7 %shard_map.46 = f32[300,1,4096]{2,1,0:T(1,128)} custom-call(bf16[300,600]{1,0:T(8,128)(2,1)} %fusion.1.amp_ref, bf16[4096,600]{1,0:T(8,128)(2,1)} %all-gather.2.cloned.1.call-done.owned_ref), custom_call_target="tpu_custom_call" | custom-call | tf_op jit(solution)/shard_map/pallas_call | solution.py:71
  (4 shorter events, 0.1 us)
Async XLA Ops:
  6.5 110.1 %all-gather.2.cloned.1.call-start = ((), (), s32[]{:S(2)}) async-start(), calls=%async_computation.2 | async-start | bytes 5898240 | tf_op jit(solution)/shard_map/all_gather | solution.py:91
  16.1 97.6 %all-to-all-start = ((bf16[8,512,256]{1,2,0:T(8,128)(2,1)}), bf16[8,512,256]{1,2,0:T(8,128)(2,1)}, u32[]{:S(2)}, u32[]{:S(2)}) async-start(bf16[8,512,256]{1,2,0:T(8,128)(2,1)} %slice.16), calls=%async_computation | async-start | bytes 4194304 | tf_op jit(solution)/shard_map/all_to_all | solution.py:45
  116.6 8.5 %copy-start = (f32[2400]{0:T(1024)S(1)}, f32[2400]{0:T(1024)}, u32[]{:S(2)}) copy-start(f32[2400]{0:T(1024)} %param.6) | copy-start | bytes 28804
  120.9 15.9 %all-to-all-start.1 = ((bf16[8,512,44]{1,2,0:T(8,128)(2,1)}), bf16[8,512,44]{1,2,0:T(8,128)(2,1)S(1)}, u32[]{:S(2)}, u32[]{:S(2)}) async-start(bf16[8,512,44]{1,2,0:T(8,128)(2,1)} %slice.17), calls=%async_computation.1 | async-start | bytes 786432 | tf_op jit(solution)/shard_map/all_to_all | solution.py:45
  125.3 17.0 %collective-permute-start = (f32[256,600]{0,1:T(8,128)S(1)}, f32[256,600]{0,1:T(8,128)S(1)}, u32[]{:S(2)}, u32[]{:S(2)}) collective-permute-start(f32[256,600]{0,1:T(8,128)S(1)} %copy.17), channel_id=1, source_target_pairs={{0,2},{2,0},{1,3},{3,1},{4,6},{6,4},{5,7},{7,5},{8,10},{10,8},{9,1... | collective-permute-start | bytes 1843208 | tf_op jit(solution)/shard_map/ppermute | solution.py:57
  140.7 4.9 %collective-permute-start.1 = (f32[44,600]{1,0:T(8,128)S(1)}, f32[44,600]{1,0:T(8,128)S(1)}, u32[]{:S(2)}, u32[]{:S(2)}) collective-permute-start(f32[44,600]{1,0:T(8,128)S(1)} %fusion.4), channel_id=1, source_target_pairs={{0,2},{2,0},{1,3},{3,1},{4,6},{6,4},{5,7},{7,5},{8,10},{10,8},{9,1... | collective-permute-start | bytes 316808 | tf_op jit(solution)/shard_map/ppermute | solution.py:57
Sparse Core Ops, SparseCore 0:
  12.1 101.8 all-gather.1

commit v13 on v12

--- a/solution.py
+++ b/solution.py
@@ -3,11 +3,12 @@
 from jax import lax
 from jax.experimental import pallas as pl
 from jax.experimental.pallas import tpu as pltpu
+from jax.experimental.layout import Layout, with_layout_constraint
 from jax.sharding import PartitionSpec as P
 
 os_scale = 1.3
 COLS = ("col", "rep")
-PARTIAL_BYTES_MAX = 0
+PARTIAL_BYTES_MAX = 16 * 2**20
 LANES = 128
 ROW_BLOCK = 1024
 
@@ -64,10 +65,12 @@
     )
 
 
-def gamma_rows_last(amplitude, owned_all):
+def gamma_rows_last(amplitude, owned_all, block=None, place=None):
     width, depth = amplitude.shape
     rows = owned_all.shape[0]
-    block = ROW_BLOCK if rows % ROW_BLOCK == 0 else rows
+    if block is None:
+        block = ROW_BLOCK if rows % ROW_BLOCK == 0 else rows
+        place = lambda i: i
     out = pl.pallas_call(
         gamma_kernel,
         out_shape=jax.ShapeDtypeStruct((width, 1, rows), jnp.float32),
@@ -76,19 +79,32 @@
             pl.BlockSpec((width, depth), lambda i: (0, 0)),
             pl.BlockSpec((block, depth), lambda i: (i, 0)),
         ],
-        out_specs=pl.BlockSpec((width, 1, block), lambda i: (0, 0, i)),
+        out_specs=pl.BlockSpec((width, 1, block), lambda i: (0, 0, place(i))),
     )(amplitude, owned_all)
     return out.transpose(1, 2, 0)
 
 
-def body(b_aux, occ_energies, vir_energies, owners, *, shards, n_aux, by_partials):
+def gather_by_chip(owned):
+    owned = with_layout_constraint(owned, Layout((0, 1)))
+    gathered = lax.all_gather(owned, "col", axis=0, tiled=True)
+    return lax.all_gather(gathered, "rep", axis=0, tiled=True)
+
+
+def body(b_aux, occ_energies, vir_energies, owners, *, shards, n_rep, n_aux, by_partials):
     local = b_aux[0]
     width = local.shape[1] // shards
     col_energy = (vir_energies[None, :] - occ_energies[:, None]).reshape(-1)
     shard_index = lax.axis_index(COLS)
     energy_mine = lax.dynamic_slice_in_dim(col_energy, shard_index * width, width, 0)
     owned, owner_energy = owner_columns(local, col_energy, owners, width)
-    owned_all = lax.all_gather(owned, COLS, axis=0, tiled=True)
+    if by_partials:
+        n_col = shards // n_rep
+        owned_all = gather_by_chip(owned)
+        block = local.shape[0]
+        place = lambda i: (i % n_col) * n_rep + i // n_col
+    else:
+        owned_all = lax.all_gather(owned, COLS, axis=0, tiled=True)
+        block = place = None
     if by_partials:
         coupling = coupling_by_partials(local, owned, shards, width)
         coupling = exchange_sum(coupling, "aux", n_aux)
@@ -96,7 +112,7 @@
         coupling = coupling_by_columns(local, owned_all, shards, width, n_aux)
     denominator = energy_mine[:, None] + owner_energy[None, :]
     amplitude = (os_scale * coupling / denominator).astype(jnp.bfloat16)
-    return gamma_rows_last(amplitude, owned_all)
+    return gamma_rows_last(amplitude, owned_all, block, place)
 
 
 def solution(mesh):
@@ -108,7 +124,10 @@
         by_partials = partial_bytes <= PARTIAL_BYTES_MAX
         placed = (P(("groups", "aux"), COLS, None), P("groups"), P("groups"), P())
         return jax.shard_map(
-            lambda *a: body(*a, shards=shards, n_aux=mesh.shape["aux"], by_partials=by_partials),
+            lambda *a: body(
+                *a, shards=shards, n_rep=mesh.shape["rep"], n_aux=mesh.shape["aux"],
+                by_partials=by_partials,
+            ),
             mesh=mesh,
             in_specs=placed,
             out_specs=P(("groups", "aux"), None, COLS),

time: 161 us -> 165 us (1.025)
  waiting for transfers between devices: 103 us -> 123 us
  starting transfers between devices: 12.9 us -> 1.57 us
  local copies, waits for them, and re-layouts: 11.7 us -> 5.77 us
  matrix products: 7.73 us -> 4.75 us
  Pallas kernels: 6.68 us -> 8.61 us
    all_to_all x2 -> x0, waiting for transfers between devices: 100 us -> none  [coupling_by_columns(): moved = lax.all_to_all(chunk, COLS, split_axis=0, concat_axis=0, tiled=True)]
    all_gather x1 -> x2, waiting for transfers between devices: 0.02 us -> 71.4 us  [the longest x1 71.4 us: gather_by_chip(): gathered = lax.all_gather(owned, 'col', axis=0, tiled=True)]
    reduce_scatter x0 -> x1, waiting for transfers between devices: none -> 38 us  [coupling_by_partials(): lax.psum_scatter(partial_value, COLS, scatter_dimension=0, tiled=False)]
    ppermute x2 -> x1, waiting for transfers between devices: 3 us -> 13.6 us  [exchange_sum(): lax.ppermute(value, axis, [(i, (i + step) % size) for i in range(size)])]
    all_to_all x2 -> x0, starting transfers between devices: 9.79 us -> none  [coupling_by_columns(): moved = lax.all_to_all(chunk, COLS, split_axis=0, concat_axis=0, tiled=True)]
    all_to_all x2 -> x0, local copies, waits for them, and re-layouts: 3.05 us -> none  [coupling_by_columns(): moved = lax.all_to_all(chunk, COLS, split_axis=0, concat_axis=0, tiled=True)]
    dot_general x2 -> x1, matrix products: 7.73 us -> 4.75 us  [coupling_by_partials(): lax.dot_general(blocked, owned, (((0,), (0,)), ((), ())), preferred_eleme...]
    slice x2 -> x0, local copies, waits for them, and re-layouts: 2.32 us -> none  [coupling_by_columns(): chunk = blocked[:, :, first:last]]
  transfers between devices with their start and end apart: 5 -> 4, of which waited for: 3 -> 3; matrix products, arithmetic and copies ran while one was open for 8% -> 6% of each run, Pallas kernels for 0% -> 0%
where the time goes in v13:
time: 165 us; the launch traced here: 164 us
  waiting for transfers between devices  123 us (75%)
  between operations  16.9 us (10%)
  Pallas kernels  8.61 us (5%)
  local copies, waits for them, and re-layouts  5.77 us (3%)
  matrix products  4.75 us (3%)
  other arithmetic  3.24 us (2%)
    all_gather x1, waiting for transfers between devices, gather_by_chip(): gathered = lax.all_gather(owned, 'col', axis=0, tiled=True)  71.4 us
    reduce_scatter x1, waiting for transfers between devices, coupling_by_partials(): lax.psum_scatter(partial_value, COLS, scatter_dimension=0, tiled=False)  38 us
    ppermute x1, waiting for transfers between devices, exchange_sum(): lax.ppermute(value, axis, [(i, (i + step) % size) for i in range(size)])  13.6 us
    pallas_call x1, Pallas kernels, gamma_rows_last(): pl.pallas_call(gamma_kernel, out_shape=jax.ShapeDtypeStruct((width, 1, ro...  8.61 us
    dot_general x1, matrix products, coupling_by_partials(): lax.dot_general(blocked, owned, (((0,), (0,)), ((), ())), preferred_eleme...  4.75 us
  transfers between devices with their start and end apart: 4, of which 3 were waited for; matrix products, arithmetic and copies ran while one was open for 6% of the time, Pallas kernels for 0%

profile of v13, /device:TPU:0, one launch (start us, length us, event | category | flops | bytes accessed | tf_op | source)
XLA Modules:
  0.0 163.9 jit_solution(13116950963147131829)
XLA Ops:
  7.4 0.0 all-gather.3.cloned.1.call-start
  7.4 1.3 fusion.2
  10.0 1.2 constant_dynamic-slice_fusion.1
  11.2 0.2 copy.7
  11.4 0.2 copy.8
  11.7 1.1 pad_maximum_fusion
  12.7 0.0 all-gather.3.cloned.1.call-update
  12.7 0.0 copy-start
  12.8 0.0 reduce-scatter.2.cloned.1.call-start
  12.8 2.7 %reshape_squeeze.3 = bf16[512,8,300]{0,2,1:T(8,128)(2,1)S(1)} reshape(bf16[1,512,2400]{1,2,0:T(8,128)(2,1)} %param.4) | data formatting | bytes 4915200 | tf_op jit(solution)/shard_map/reshape;squeeze | solution.py:28
  15.5 0.0 copy-done
  15.5 4.8 %convolution_bitcast_fusion = f32[8,300,600]{2,1,0:T(8,128)} fusion(bf16[512,8,300]{0,2,1:T(8,128)(2,1)S(1)} %reshape_squeeze.3, bf16[512,600]{1,0:T(8,128)(2,1)S(1)} %copy-done), kind=kOutput, calls=%fused_computation | convolution fusion | flops 1474560000 | bytes 8832000 | tf_op jit(solution)/shard_map/dot_general | solution.py:29
  20.3 0.0 reduce-scatter.2.cloned.1.call-update
  20.3 0.0 copy-start.1
  20.3 0.0 all-gather.5.cloned.1.call-start
  20.4 71.4 %all-gather.3.cloned.1.call-done = bf16[2048,600]{1,0:T(8,128)(2,1)} async-done(((bf16[512,600]{1,0:T(8,128)(2,1)}), bf16[2048,600]{1,0:T(8,128)(2,1)}) %all-gather.3.cloned.1.call-update) | async-done | bytes 2457616 | tf_op jit(solution)/shard_map/all_gather | solution.py:89
  91.7 0.0 all-gather.5.cloned.1.call-update
  91.8 38.0 %reduce-scatter.2.cloned.1.call-done = f32[1,300,600]{2,1,0:T(8,128)} async-done(((f32[8,300,600]{2,1,0:T(8,128)}), f32[1,300,600]{2,1,0:T(8,128)}) %reduce-scatter.2.cloned.1.call-update) | async-done | bytes 720016 | tf_op jit(solution)/shard_map/reduce_scatter | solution.py:32
  129.8 1.5 collective-permute-start
  131.9 0.0 copy-done.1
  132.0 0.1 fusion.1
  132.1 0.1 pad_maximum_fusion.1
  132.1 13.6 %collective-permute-done = f32[300,600]{1,0:T(8,128)S(1)} collective-permute-done((f32[300,600]{1,0:T(8,128)}, f32[300,600]{1,0:T(8,128)S(1)}, u32[]{:S(2)}, u32[]{:S(2)}) %collective-permute-start) | collective-permute-done | bytes 720032 | tf_op jit(solution)/shard_map/ppermute | solution.py:58
  145.7 2.1 %divide_convert_fusion.amp_ref = bf16[300,600]{1,0:T(8,128)(2,1)} fusion(f32[300,600]{1,0:T(8,128)S(1)} %collective-permute-done, f32[600]{0:T(1024)S(1)} %pad_maximum_fusion.1, f32[300]{0:T(512)S(1)} %get-tuple-element.7, f32[1,300,600]{2,1,0:T(8,128)} %reduce-scatter.2.cloned.1.call-done), kind=kLoop, calls=%fused_computation.1 | loop fusion | flops 900000 | bytes 1803600 | tf_op jit(solution)/shard_map/convert_element_type | solution.py:114
  147.8 0.0 all-gather.5.cloned.1.call-done.owned_ref
  147.8 8.6 %shard_map.46 = f32[300,1,4096]{2,1,0:T(1,128)} custom-call(bf16[300,600]{1,0:T(8,128)(2,1)} %divide_convert_fusion.amp_ref, bf16[4096,600]{1,0:T(8,128)(2,1)} %all-gather.5.cloned.1.call-done.owned_ref), custom_call_target="tpu_custom_call" | custom-call | tf_op jit(solution)/shard_map/pallas_call | solution.py:74
  (1 shorter events, 0.0 us)
Async XLA Ops:
  7.4 84.4 %all-gather.3.cloned.1.call-start = ((), (), s32[]{:S(2)}) async-start(), calls=%async_computation.2 | async-start | bytes 3276800 | tf_op jit(solution)/shard_map/all_gather | solution.py:89
  12.7 2.8 %copy-start = (bf16[512,600]{1,0:T(8,128)(2,1)S(1)}, bf16[512,600]{1,0:T(8,128)(2,1)}, u32[]{:S(2)}) copy-start(bf16[512,600]{1,0:T(8,128)(2,1)} %pad_maximum_fusion) | copy-start | bytes 1843204
  12.8 117.1 %reduce-scatter.2.cloned.1.call-start = ((), (), s32[]{:S(2)}) async-start(), calls=%async_computation.1 | async-start | bytes 7004160 | tf_op jit(solution)/shard_map/reduce_scatter | solution.py:32
  20.3 111.7 %copy-start.1 = (f32[2400]{0:T(1024)S(1)}, f32[2400]{0:T(1024)}, u32[]{:S(2)}) copy-start(f32[2400]{0:T(1024)} %param.6) | copy-start | bytes 28804
  20.3 127.5 %all-gather.5.cloned.1.call-start = ((), (), s32[]{:S(2)}) async-start(), calls=%async_computation.3 | async-start | bytes 7864320 | tf_op jit(solution)/shard_map/all_gather | solution.py:90
  129.8 15.9 %collective-permute-start = (f32[300,600]{1,0:T(8,128)}, f32[300,600]{1,0:T(8,128)S(1)}, u32[]{:S(2)}, u32[]{:S(2)}) collective-permute-start(f32[300,600]{1,0:T(8,128)} %bitcast.19), channel_id=1, source_target_pairs={{0,2},{2,0},{1,3},{3,1},{4,6},{6,4},{5,7},{7,5},{8,10},{10,8},{9,1... | collective-permute-start | bytes 2160008 | tf_op jit(solution)/shard_map/ppermute | solution.py:58
Sparse Core Ops, SparseCore 0:
  12.9 78.8 all-gather.2
  93.4 17.1 all-gather.4
Sparse Core Ops, SparseCore 1:
  20.4 109.4 reduce-scatter.1

commit v14 on v8

--- a/solution.py
+++ b/solution.py
@@ -8,6 +8,7 @@
 os_scale = 1.3
 COLS = ("col", "rep")
 PARTIAL_BYTES_MAX = 0
+LINE_MAX = 8
 
 
 def owner_columns(local, col_energy, owners, width):
@@ -29,10 +30,12 @@
     return lax.psum_scatter(partial_value, COLS, scatter_dimension=0, tiled=False)
 
 
-def coupling_by_columns(local, owned_all, shards, width):
+def coupling_by_columns(local, owned_all, shards, width, order=None):
     rows = local.shape[0]
     blocked = local.reshape(rows, shards, width).transpose(1, 0, 2)
     moved = lax.all_to_all(blocked, COLS, split_axis=0, concat_axis=0, tiled=True)
+    if order is not None:
+        moved = order(moved)
     return lax.dot_general(
         moved.reshape(shards * rows, width), owned_all, (((0,), (0,)), ((), ())),
         preferred_element_type=jnp.float32,
@@ -46,41 +49,80 @@
     return total
 
 
-def gamma_kernel(amp_ref, owned_ref, out_ref):
+def gamma_kernel(ids_ref, amp_ref, owned_ref, out_ref):
     out_ref[:, 0, :] = lax.dot_general(
         amp_ref[...], owned_ref[...], (((1,), (1,)), ((), ())), preferred_element_type=jnp.float32
     )
 
 
-def gamma_rows_last(amplitude, owned_all):
-    width = amplitude.shape[0]
+def gamma_rows_last(amplitude, owned_all, ids, block, place):
+    width, depth = amplitude.shape
     rows = owned_all.shape[0]
     out = pl.pallas_call(
         gamma_kernel,
         out_shape=jax.ShapeDtypeStruct((width, 1, rows), jnp.float32),
-        in_specs=[pl.BlockSpec(memory_space=pltpu.VMEM)] * 2,
-        out_specs=pl.BlockSpec(memory_space=pltpu.VMEM),
-        compiler_params=pltpu.CompilerParams(vmem_limit_bytes=48 * 2**20),
-    )(amplitude, owned_all)
+        grid_spec=pltpu.PrefetchScalarGridSpec(
+            num_scalar_prefetch=1,
+            grid=(rows // block,),
+            in_specs=[
+                pl.BlockSpec((width, depth), lambda i, ids: (0, 0)),
+                pl.BlockSpec((block, depth), lambda i, ids: (i, 0)),
+            ],
+            out_specs=pl.BlockSpec((width, 1, block), lambda i, ids: (0, 0, place(i, ids))),
+        ),
+    )(ids, amplitude, owned_all)
     return out.transpose(1, 2, 0)
 
 
-def body(b_aux, occ_energies, vir_energies, owners, *, shards, n_aux, by_partials):
+def gather_relative(owned, n_col, n_rep):
+    mine = [owned]
+    for step in range(1, n_col):
+        mine.append(lax.ppermute(owned, "col", [(i, (i - step) % n_col) for i in range(n_col)]))
+    mine = jnp.stack(mine)
+    blocks = [mine]
+    for step in range(1, n_rep):
+        blocks.append(lax.ppermute(mine, "rep", [(i, (i - step) % n_rep) for i in range(n_rep)]))
+    return jnp.stack(blocks, axis=1)
+
+
+def relative_order(moved, n_col, n_rep):
+    me = lax.axis_index("col")
+    rep = lax.axis_index("rep")
+    by_chip = moved.reshape((n_col, n_rep) + moved.shape[1:])
+    doubled = jnp.concatenate([by_chip, by_chip], axis=0)
+    by_chip = lax.dynamic_slice_in_dim(doubled, me, n_col, 0)
+    doubled = jnp.concatenate([by_chip, by_chip], axis=1)
+    return lax.dynamic_slice_in_dim(doubled, rep, n_rep, 1)
+
+
+def body(b_aux, occ_energies, vir_energies, owners, *, shards, n_rep, n_aux, by_partials):
     local = b_aux[0]
     width = local.shape[1] // shards
     col_energy = (vir_energies[None, :] - occ_energies[:, None]).reshape(-1)
     shard_index = lax.axis_index(COLS)
     energy_mine = lax.dynamic_slice_in_dim(col_energy, shard_index * width, width, 0)
     owned, owner_energy = owner_columns(local, col_energy, owners, width)
-    owned_all = lax.all_gather(owned, COLS, axis=0, tiled=True)
+    n_col = shards // n_rep
+    rows = local.shape[0]
+    ids = jnp.stack([lax.axis_index("col"), lax.axis_index("rep")]).astype(jnp.int32)
+    if n_col <= LINE_MAX and not by_partials:
+        owned_all = gather_relative(owned, n_col, n_rep).reshape(shards * rows, owned.shape[1])
+        order = lambda moved: relative_order(moved, n_col, n_rep)
+        block = rows
+        place = lambda i, ids: ((ids[0] + i // n_rep) % n_col) * n_rep + (ids[1] + i % n_rep) % n_rep
+    else:
+        owned_all = lax.all_gather(owned, COLS, axis=0, tiled=True)
+        order = None
+        block = owned_all.shape[0]
+        place = lambda i, ids: i
     if by_partials:
         coupling = coupling_by_partials(local, owned, shards, width)
     else:
-        coupling = coupling_by_columns(local, owned_all, shards, width)
+        coupling = coupling_by_columns(local, owned_all, shards, width, order)
     coupling = exchange_sum(coupling, "aux", n_aux)
     denominator = energy_mine[:, None] + owner_energy[None, :]
     amplitude = (os_scale * coupling / denominator).astype(jnp.bfloat16)
-    return gamma_rows_last(amplitude, owned_all)
+    return gamma_rows_last(amplitude, owned_all, ids, block, place)
 
 
 def solution(mesh):
@@ -92,7 +134,10 @@
         by_partials = partial_bytes <= PARTIAL_BYTES_MAX
         placed = (P(("groups", "aux"), COLS, None), P("groups"), P("groups"), P())
         return jax.shard_map(
-            lambda *a: body(*a, shards=shards, n_aux=mesh.shape["aux"], by_partials=by_partials),
+            lambda *a: body(
+                *a, shards=shards, n_rep=mesh.shape["rep"], n_aux=mesh.shape["aux"],
+                by_partials=by_partials,
+            ),
             mesh=mesh,
             in_specs=placed,
             out_specs=P(("groups", "aux"), None, COLS),

time: 162 us -> 162 us (level)
  the two profiles are of different devices: /device:TPU:0 before, /device:TPU:8 now
where the time goes in v14:
time: 162 us; the launch traced here: 161 us
  waiting for transfers between devices  109 us (67%)
  local copies, waits for them, and re-layouts  13.8 us (9%)
  starting transfers between devices  11.5 us (7%)
  other arithmetic  10.7 us (7%)
  Pallas kernels  9.32 us (6%)
  matrix products  4.41 us (3%)
  between operations  2 us (1%)
    ppermute x3, waiting for transfers between devices, gather_relative(): lax.ppermute(owned, 'col', [(i, (i - step) % n_col) for i in range(n_col)])  101 us
    pallas_call x1, Pallas kernels, gamma_rows_last(): pl.pallas_call(gamma_kernel, out_shape=jax.ShapeDtypeStruct((width, 1, ro...  9.32 us
    another operation x1, local copies, waits for them, and re-layouts, gather_relative(): return jnp.stack(blocks, axis=1)  7.75 us
    another operation x2, other arithmetic, gather_relative(): return jnp.stack(blocks, axis=1)  6.8 us
    all_to_all x1, starting transfers between devices, coupling_by_columns(): lax.all_to_all(blocked, COLS, split_axis=0, concat_axis=0, tiled=True)  5.45 us
    ppermute x3, starting transfers between devices, gather_relative(): lax.ppermute(owned, 'col', [(i, (i - step) % n_col) for i in range(n_col)])  4.44 us
    dot_general x1, matrix products, coupling_by_columns(): lax.dot_general(moved.reshape(shards * rows, width), owned_all, (((0,), (...  4.41 us
    ppermute x1, waiting for transfers between devices, exchange_sum(): lax.ppermute(value, axis, [(i, (i + step) % size) for i in range(size)])  4.37 us
  transfers between devices with their start and end apart: 6, of which 5 were waited for; matrix products, arithmetic and copies ran while one was open for 11% of the time, Pallas kernels for 0%

profile of v14, /device:TPU:8, one launch (start us, length us, event | category | flops | bytes accessed | tf_op | source)
XLA Modules:
  0.0 161.1 jit_solution(15490851419847398495)
XLA Ops:
  0.0 4.1 %reshape_squeeze.3 = bf16[512,8,300]{0,2,1:T(8,128)(2,1)} reshape(bf16[1,512,2400]{1,2,0:T(8,128)(2,1)} %param.4) | data formatting | bytes 4915200 | tf_op jit(solution)/shard_map/reshape;squeeze | solution.py:35
  4.1 0.0 copy-start.3
  4.1 5.5 %all-to-all-start = ((bf16[8,512,300]{1,2,0:T(8,128)(2,1)}), bf16[8,512,300]{1,2,0:T(8,128)(2,1)S(1)}, u32[]{:S(2)}, u32[]{:S(2)}) async-start(bf16[8,512,300]{1,2,0:T(8,128)(2,1)} %bitcast.32), calls=%async_computation | async-start | bytes 4980736 | tf_op jit(solution)/shard_map/all_to_all | solution.py:36
  9.5 0.0 copy-done.3
  9.5 0.6 fusion.11
  11.4 1.2 dynamic-slice_bitcast_fusion.1
  12.7 0.1 pad_maximum_fusion.2
  12.8 1.5 collective-permute-start.2
  14.3 1.0 collective-permute-start.1
  15.3 1.9 %collective-permute-start = (bf16[512,600]{0,1:T(8,128)(2,1)S(1)}, bf16[512,600]{0,1:T(8,128)(2,1)S(1)}, u32[]{:S(2)}, u32[]{:S(2)}) collective-permute-start(bf16[512,600]{0,1:T(8,128)(2,1)S(1)} %pad_maximum_fusion.2), channel_id=1, source_target_pairs={{0,12},{4,0},{8,4},{12,8},{1,13},{5,1},{9,5},{13,9},{2,14},{6,2},{... | collective-permute-start | bytes 1843208 | tf_op jit(solution)/shard_map/ppermute | solution.py:80
  17.2 0.1 fusion.12
  17.3 85.7 %collective-permute-done.2 = bf16[512,600]{0,1:T(8,128)(2,1)S(1)} collective-permute-done((bf16[512,600]{0,1:T(8,128)(2,1)S(1)}, bf16[512,600]{0,1:T(8,128)(2,1)S(1)}, u32[]{:S(2)}, u32[]{:S(2)}) %collective-permute-start.2) | collective-permute-done | bytes 614432 | tf_op jit(solution)/shard_map/ppermute | solution.py:80
  103.0 13.1 %collective-permute-done.1 = bf16[512,600]{0,1:T(8,128)(2,1)S(1)} collective-permute-done((bf16[512,600]{0,1:T(8,128)(2,1)S(1)}, bf16[512,600]{0,1:T(8,128)(2,1)S(1)}, u32[]{:S(2)}, u32[]{:S(2)}) %collective-permute-start.1) | collective-permute-done | bytes 614432 | tf_op jit(solution)/shard_map/ppermute | solution.py:80
  116.1 2.1 %collective-permute-done = bf16[512,600]{0,1:T(8,128)(2,1)S(1)} collective-permute-done((bf16[512,600]{0,1:T(8,128)(2,1)S(1)}, bf16[512,600]{0,1:T(8,128)(2,1)S(1)}, u32[]{:S(2)}, u32[]{:S(2)}) %collective-permute-start) | collective-permute-done | bytes 614432 | tf_op jit(solution)/shard_map/ppermute | solution.py:80
  118.3 2.4 %fusion.9 = (bf16[4,1,512,600]{2,3,1,0:T(8,128)(2,1)}, bf16[4,512,600]{1,2,0:T(8,128)(2,1)}) fusion(bf16[1,512,600]{1,2,0:T(8,128)(2,1)S(1)} %bitcast.33, bf16[1,512,600]{1,2,0:T(8,128)(2,1)S(1)} %bitcast.34, bf16[1,512,600]{1,2,0:T(8,128)(2,1)S(1)} %bitcast.35, bf16[1,512,600]{1,2,0:T(8,128)(2,1)S(1)} %fusion.12), kind=kLoop, calls=%fused_computation.19 | loop fusion | flops 3686400 | bytes 7372800 | tf_op jit(solution)/shard_map/stack | solution.py:85
  120.7 0.0 collective-permute-start.3
  120.7 0.0 all-to-all-done
  120.7 0.9 fusion.3
  121.6 4.1 %collective-permute-done.3 = bf16[4,512,600]{1,2,0:T(8,128)(2,1)} collective-permute-done((bf16[4,512,600]{1,2,0:T(8,128)(2,1)}, bf16[4,512,600]{1,2,0:T(8,128)(2,1)}, u32[]{:S(2)}, u32[]{:S(2)}) %collective-permute-start.3) | collective-permute-done | bytes 2457632 | tf_op jit(solution)/shard_map/ppermute | solution.py:84
  125.7 0.0 copy-done
  125.7 4.4 %fusion.4 = f32[300,600]{1,0:T(8,128)S(1)} fusion(s32[]{:T(128)S(6)} %select_n.18, bf16[4,2,512,300]{2,3,1,0:T(8,128)(2,1)S(1)} %fusion.3, bf16[4,1,512,600]{2,3,1,0:T(8,128)(2,1)} %bitcast.14, bf16[4,1,512,600]{2,3,1,0:T(8,128)(2,1)S(1)} %copy-done), kind=kOutput, calls=%fused_computation.9 | convolution fusion | flops 1478246400 | bytes 8092804 | tf_op jit(solution)/shard_map/dot_general | solution.py:39
  130.1 1.6 collective-permute-start.4
  131.7 0.7 pad_add_fusion.ids_ref
  133.0 0.0 copy-done.2
  133.0 0.1 fusion.10
  133.1 0.1 pad_maximum_fusion.3
  133.2 0.0 copy-done.1
  133.2 4.4 %pad_maximum_fusion = bf16[4,2,512,600]{2,3,1,0:T(8,128)(2,1)} fusion(bf16[4,1,512,600]{2,3,1,0:T(8,128)(2,1)} %bitcast.14, bf16[4,1,512,600]{2,3,1,0:T(8,128)(2,1)S(1)} %copy-done.1), kind=kLoop, calls=%fused_computation.4 | loop fusion | flops 2457600 | bytes 9830400 | tf_op jit(solution)/shard_map/stack | solution.py:85
  137.6 7.7 %copy.8 = bf16[4,2,512,600]{3,2,1,0:T(8,128)(2,1)} copy(bf16[4,2,512,600]{2,3,1,0:T(8,128)(2,1)} %pad_maximum_fusion) | data formatting | bytes 9830400 | tf_op jit(solution)/shard_map/stack | solution.py:85
  145.3 4.4 %collective-permute-done.4 = f32[300,600]{1,0:T(8,128)} collective-permute-done((f32[300,600]{1,0:T(8,128)S(1)}, f32[300,600]{1,0:T(8,128)}, u32[]{:S(2)}, u32[]{:S(2)}) %collective-permute-start.4) | collective-permute-done | bytes 720032 | tf_op jit(solution)/shard_map/ppermute | solution.py:48
  149.7 2.1 %divide_convert_fusion.amp_ref = bf16[300,600]{1,0:T(8,128)(2,1)} fusion(f32[300,600]{1,0:T(8,128)S(1)} %fusion.4, f32[300,600]{1,0:T(8,128)} %collective-permute-done.4, f32[600]{0:T(1024)S(1)} %pad_maximum_fusion.3, f32[300]{0:T(512)S(1)} %get-tuple-element.9), kind=kLoop, calls=%fused_computation.10 | loop fusion | flops 900000 | bytes 1803600 | tf_op jit(solution)/shard_map/convert_element_type | solution.py:124
  151.8 9.3 %shard_map.46 = f32[300,1,4096]{2,1,0:T(1,128)} custom-call(s32[2]{0:T(128)} %pad_add_fusion.ids_ref, bf16[300,600]{1,0:T(8,128)(2,1)} %divide_convert_fusion.amp_ref, bf16[4096,600]{1,0:T(8,128)(2,1)} %bitcast.30), custom_call_target="tpu_custom_call" | custom-call | tf_op jit(solution)/shard_map/pallas_call | solution.py:61
  (4 shorter events, 0.0 us)
Async XLA Ops:
  4.1 5.5 %copy-start.3 = (s32[2]{0:T(128)S(1)}, s32[2]{0:T(128)}, u32[]{:S(2)}) copy-start(s32[2]{0:T(128)} %param.7) | copy-start | bytes 28
  4.1 116.6 %all-to-all-start = ((bf16[8,512,300]{1,2,0:T(8,128)(2,1)}), bf16[8,512,300]{1,2,0:T(8,128)(2,1)S(1)}, u32[]{:S(2)}, u32[]{:S(2)}) async-start(bf16[8,512,300]{1,2,0:T(8,128)(2,1)} %bitcast.32), calls=%async_computation | async-start | bytes 4980736 | tf_op jit(solution)/shard_map/all_to_all | solution.py:36
  12.8 90.2 %collective-permute-start.2 = (bf16[512,600]{0,1:T(8,128)(2,1)S(1)}, bf16[512,600]{0,1:T(8,128)(2,1)S(1)}, u32[]{:S(2)}, u32[]{:S(2)}) collective-permute-start(bf16[512,600]{0,1:T(8,128)(2,1)S(1)} %pad_maximum_fusion.2), channel_id=1, source_target_pairs={{0,4},{4,8},{8,12},{12,0},{1,5},{5,9},{9,13},{13,1},{2,6},{6,10},{... | collective-permute-start | bytes 1843208 | tf_op jit(solution)/shard_map/ppermute | solution.py:80
  14.3 101.8 %collective-permute-start.1 = (bf16[512,600]{0,1:T(8,128)(2,1)S(1)}, bf16[512,600]{0,1:T(8,128)(2,1)S(1)}, u32[]{:S(2)}, u32[]{:S(2)}) collective-permute-start(bf16[512,600]{0,1:T(8,128)(2,1)S(1)} %pad_maximum_fusion.2), channel_id=1, source_target_pairs={{0,8},{4,12},{8,0},{12,4},{1,9},{5,13},{9,1},{13,5},{2,10},{6,14},... | collective-permute-start | bytes 1843208 | tf_op jit(solution)/shard_map/ppermute | solution.py:80
  15.3 103.0 %collective-permute-start = (bf16[512,600]{0,1:T(8,128)(2,1)S(1)}, bf16[512,600]{0,1:T(8,128)(2,1)S(1)}, u32[]{:S(2)}, u32[]{:S(2)}) collective-permute-start(bf16[512,600]{0,1:T(8,128)(2,1)S(1)} %pad_maximum_fusion.2), channel_id=1, source_target_pairs={{0,12},{4,0},{8,4},{12,8},{1,13},{5,1},{9,5},{13,9},{2,14},{6,2},{... | collective-permute-start | bytes 1843208 | tf_op jit(solution)/shard_map/ppermute | solution.py:80
  120.7 5.0 %collective-permute-start.3 = (bf16[4,512,600]{1,2,0:T(8,128)(2,1)}, bf16[4,512,600]{1,2,0:T(8,128)(2,1)}, u32[]{:S(2)}, u32[]{:S(2)}) collective-permute-start(bf16[4,512,600]{1,2,0:T(8,128)(2,1)} %get-tuple-element.6), channel_id=1, source_target_pairs={{0,1},{1,0},{2,3},{3,2},{4,5},{5,4},{6,7},{7,6},{8,9},{9,8},{10,11... | collective-permute-start | bytes 7372808 | tf_op jit(solution)/shard_map/ppermute | solution.py:84
  120.7 5.0 %copy-start = (bf16[4,1,512,600]{2,3,1,0:T(8,128)(2,1)S(1)}, bf16[4,1,512,600]{2,3,1,0:T(8,128)(2,1)}, u32[]{:S(2)}) copy-start(bf16[4,1,512,600]{2,3,1,0:T(8,128)(2,1)} %get-tuple-element.5) | copy-start | bytes 7372804
  125.7 7.3 %copy-start.2 = (f32[2400]{0:T(1024)S(1)}, f32[2400]{0:T(1024)}, u32[]{:S(2)}) copy-start(f32[2400]{0:T(1024)} %param.6) | copy-start | bytes 28804
  125.7 7.5 %copy-start.1 = (bf16[4,1,512,600]{2,3,1,0:T(8,128)(2,1)S(1)}, bf16[4,1,512,600]{2,3,1,0:T(8,128)(2,1)}, u32[]{:S(2)}) copy-start(bf16[4,1,512,600]{2,3,1,0:T(8,128)(2,1)} %get-tuple-element.5) | copy-start | bytes 7372804
  130.1 19.6 %collective-permute-start.4 = (f32[300,600]{1,0:T(8,128)S(1)}, f32[300,600]{1,0:T(8,128)}, u32[]{:S(2)}, u32[]{:S(2)}) collective-permute-start(f32[300,600]{1,0:T(8,128)S(1)} %fusion.4), channel_id=1, source_target_pairs={{0,2},{2,0},{1,3},{3,1},{4,6},{6,4},{5,7},{7,5},{8,10},{10,8},{9,1... | collective-permute-start | bytes 2160008 | tf_op jit(solution)/shard_map/ppermute | solution.py:48

commit v15 on v14

--- a/solution.py
+++ b/solution.py
@@ -30,16 +30,18 @@
     return lax.psum_scatter(partial_value, COLS, scatter_dimension=0, tiled=False)
 
 
-def coupling_by_columns(local, owned_all, shards, width, order=None):
+def coupling_by_columns(local, owned_parts, shards, width, order=None):
     rows = local.shape[0]
     blocked = local.reshape(rows, shards, width).transpose(1, 0, 2)
     moved = lax.all_to_all(blocked, COLS, split_axis=0, concat_axis=0, tiled=True)
-    if order is not None:
-        moved = order(moved)
-    return lax.dot_general(
-        moved.reshape(shards * rows, width), owned_all, (((0,), (0,)), ((), ())),
-        preferred_element_type=jnp.float32,
-    )
+    moved_parts = [moved.reshape(shards * rows, width)] if order is None else order(moved)
+    total = None
+    for moved_part, owned_part in zip(moved_parts, owned_parts):
+        term = lax.dot_general(
+            moved_part, owned_part, (((0,), (0,)), ((), ())), preferred_element_type=jnp.float32
+        )
+        total = term if total is None else total + term
+    return total
 
 
 def exchange_sum(value, axis, size):
@@ -49,28 +51,36 @@
     return total
 
 
-def gamma_kernel(ids_ref, amp_ref, owned_ref, out_ref):
-    out_ref[:, 0, :] = lax.dot_general(
-        amp_ref[...], owned_ref[...], (((1,), (1,)), ((), ())), preferred_element_type=jnp.float32
-    )
+def gamma_kernel(ids_ref, amp_ref, *refs):
+    out_ref = refs[-1]
+    owned_refs = refs[:-1]
+    n_rep = len(owned_refs)
+    rows = owned_refs[0].shape[0]
+    for step, owned_ref in enumerate(owned_refs):
+        start = pl.multiple_of(((ids_ref[1] + step) % n_rep) * rows, rows)
+        out_ref[:, 0, pl.ds(start, rows)] = lax.dot_general(
+            amp_ref[...], owned_ref[...], (((1,), (1,)), ((), ())),
+            preferred_element_type=jnp.float32,
+        )
 
 
-def gamma_rows_last(amplitude, owned_all, ids, block, place):
+def gamma_rows_last(amplitude, owned_parts, ids, block, place):
     width, depth = amplitude.shape
-    rows = owned_all.shape[0]
+    n_parts = len(owned_parts)
+    rows = owned_parts[0].shape[0] * n_parts
     out = pl.pallas_call(
         gamma_kernel,
         out_shape=jax.ShapeDtypeStruct((width, 1, rows), jnp.float32),
         grid_spec=pltpu.PrefetchScalarGridSpec(
             num_scalar_prefetch=1,
-            grid=(rows // block,),
-            in_specs=[
-                pl.BlockSpec((width, depth), lambda i, ids: (0, 0)),
-                pl.BlockSpec((block, depth), lambda i, ids: (i, 0)),
-            ],
-            out_specs=pl.BlockSpec((width, 1, block), lambda i, ids: (0, 0, place(i, ids))),
+            grid=(rows // (block * n_parts),),
+            in_specs=[pl.BlockSpec((width, depth), lambda i, ids: (0, 0))]
+            + [pl.BlockSpec((block, depth), lambda i, ids: (i, 0))] * n_parts,
+            out_specs=pl.BlockSpec(
+                (width, 1, block * n_parts), lambda i, ids: (0, 0, place(i, ids))
+            ),
         ),
-    )(ids, amplitude, owned_all)
+    )(ids, amplitude, *owned_parts)
     return out.transpose(1, 2, 0)
 
 
@@ -78,11 +88,11 @@
     mine = [owned]
     for step in range(1, n_col):
         mine.append(lax.ppermute(owned, "col", [(i, (i - step) % n_col) for i in range(n_col)]))
-    mine = jnp.stack(mine)
-    blocks = [mine]
+    mine = jnp.concatenate(mine, axis=0)
+    parts = [mine]
     for step in range(1, n_rep):
-        blocks.append(lax.ppermute(mine, "rep", [(i, (i - step) % n_rep) for i in range(n_rep)]))
-    return jnp.stack(blocks, axis=1)
+        parts.append(lax.ppermute(mine, "rep", [(i, (i - step) % n_rep) for i in range(n_rep)]))
+    return parts
 
 
 def relative_order(moved, n_col, n_rep):
@@ -91,8 +101,11 @@
     by_chip = moved.reshape((n_col, n_rep) + moved.shape[1:])
     doubled = jnp.concatenate([by_chip, by_chip], axis=0)
     by_chip = lax.dynamic_slice_in_dim(doubled, me, n_col, 0)
-    doubled = jnp.concatenate([by_chip, by_chip], axis=1)
-    return lax.dynamic_slice_in_dim(doubled, rep, n_rep, 1)
+    parts = []
+    for step in range(n_rep):
+        part = lax.dynamic_index_in_dim(by_chip, (rep + step) % n_rep, 1, keepdims=False)
+        parts.append(part.reshape((-1,) + moved.shape[2:]))
+    return parts
 
 
 def body(b_aux, occ_energies, vir_energies, owners, *, shards, n_rep, n_aux, by_partials):
@@ -106,23 +119,23 @@
     rows = local.shape[0]
     ids = jnp.stack([lax.axis_index("col"), lax.axis_index("rep")]).astype(jnp.int32)
     if n_col <= LINE_MAX and not by_partials:
-        owned_all = gather_relative(owned, n_col, n_rep).reshape(shards * rows, owned.shape[1])
+        owned_parts = gather_relative(owned, n_col, n_rep)
         order = lambda moved: relative_order(moved, n_col, n_rep)
         block = rows
-        place = lambda i, ids: ((ids[0] + i // n_rep) % n_col) * n_rep + (ids[1] + i % n_rep) % n_rep
+        place = lambda i, ids: (ids[0] + i) % n_col
     else:
-        owned_all = lax.all_gather(owned, COLS, axis=0, tiled=True)
+        owned_parts = [lax.all_gather(owned, COLS, axis=0, tiled=True)]
         order = None
-        block = owned_all.shape[0]
+        block = owned_parts[0].shape[0]
         place = lambda i, ids: i
     if by_partials:
         coupling = coupling_by_partials(local, owned, shards, width)
     else:
-        coupling = coupling_by_columns(local, owned_all, shards, width, order)
+        coupling = coupling_by_columns(local, owned_parts, shards, width, order)
     coupling = exchange_sum(coupling, "aux", n_aux)
     denominator = energy_mine[:, None] + owner_energy[None, :]
     amplitude = (os_scale * coupling / denominator).astype(jnp.bfloat16)
-    return gamma_rows_last(amplitude, owned_all, ids, block, place)
+    return gamma_rows_last(amplitude, owned_parts, ids, block, place)
 
 
 def solution(mesh):

time: 162 us -> 171 us (1.056)
  the two profiles are of different devices: /device:TPU:8 before, /device:TPU:10 now
where the time goes in v15:
time: 171 us
  waiting for transfers between devices  112 us (65%)
  local copies, waits for them, and re-layouts  22.5 us (13%)
  other arithmetic  12.8 us (7%)
  starting transfers between devices  10.5 us (6%)
  Pallas kernels  7.29 us (4%)
  matrix products  4.03 us (2%)
  between operations  1.98 us (1%)
    ppermute x3, waiting for transfers between devices, gather_relative(): lax.ppermute(owned, 'col', [(i, (i - step) % n_col) for i in range(n_col)])  98.1 us
    ppermute x1, waiting for transfers between devices, exchange_sum(): lax.ppermute(value, axis, [(i, (i + step) % size) for i in range(size)])  13.4 us
    pallas_call x1, Pallas kernels, gamma_rows_last(): pl.pallas_call(gamma_kernel, out_shape=jax.ShapeDtypeStruct((width, 1, ro...  7.29 us
    concatenate x1, other arithmetic, gather_relative(): mine = jnp.concatenate(mine, axis=0)  6.33 us
    all_to_all x1, starting transfers between devices, coupling_by_columns(): lax.all_to_all(blocked, COLS, split_axis=0, concat_axis=0, tiled=True)  5.45 us
    unnamed x1, other arithmetic  4.51 us
    ppermute x3, starting transfers between devices, gather_relative(): lax.ppermute(owned, 'col', [(i, (i - step) % n_col) for i in range(n_col)])  4.44 us
    ppermute x1, local copies, waits for them, and re-layouts, gather_relative(): lax.ppermute(mine, 'rep', [(i, (i - step) % n_rep) for i in range(n_rep)])  4.35 us
  transfers between devices with their start and end apart: 6, of which 4 were waited for; matrix products, arithmetic and copies ran while one was open for 18% of the time, Pallas kernels for 0%

profile of v15, /device:TPU:10, one launch (start us, length us, event | category | flops | bytes accessed | tf_op | source)
XLA Modules:
  0.0 170.7 jit_solution(18348159210728554103)
XLA Ops:
  0.0 4.1 %reshape_squeeze.3 = bf16[512,8,300]{0,2,1:T(8,128)(2,1)} reshape(bf16[1,512,2400]{1,2,0:T(8,128)(2,1)} %param.4) | data formatting | bytes 4915200 | tf_op jit(solution)/shard_map/reshape;squeeze | solution.py:35
  4.1 5.5 %all-to-all-start = ((bf16[8,512,300]{1,2,0:T(8,128)(2,1)}), bf16[8,512,300]{1,2,0:T(8,128)(2,1)}, u32[]{:S(2)}, u32[]{:S(2)}) async-start(bf16[8,512,300]{1,2,0:T(8,128)(2,1)} %bitcast.2), calls=%async_computation | async-start | bytes 4980736 | tf_op jit(solution)/shard_map/all_to_all | solution.py:36
  9.5 0.6 fusion.5
  11.4 1.2 constant_dynamic-slice_fusion.1
  12.6 0.2 copy.13
  13.0 0.2 pad_maximum_fusion.1
  13.3 0.2 copy.15
  13.5 1.5 collective-permute-start.2
  15.1 1.0 collective-permute-start.1
  16.0 1.9 %collective-permute-start = (bf16[512,600]{0,1:T(8,128)(2,1)S(1)}, bf16[512,600]{0,1:T(8,128)(2,1)S(1)}, u32[]{:S(2)}, u32[]{:S(2)}) collective-permute-start(bf16[512,600]{0,1:T(8,128)(2,1)S(1)} %copy.15), channel_id=1, source_target_pairs={{0,12},{4,0},{8,4},{12,8},{1,13},{5,1},{9,5},{13,9},{2,14},{6,2},{... | collective-permute-start | bytes 1843208 | tf_op jit(solution)/shard_map/ppermute | solution.py:90
  18.0 85.0 %collective-permute-done.2 = bf16[512,600]{0,1:T(8,128)(2,1)S(1)} collective-permute-done((bf16[512,600]{0,1:T(8,128)(2,1)S(1)}, bf16[512,600]{0,1:T(8,128)(2,1)S(1)}, u32[]{:S(2)}, u32[]{:S(2)}) %collective-permute-start.2) | collective-permute-done | bytes 614432 | tf_op jit(solution)/shard_map/ppermute | solution.py:90
  103.0 1.1 copy.20
  104.1 12.0 %collective-permute-done.1 = bf16[512,600]{0,1:T(8,128)(2,1)S(1)} collective-permute-done((bf16[512,600]{0,1:T(8,128)(2,1)S(1)}, bf16[512,600]{0,1:T(8,128)(2,1)S(1)}, u32[]{:S(2)}, u32[]{:S(2)}) %collective-permute-start.1) | collective-permute-done | bytes 614432 | tf_op jit(solution)/shard_map/ppermute | solution.py:90
  116.1 1.1 copy.19
  117.2 1.0 collective-permute-done
  118.3 1.1 copy.18
  119.4 6.3 %pad_maximum_fusion.refs_0_ = bf16[2048,600]{1,0:T(8,128)(2,1)S(1)} fusion(bf16[512,600]{1,0:T(8,128)(2,1)} %copy.20, bf16[512,600]{1,0:T(8,128)(2,1)} %copy.19, bf16[512,600]{1,0:T(8,128)(2,1)} %copy.18, bf16[512,300]{1,0:T(8,128)(2,1)S(1)} %bitcast.36, bf16[512,300]{1,0:T(8,128)(2,1)S(1)} %bitcast.34), kind=kLoop, calls=%fused_computation.4 | loop fusion | flops 12288000 | bytes 4915200 | tf_op jit(solution)/shard_map/concatenate | solution.py:91
  125.7 3.0 %copy.21 = bf16[2048,600]{0,1:T(8,128)(2,1)} copy(bf16[2048,600]{1,0:T(8,128)(2,1)S(1)} %pad_maximum_fusion.refs_0_) | data formatting | bytes 4915200 | tf_op jit(solution)/shard_map/concatenate | solution.py:91
  128.8 3.6 %copy.11 = bf16[4,2,512,300]{2,0,3,1:T(4,128)(2,1)S(1)} copy(bf16[4,2,512,300]{2,3,1,0:T(8,128)(2,1)} %bitcast.3) | data formatting | bytes 4915200 | tf_op jit(solution)/shard_map/reshape | solution.py:101
  132.4 4.5 %fusion.3 = (bf16[300,4,512]{2,1,0:T(4,128)(2,1)S(1)}, bf16[300,4,512]{2,1,0:T(4,128)(2,1)S(1)}) fusion(s32[]{:T(128)S(6)} %select_n.39, s32[]{:T(128)S(6)} %select_n.42, bf16[4,2,512,300]{2,0,3,1:T(4,128)(2,1)S(1)} %copy.11, s32[]{:T(128)S(6)} %select_n.47), kind=kLoop, calls=%fused_computation.9 | loop fusion | flops 4915200 | bytes 4915212
  136.9 0.5 pad.13
  137.4 0.3 copy.23
  137.7 0.5 pad.14
  138.2 0.3 copy.24
  138.5 2.9 %fusion.6 = f32[300,600]{1,0:T(8,128)S(1)} fusion(bf16[2048,300]{0,1:T(8,128)(2,1)S(1)} %bitcast.38, bf16[2048,600]{0,1:T(8,128)(2,1)} %collective-permute-done.3), kind=kOutput, calls=%fused_computation.19 | convolution fusion | flops 737280000 | bytes 4406400 | tf_op jit(solution)/shard_map/dot_general | solution.py:40
  141.4 1.2 convolution_add_fusion
  142.6 0.6 collective-permute-start.4
  143.8 0.7 pad_add_fusion.ids_ref
  144.6 4.3 %copy.22.refs_1_ = bf16[2048,600]{1,0:T(8,128)(2,1)} copy(bf16[2048,600]{0,1:T(8,128)(2,1)} %collective-permute-done.3) | data formatting | bytes 4915200 | tf_op jit(solution)/shard_map/ppermute | solution.py:94
  149.0 13.4 %collective-permute-done.4 = f32[300,600]{1,0:T(8,128)S(1)} collective-permute-done((f32[300,600]{1,0:T(8,128)S(1)}, f32[300,600]{1,0:T(8,128)S(1)}, u32[]{:S(2)}, u32[]{:S(2)}) %collective-permute-start.4) | collective-permute-done | bytes 720032 | tf_op jit(solution)/shard_map/ppermute | solution.py:50
  162.4 1.0 divide_convert_fusion.amp_ref
  163.4 7.3 %shard_map.46 = f32[300,1,4096]{2,1,0:T(1,128)} custom-call(s32[2]{0:T(128)} %pad_add_fusion.ids_ref, bf16[300,600]{1,0:T(8,128)(2,1)} %divide_convert_fusion.amp_ref, bf16[2048,600]{1,0:T(8,128)(2,1)} %copy-done, bf16[2048,600]{1,0:T(8,128)(2,1)} %copy.22.refs_1_), custom_call_target="tpu_custom_call" | custom-call | tf_op jit(solution)/shard_map/pallas_call | solution.py:71
  (13 shorter events, 0.4 us)
Async XLA Ops:
  4.1 5.5 %copy-start.2 = (s32[2]{0:T(128)S(1)}, s32[2]{0:T(128)}, u32[]{:S(2)}) copy-start(s32[2]{0:T(128)} %param.7) | copy-start | bytes 28
  4.1 124.7 %all-to-all-start = ((bf16[8,512,300]{1,2,0:T(8,128)(2,1)}), bf16[8,512,300]{1,2,0:T(8,128)(2,1)}, u32[]{:S(2)}, u32[]{:S(2)}) async-start(bf16[8,512,300]{1,2,0:T(8,128)(2,1)} %bitcast.2), calls=%async_computation | async-start | bytes 4980736 | tf_op jit(solution)/shard_map/all_to_all | solution.py:36
  13.5 89.5 %collective-permute-start.2 = (bf16[512,600]{0,1:T(8,128)(2,1)S(1)}, bf16[512,600]{0,1:T(8,128)(2,1)S(1)}, u32[]{:S(2)}, u32[]{:S(2)}) collective-permute-start(bf16[512,600]{0,1:T(8,128)(2,1)S(1)} %copy.15), channel_id=1, source_target_pairs={{0,4},{4,8},{8,12},{12,0},{1,5},{5,9},{9,13},{13,1},{2,6},{6,10},{... | collective-permute-start | bytes 1843208 | tf_op jit(solution)/shard_map/ppermute | solution.py:90
  15.1 101.1 %collective-permute-start.1 = (bf16[512,600]{0,1:T(8,128)(2,1)S(1)}, bf16[512,600]{0,1:T(8,128)(2,1)S(1)}, u32[]{:S(2)}, u32[]{:S(2)}) collective-permute-start(bf16[512,600]{0,1:T(8,128)(2,1)S(1)} %copy.15), channel_id=1, source_target_pairs={{0,8},{4,12},{8,0},{12,4},{1,9},{5,13},{9,1},{13,5},{2,10},{6,14},... | collective-permute-start | bytes 1843208 | tf_op jit(solution)/shard_map/ppermute | solution.py:90
  16.0 102.2 %collective-permute-start = (bf16[512,600]{0,1:T(8,128)(2,1)S(1)}, bf16[512,600]{0,1:T(8,128)(2,1)S(1)}, u32[]{:S(2)}, u32[]{:S(2)}) collective-permute-start(bf16[512,600]{0,1:T(8,128)(2,1)S(1)} %copy.15), channel_id=1, source_target_pairs={{0,12},{4,0},{8,4},{12,8},{1,13},{5,1},{9,5},{13,9},{2,14},{6,2},{... | collective-permute-start | bytes 1843208 | tf_op jit(solution)/shard_map/ppermute | solution.py:90
  125.7 15.7 %copy-start = (bf16[2048,600]{1,0:T(8,128)(2,1)}, bf16[2048,600]{1,0:T(8,128)(2,1)S(1)}, u32[]{:S(2)}) copy-start(bf16[2048,600]{1,0:T(8,128)(2,1)S(1)} %pad_maximum_fusion.refs_0_) | copy-start | bytes 7372804
  128.7 9.7 %collective-permute-start.3 = (bf16[2048,600]{0,1:T(8,128)(2,1)}, bf16[2048,600]{0,1:T(8,128)(2,1)}, u32[]{:S(2)}, u32[]{:S(2)}) collective-permute-start(bf16[2048,600]{0,1:T(8,128)(2,1)} %copy.21), channel_id=1, source_target_pairs={{0,1},{1,0},{2,3},{3,2},{4,5},{5,4},{6,7},{7,6},{8,9},{9,8},{10,11... | collective-permute-start | bytes 7372808 | tf_op jit(solution)/shard_map/ppermute | solution.py:94
  141.4 3.1 %copy-start.1 = (f32[2400]{0:T(1024)S(1)}, f32[2400]{0:T(1024)}, u32[]{:S(2)}) copy-start(f32[2400]{0:T(1024)} %param.6) | copy-start | bytes 28804
  142.6 19.8 %collective-permute-start.4 = (f32[300,600]{1,0:T(8,128)S(1)}, f32[300,600]{1,0:T(8,128)S(1)}, u32[]{:S(2)}, u32[]{:S(2)}) collective-permute-start(f32[300,600]{1,0:T(8,128)S(1)} %convolution_add_fusion), channel_id=1, source_target_pairs={{0,2},{2,0},{1,3},{3,1},{4,6},{6,4},{5,7},{7,5},{8,10},{10,8},{9,1... | collective-permute-start | bytes 2160008 | tf_op jit(solution)/shard_map/ppermute | solution.py:50

commit v16 on v14

--- a/solution.py
+++ b/solution.py
@@ -3,6 +3,7 @@
 from jax import lax
 from jax.experimental import pallas as pl
 from jax.experimental.pallas import tpu as pltpu
+from jax.experimental.layout import Layout, with_layout_constraint
 from jax.sharding import PartitionSpec as P
 
 os_scale = 1.3
@@ -82,7 +83,8 @@
     blocks = [mine]
     for step in range(1, n_rep):
         blocks.append(lax.ppermute(mine, "rep", [(i, (i - step) % n_rep) for i in range(n_rep)]))
-    return jnp.stack(blocks, axis=1)
+    stacked = jnp.stack(blocks, axis=1)
+    return with_layout_constraint(stacked, Layout(tuple(range(stacked.ndim))))
 
 
 def relative_order(moved, n_col, n_rep):

time: 162 us -> 171 us (1.056)
  the two profiles are of different devices: /device:TPU:8 before, /device:TPU:26 now
where the time goes in v16:
time: 171 us
  waiting for transfers between devices  116 us (68%)
  local copies, waits for them, and re-layouts  17.8 us (10%)
  other arithmetic  13.8 us (8%)
  Pallas kernels  9.32 us (5%)
  starting transfers between devices  8.53 us (5%)
  matrix products  2.82 us (2%)
  between operations  2.05 us (1%)
    ppermute x3, waiting for transfers between devices, gather_relative(): lax.ppermute(owned, 'col', [(i, (i - step) % n_col) for i in range(n_col)])  98.6 us
    ppermute x1, waiting for transfers between devices, exchange_sum(): lax.ppermute(value, axis, [(i, (i + step) % size) for i in range(size)])  12.8 us
    pallas_call x1, Pallas kernels, gamma_rows_last(): pl.pallas_call(gamma_kernel, out_shape=jax.ShapeDtypeStruct((width, 1, ro...  9.32 us
    another operation x2, other arithmetic, gather_relative(): stacked = jnp.stack(blocks, axis=1)  7.75 us
    ppermute x3, local copies, waits for them, and re-layouts, gather_relative(): lax.ppermute(owned, 'col', [(i, (i - step) % n_col) for i in range(n_col)])  5.39 us
    all_to_all x1, starting transfers between devices, coupling_by_columns(): lax.all_to_all(blocked, COLS, split_axis=0, concat_axis=0, tiled=True)  5.23 us
    ppermute x1, waiting for transfers between devices, gather_relative(): lax.ppermute(mine, 'rep', [(i, (i - step) % n_rep) for i in range(n_rep)])  4.95 us
    another operation x1, local copies, waits for them, and re-layouts, coupling_by_columns(): blocked = local.reshape(rows, shards, width).transpose(1, 0, 2)  4.1 us
  transfers between devices with their start and end apart: 6, of which 4 were waited for; matrix products, arithmetic and copies ran while one was open for 13% of the time, Pallas kernels for 0%

profile of v16, /device:TPU:26, one launch (start us, length us, event | category | flops | bytes accessed | tf_op | source)
XLA Modules:
  0.0 170.6 jit_solution(1398889754182189292)
XLA Ops:
  0.0 4.1 %reshape_squeeze.3 = bf16[512,8,300]{0,2,1:T(8,128)(2,1)} reshape(bf16[1,512,2400]{1,2,0:T(8,128)(2,1)} %param.4) | data formatting | bytes 4915200 | tf_op jit(solution)/shard_map/reshape;squeeze | solution.py:36
  4.1 5.2 %all-to-all-start = ((bf16[8,512,300]{1,2,0:T(8,128)(2,1)}), bf16[8,512,300]{1,2,0:T(8,128)(2,1)}, u32[]{:S(2)}, u32[]{:S(2)}) async-start(bf16[8,512,300]{1,2,0:T(8,128)(2,1)} %bitcast.2), calls=%async_computation | async-start | bytes 4980736 | tf_op jit(solution)/shard_map/all_to_all | solution.py:37
  9.3 0.6 fusion.11
  11.3 1.2 constant_dynamic-slice_fusion.1
  12.5 0.2 copy.12
  12.7 0.2 copy.11
  12.9 0.2 pad_maximum_fusion.2
  13.2 0.2 copy.13
  13.4 0.1 collective-permute-start.2
  13.5 2.0 %collective-permute-start.1 = (bf16[512,600]{0,1:T(8,128)(2,1)S(1)}, bf16[512,600]{0,1:T(8,128)(2,1)}, u32[]{:S(2)}, u32[]{:S(2)}) collective-permute-start(bf16[512,600]{0,1:T(8,128)(2,1)S(1)} %copy.13), channel_id=1, source_target_pairs={{0,8},{4,12},{8,0},{12,4},{1,9},{5,13},{9,1},{13,5},{2,10},{6,14},... | collective-permute-start | bytes 1843208 | tf_op jit(solution)/shard_map/ppermute | solution.py:81
  15.5 0.6 collective-permute-start
  16.1 0.2 fusion.12
  16.3 47.6 %collective-permute-done.2 = bf16[512,600]{0,1:T(8,128)(2,1)} collective-permute-done((bf16[512,600]{0,1:T(8,128)(2,1)S(1)}, bf16[512,600]{0,1:T(8,128)(2,1)}, u32[]{:S(2)}, u32[]{:S(2)}) %collective-permute-start.2) | collective-permute-done | bytes 614432 | tf_op jit(solution)/shard_map/ppermute | solution.py:81
  63.9 2.2 %copy.18 = bf16[512,600]{1,0:T(8,128)(2,1)} copy(bf16[512,600]{0,1:T(8,128)(2,1)} %collective-permute-done.2) | data formatting | bytes 1228800 | tf_op jit(solution)/shard_map/ppermute | solution.py:81
  66.0 51.0 %collective-permute-done.1 = bf16[512,600]{0,1:T(8,128)(2,1)} collective-permute-done((bf16[512,600]{0,1:T(8,128)(2,1)S(1)}, bf16[512,600]{0,1:T(8,128)(2,1)}, u32[]{:S(2)}, u32[]{:S(2)}) %collective-permute-start.1) | collective-permute-done | bytes 614432 | tf_op jit(solution)/shard_map/ppermute | solution.py:81
  117.0 2.1 %copy.16 = bf16[512,600]{1,0:T(8,128)(2,1)} copy(bf16[512,600]{0,1:T(8,128)(2,1)} %collective-permute-done.1) | data formatting | bytes 1228800 | tf_op jit(solution)/shard_map/ppermute | solution.py:81
  119.2 1.1 copy.14
  120.3 2.9 %fusion.9 = (bf16[4,1,512,600]{3,2,1,0:T(8,128)(2,1)}, bf16[4,512,600]{2,1,0:T(8,128)(2,1)S(1)}) fusion(bf16[1,512,600]{2,1,0:T(8,128)(2,1)} %bitcast.33, bf16[1,512,600]{2,1,0:T(8,128)(2,1)} %bitcast.34, bf16[1,512,600]{2,1,0:T(8,128)(2,1)} %bitcast.35, bf16[1,512,600]{2,1,0:T(8,128)(2,1)S(1)} %fusion.12), kind=kLoop, calls=%fused_computation.19 | loop fusion | flops 3686400 | bytes 7372800 | tf_op jit(solution)/shard_map/stack | solution.py:86
  123.2 2.6 %copy.19 = bf16[4,512,600]{1,2,0:T(8,128)(2,1)} copy(bf16[4,512,600]{2,1,0:T(8,128)(2,1)S(1)} %get-tuple-element.6) | data formatting | bytes 4915200 | tf_op jit(solution)/shard_map/stack | solution.py:82
  125.8 0.1 collective-permute-start.3
  125.9 5.0 %collective-permute-done.3 = bf16[4,512,600]{1,2,0:T(8,128)(2,1)} collective-permute-done((bf16[4,512,600]{1,2,0:T(8,128)(2,1)}, bf16[4,512,600]{1,2,0:T(8,128)(2,1)}, u32[]{:S(2)}, u32[]{:S(2)}) %collective-permute-start.3) | collective-permute-done | bytes 2457632 | tf_op jit(solution)/shard_map/ppermute | solution.py:85
  130.8 3.1 %copy.20 = bf16[4,512,600]{2,1,0:T(8,128)(2,1)S(1)} copy(bf16[4,512,600]{1,2,0:T(8,128)(2,1)} %collective-permute-done.3) | data formatting | bytes 4915200 | tf_op jit(solution)/shard_map/ppermute | solution.py:85
  133.9 2.8 %fusion.3 = bf16[4,2,512,300]{2,3,1,0:T(8,128)(2,1)S(1)} fusion(s32[]{:T(128)S(6)} %select_n.17, bf16[4,2,512,300]{2,3,1,0:T(8,128)(2,1)} %bitcast.3), kind=kLoop, calls=%fused_computation.8 | loop fusion | flops 1228800 | bytes 4915204 | tf_op jit(solution)/shard_map/concatenate | solution.py:94
  136.7 2.8 %fusion.4 = f32[300,600]{1,0:T(8,128)S(1)} fusion(s32[]{:T(128)S(6)} %select_n.18, bf16[4,2,512,300]{2,3,1,0:T(8,128)(2,1)S(1)} %fusion.3, bf16[4,1,512,600]{3,2,1,0:T(8,128)(2,1)S(1)} %bitcast.27, bf16[4,1,512,600]{3,2,1,0:T(8,128)(2,1)S(1)} %copy-done), kind=kOutput, calls=%fused_computation.9 | convolution fusion | flops 1478246400 | bytes 8092804 | tf_op jit(solution)/shard_map/dot_general | solution.py:40
  139.5 0.6 collective-permute-start.4
  140.1 0.6 pad_add_fusion.ids_ref
  141.4 0.1 fusion.10
  141.5 0.1 pad_maximum_fusion.3
  141.6 4.8 %pad_maximum_fusion = bf16[4,2,512,600]{3,2,1,0:T(8,128)(2,1)} fusion(bf16[4,1,512,600]{3,2,1,0:T(8,128)(2,1)S(1)} %bitcast.28, bf16[4,1,512,600]{3,2,1,0:T(8,128)(2,1)} %get-tuple-element.5), kind=kLoop, calls=%fused_computation | loop fusion | flops 2457600 | bytes 9830400 | tf_op jit(solution)/shard_map/stack | solution.py:86
  146.4 12.8 %collective-permute-done.4 = f32[300,600]{1,0:T(8,128)} collective-permute-done((f32[300,600]{1,0:T(8,128)S(1)}, f32[300,600]{1,0:T(8,128)}, u32[]{:S(2)}, u32[]{:S(2)}) %collective-permute-start.4) | collective-permute-done | bytes 720032 | tf_op jit(solution)/shard_map/ppermute | solution.py:49
  159.1 2.1 %divide_convert_fusion.amp_ref = bf16[300,600]{1,0:T(8,128)(2,1)} fusion(f32[300,600]{1,0:T(8,128)S(1)} %fusion.4, f32[300,600]{1,0:T(8,128)} %collective-permute-done.4, f32[600]{0:T(1024)S(1)} %pad_maximum_fusion.3, f32[300]{0:T(512)S(1)} %get-tuple-element.9), kind=kLoop, calls=%fused_computation.10 | loop fusion | flops 900000 | bytes 1803600 | tf_op jit(solution)/shard_map/convert_element_type | solution.py:126
  161.2 9.3 %shard_map.46 = f32[300,1,4096]{2,1,0:T(1,128)} custom-call(s32[2]{0:T(128)} %pad_add_fusion.ids_ref, bf16[300,600]{1,0:T(8,128)(2,1)} %divide_convert_fusion.amp_ref, bf16[4096,600]{1,0:T(8,128)(2,1)} %bitcast.26), custom_call_target="tpu_custom_call" | custom-call | tf_op jit(solution)/shard_map/pallas_call | solution.py:62
  (9 shorter events, 0.0 us)
Async XLA Ops:
  4.1 5.2 %copy-start.2 = (s32[2]{0:T(128)S(1)}, s32[2]{0:T(128)}, u32[]{:S(2)}) copy-start(s32[2]{0:T(128)} %param.7) | copy-start | bytes 28
  4.1 129.8 %all-to-all-start = ((bf16[8,512,300]{1,2,0:T(8,128)(2,1)}), bf16[8,512,300]{1,2,0:T(8,128)(2,1)}, u32[]{:S(2)}, u32[]{:S(2)}) async-start(bf16[8,512,300]{1,2,0:T(8,128)(2,1)} %bitcast.2), calls=%async_computation | async-start | bytes 4980736 | tf_op jit(solution)/shard_map/all_to_all | solution.py:37
  13.4 50.4 %collective-permute-start.2 = (bf16[512,600]{0,1:T(8,128)(2,1)S(1)}, bf16[512,600]{0,1:T(8,128)(2,1)}, u32[]{:S(2)}, u32[]{:S(2)}) collective-permute-start(bf16[512,600]{0,1:T(8,128)(2,1)S(1)} %copy.13), channel_id=1, source_target_pairs={{0,4},{4,8},{8,12},{12,0},{1,5},{5,9},{9,13},{13,1},{2,6},{6,10},{... | collective-permute-start | bytes 1843208 | tf_op jit(solution)/shard_map/ppermute | solution.py:81
  13.5 103.5 %collective-permute-start.1 = (bf16[512,600]{0,1:T(8,128)(2,1)S(1)}, bf16[512,600]{0,1:T(8,128)(2,1)}, u32[]{:S(2)}, u32[]{:S(2)}) collective-permute-start(bf16[512,600]{0,1:T(8,128)(2,1)S(1)} %copy.13), channel_id=1, source_target_pairs={{0,8},{4,12},{8,0},{12,4},{1,9},{5,13},{9,1},{13,5},{2,10},{6,14},... | collective-permute-start | bytes 1843208 | tf_op jit(solution)/shard_map/ppermute | solution.py:81
  15.5 103.7 %collective-permute-start = (bf16[512,600]{0,1:T(8,128)(2,1)S(1)}, bf16[512,600]{0,1:T(8,128)(2,1)S(1)}, u32[]{:S(2)}, u32[]{:S(2)}) collective-permute-start(bf16[512,600]{0,1:T(8,128)(2,1)S(1)} %copy.13), channel_id=1, source_target_pairs={{0,12},{4,0},{8,4},{12,8},{1,13},{5,1},{9,5},{13,9},{2,14},{6,2},{... | collective-permute-start | bytes 1843208 | tf_op jit(solution)/shard_map/ppermute | solution.py:81
  125.8 5.0 %collective-permute-start.3 = (bf16[4,512,600]{1,2,0:T(8,128)(2,1)}, bf16[4,512,600]{1,2,0:T(8,128)(2,1)}, u32[]{:S(2)}, u32[]{:S(2)}) collective-permute-start(bf16[4,512,600]{1,2,0:T(8,128)(2,1)} %copy.19), channel_id=1, source_target_pairs={{0,1},{1,0},{2,3},{3,2},{4,5},{5,4},{6,7},{7,6},{8,9},{9,8},{10,11... | collective-permute-start | bytes 7372808 | tf_op jit(solution)/shard_map/ppermute | solution.py:85
  133.9 2.8 %copy-start = (bf16[4,1,512,600]{3,2,1,0:T(8,128)(2,1)S(1)}, bf16[4,1,512,600]{3,2,1,0:T(8,128)(2,1)}, u32[]{:S(2)}) copy-start(bf16[4,1,512,600]{3,2,1,0:T(8,128)(2,1)} %get-tuple-element.5) | copy-start | bytes 7372804
  136.7 4.7 %copy-start.1 = (f32[2400]{0:T(1024)S(1)}, f32[2400]{0:T(1024)}, u32[]{:S(2)}) copy-start(f32[2400]{0:T(1024)} %param.6) | copy-start | bytes 28804
  139.5 19.6 %collective-permute-start.4 = (f32[300,600]{1,0:T(8,128)S(1)}, f32[300,600]{1,0:T(8,128)}, u32[]{:S(2)}, u32[]{:S(2)}) collective-permute-start(f32[300,600]{1,0:T(8,128)S(1)} %fusion.4), channel_id=1, source_target_pairs={{0,2},{2,0},{1,3},{3,1},{4,6},{6,4},{5,7},{7,5},{8,10},{10,8},{9,1... | collective-permute-start | bytes 2160008 | tf_op jit(solution)/shard_map/ppermute | solution.py:49

commit v17 on v11

--- a/solution.py
+++ b/solution.py
@@ -1,3 +1,5 @@
+import functools
+
 import jax
 import jax.numpy as jnp
 from jax import lax
@@ -47,7 +49,7 @@
             preferred_element_type=jnp.float32,
         )
         pieces.append(exchange_sum(previous, "aux", n_aux))
-    return jnp.concatenate(pieces, axis=0)
+    return pieces
 
 
 def exchange_sum(value, axis, size):
@@ -63,16 +65,42 @@
     )
 
 
-def gamma_rows_last(amplitude, owned_all):
-    width = amplitude.shape[0]
+def gamma_tail_kernel(amp_ref, owned_ref, prev_ref, out_ref, held, sem, *, first):
+    held[:, 0, :] = lax.dot_general(
+        amp_ref[...], owned_ref[...], (((1,), (1,)), ((), ())), preferred_element_type=jnp.float32
+    )
+    copy = pltpu.make_async_copy(held, out_ref.at[pl.ds(first, held.shape[0])], sem)
+    copy.start()
+    copy.wait()
+
+
+def gamma_rows_last(amp_pieces, owned_all, width):
     rows = owned_all.shape[0]
+    head = amp_pieces[0].shape[0]
+    depth = owned_all.shape[1]
     out = pl.pallas_call(
         gamma_kernel,
         out_shape=jax.ShapeDtypeStruct((width, 1, rows), jnp.float32),
-        in_specs=[pl.BlockSpec(memory_space=pltpu.VMEM)] * 2,
-        out_specs=pl.BlockSpec(memory_space=pltpu.VMEM),
+        grid=(1,),
+        in_specs=[
+            pl.BlockSpec((head, depth), lambda i: (0, 0)),
+            pl.BlockSpec((rows, depth), lambda i: (0, 0)),
+        ],
+        out_specs=pl.BlockSpec((head, 1, rows), lambda i: (0, 0, 0)),
         compiler_params=pltpu.CompilerParams(vmem_limit_bytes=48 * 2**20),
-    )(amplitude, owned_all)
+    )(amp_pieces[0], owned_all)
+    if len(amp_pieces) > 1:
+        tail = amp_pieces[1].shape[0]
+        out = pl.pallas_call(
+            functools.partial(gamma_tail_kernel, first=head),
+            out_shape=jax.ShapeDtypeStruct((width, 1, rows), jnp.float32),
+            in_specs=[pl.BlockSpec(memory_space=pltpu.VMEM)] * 2
+            + [pl.BlockSpec(memory_space=pl.ANY)],
+            out_specs=pl.BlockSpec(memory_space=pl.ANY),
+            scratch_shapes=[pltpu.VMEM((tail, 1, rows), jnp.float32), pltpu.SemaphoreType.DMA],
+            input_output_aliases={2: 0},
+            compiler_params=pltpu.CompilerParams(vmem_limit_bytes=48 * 2**20),
+        )(amp_pieces[1], owned_all, out)
     return out.transpose(1, 2, 0)
 
 
@@ -86,12 +114,17 @@
     owned_all = lax.all_gather(owned, COLS, axis=0, tiled=True)
     if by_partials:
         coupling = coupling_by_partials(local, owned, shards, width)
-        coupling = exchange_sum(coupling, "aux", n_aux)
+        pieces = [exchange_sum(coupling, "aux", n_aux)]
     else:
-        coupling = coupling_by_columns(local, owned_all, shards, width, n_aux)
-    denominator = energy_mine[:, None] + owner_energy[None, :]
-    amplitude = (os_scale * coupling / denominator).astype(jnp.bfloat16)
-    return gamma_rows_last(amplitude, owned_all)
+        pieces = coupling_by_columns(local, owned_all, shards, width, n_aux)
+    amp_pieces = []
+    first = 0
+    for piece in pieces:
+        last = first + piece.shape[0]
+        denominator = energy_mine[first:last, None] + owner_energy[None, :]
+        amp_pieces.append((os_scale * piece / denominator).astype(jnp.bfloat16))
+        first = last
+    return gamma_rows_last(amp_pieces, owned_all, width)
 
 
 def solution(mesh):

time: 161 us -> 161 us (level)
  local copies, waits for them, and re-layouts: 14.1 us -> 11.7 us
  Pallas kernels: 4.98 us -> 6.99 us
    ppermute x2, waiting for transfers between devices: 3 us -> 14.4 us  [exchange_sum(): lax.ppermute(value, axis, [(i, (i + step) % size) for i in range(size)])]
    all_to_all x2, waiting for transfers between devices: 100 us -> 89.8 us  [coupling_by_columns(): moved = lax.all_to_all(chunk, COLS, split_axis=0, concat_axis=0, tiled=True)]
    pallas_call x0 -> x1, Pallas kernels: none -> 2.61 us  [gamma_rows_last(): pl.pallas_call(functools.partial(gamma_tail_kernel, first=head), out_shap...]
    unnamed x6, local copies, waits for them, and re-layouts: 2.64 us -> 0.16 us
  transfers between devices with their start and end apart: 5 -> 5, of which waited for: 3 -> 2; matrix products, arithmetic and copies ran while one was open for 8% -> 5% of each run, Pallas kernels for 0% -> 3%
where the time goes in v17:
time: 161 us
  waiting for transfers between devices  104 us (65%)
  between operations  15.4 us (10%)
  starting transfers between devices  12.9 us (8%)
  local copies, waits for them, and re-layouts  11.7 us (7%)
  matrix products  7.87 us (5%)
  Pallas kernels  6.99 us (4%)
    all_to_all x2, waiting for transfers between devices, coupling_by_columns(): moved = lax.all_to_all(chunk, COLS, split_axis=0, concat_axis=0, tiled=True)  89.8 us
    ppermute x2, waiting for transfers between devices, exchange_sum(): lax.ppermute(value, axis, [(i, (i + step) % size) for i in range(size)])  14.4 us
    all_to_all x2, starting transfers between devices, coupling_by_columns(): moved = lax.all_to_all(chunk, COLS, split_axis=0, concat_axis=0, tiled=True)  9.79 us
    dot_general x2, matrix products, coupling_by_columns(): lax.dot_general(moved.reshape(shards * rows, last - first), owned_all, ((...  7.87 us
    pallas_call x1, Pallas kernels, gamma_rows_last(): pl.pallas_call(gamma_kernel, out_shape=jax.ShapeDtypeStruct((width, 1, ro...  4.38 us
  transfers between devices with their start and end apart: 5, of which 2 were waited for; matrix products, arithmetic and copies ran while one was open for 5% of the time, Pallas kernels for 3%

profile of v17, /device:TPU:0, one launch (start us, length us, event | category | flops | bytes accessed | tf_op | source)
XLA Modules:
  0.0 160.6 jit_solution(1916904695098846455)
XLA Ops:
  6.5 1.3 fusion.1
  9.1 1.2 constant_dynamic-slice_fusion.1
  10.3 0.2 copy.14
  10.5 0.2 copy.15
  10.7 1.1 pad_maximum_fusion
  11.8 0.0 all-gather.2.cloned.1.call-update
  11.8 2.6 %reshape_squeeze.3 = bf16[512,8,300]{0,2,1:T(8,128)(2,1)S(1)} reshape(bf16[1,512,2400]{1,2,0:T(8,128)(2,1)} %param.4) | data formatting | bytes 4915200 | tf_op jit(solution)/shard_map/reshape;squeeze | solution.py:37
  14.5 1.5 slice.27
  16.0 6.3 %all-to-all-start = ((bf16[8,512,256]{1,2,0:T(8,128)(2,1)}), bf16[8,512,256]{1,2,0:T(8,128)(2,1)}, u32[]{:S(2)}, u32[]{:S(2)}) async-start(bf16[8,512,256]{1,2,0:T(8,128)(2,1)} %slice.27), calls=%async_computation | async-start | bytes 4194304 | tf_op jit(solution)/shard_map/all_to_all | solution.py:46
  22.3 0.8 slice.26
  23.8 89.8 %all-to-all-done = bf16[8,512,256]{1,2,0:T(8,128)(2,1)} async-done(((bf16[8,512,256]{1,2,0:T(8,128)(2,1)}), bf16[8,512,256]{1,2,0:T(8,128)(2,1)}, u32[]{:S(2)}, u32[]{:S(2)}) %all-to-all-start) | async-done | bytes 2097184 | tf_op jit(solution)/shard_map/all_to_all | solution.py:46
  113.6 2.8 %copy.16 = bf16[8,512,256]{2,1,0:T(8,128)(2,1)S(1)} copy(bf16[8,512,256]{1,2,0:T(8,128)(2,1)} %all-to-all-done) | data formatting | bytes 4194304 | tf_op jit(solution)/shard_map/all_to_all | solution.py:46
  116.5 0.0 all-gather.2.cloned.1.call-done.owned_ref
  116.5 0.0 copy-start.1
  116.5 4.3 %convolution_bitcast_fusion = f32[256,600]{1,0:T(8,128)S(1)} fusion(bf16[4096,600]{1,0:T(8,128)(2,1)} %all-gather.2.cloned.1.call-done.owned_ref, bf16[4096,256]{1,0:T(8,128)(2,1)S(1)} %bitcast.29), kind=kOutput, calls=%fused_computation | convolution fusion | flops 1258291200 | bytes 7626752 | tf_op jit(solution)/shard_map/dot_general | solution.py:47
  120.8 0.2 copy.19
  121.1 3.5 %all-to-all-start.1 = ((bf16[8,512,44]{1,2,0:T(8,128)(2,1)}), bf16[8,512,44]{1,2,0:T(8,128)(2,1)S(1)}, u32[]{:S(2)}, u32[]{:S(2)}) async-start(bf16[8,512,44]{1,2,0:T(8,128)(2,1)} %slice.26), calls=%async_computation.1 | async-start | bytes 786432 | tf_op jit(solution)/shard_map/all_to_all | solution.py:46
  124.5 1.6 collective-permute-start.1
  126.1 0.1 fusion
  126.2 0.1 pad_maximum_fusion.1
  126.3 14.4 %collective-permute-done.1 = f32[256,600]{0,1:T(8,128)S(1)} collective-permute-done((f32[256,600]{0,1:T(8,128)S(1)}, f32[256,600]{0,1:T(8,128)S(1)}, u32[]{:S(2)}, u32[]{:S(2)}) %collective-permute-start.1) | collective-permute-done | bytes 614432 | tf_op jit(solution)/shard_map/ppermute | solution.py:58
  140.7 0.2 copy.20
  140.9 0.0 all-to-all-done.1
  141.0 0.2 copy.24
  141.2 0.1 copy.22
  141.3 3.5 %fusion.2 = f32[44,600]{1,0:T(8,128)S(1)} fusion(bf16[4096,44]{0,1:T(8,128)(2,1)S(1)} %bitcast.31, bf16[4096,600]{1,0:T(8,128)(2,1)} %all-gather.2.cloned.1.call-done.owned_ref), kind=kOutput, calls=%fused_computation.12 | convolution fusion | flops 216268800 | bytes 5381248 | tf_op jit(solution)/shard_map/dot_general | solution.py:47
  144.9 1.6 collective-permute-start
  146.4 0.2 divide_convert_fusion.amp_ref
  146.7 4.4 %shard_map.46.prev_ref = f32[300,1,4096]{2,1,0:T(1,128)} custom-call(bf16[256,600]{1,0:T(8,128)(2,1)S(1)} %divide_convert_fusion.amp_ref, bf16[4096,600]{1,0:T(8,128)(2,1)S(1)} %copy-done), custom_call_target="tpu_custom_call" | custom-call | tf_op jit(solution)/shard_map/pallas_call | solution.py:81
  151.1 0.0 collective-permute-done
  151.1 0.1 divide_convert_fusion.1.amp_ref
  151.2 2.6 %shard_map.47 = f32[300,1,4096]{2,1,0:T(1,128)} custom-call(bf16[44,600]{1,0:T(8,128)(2,1)S(1)} %divide_convert_fusion.1.amp_ref, bf16[4096,600]{1,0:T(8,128)(2,1)S(1)} %copy-done, f32[300,1,4096]{2,1,0:T(1,128)} %shard_map.46.prev_ref), custom_call_target="tpu_custom_call", output_to_operand_aliasing={{}: (2, {})} | custom-call | tf_op jit(solution)/shard_map/pallas_call | solution.py:94
  (9 shorter events, 0.0 us)
Async XLA Ops:
  6.5 110.0 %all-gather.2.cloned.1.call-start = ((), (), s32[]{:S(2)}) async-start(), calls=%async_computation.2 | async-start | bytes 5898240 | tf_op jit(solution)/shard_map/all_gather | solution.py:114
  16.0 97.6 %all-to-all-start = ((bf16[8,512,256]{1,2,0:T(8,128)(2,1)}), bf16[8,512,256]{1,2,0:T(8,128)(2,1)}, u32[]{:S(2)}, u32[]{:S(2)}) async-start(bf16[8,512,256]{1,2,0:T(8,128)(2,1)} %slice.27), calls=%async_computation | async-start | bytes 4194304 | tf_op jit(solution)/shard_map/all_to_all | solution.py:46
  116.5 9.6 %copy-start.1 = (f32[2400]{0:T(1024)S(1)}, f32[2400]{0:T(1024)}, u32[]{:S(2)}) copy-start(f32[2400]{0:T(1024)} %param.6) | copy-start | bytes 28804
  121.1 19.9 %all-to-all-start.1 = ((bf16[8,512,44]{1,2,0:T(8,128)(2,1)}), bf16[8,512,44]{1,2,0:T(8,128)(2,1)S(1)}, u32[]{:S(2)}, u32[]{:S(2)}) async-start(bf16[8,512,44]{1,2,0:T(8,128)(2,1)} %slice.26), calls=%async_computation.1 | async-start | bytes 786432 | tf_op jit(solution)/shard_map/all_to_all | solution.py:46
  124.5 16.2 %collective-permute-start.1 = (f32[256,600]{0,1:T(8,128)S(1)}, f32[256,600]{0,1:T(8,128)S(1)}, u32[]{:S(2)}, u32[]{:S(2)}) collective-permute-start(f32[256,600]{0,1:T(8,128)S(1)} %copy.19), channel_id=1, source_target_pairs={{0,2},{2,0},{1,3},{3,1},{4,6},{6,4},{5,7},{7,5},{8,10},{10,8},{9,1... | collective-permute-start | bytes 1843208 | tf_op jit(solution)/shard_map/ppermute | solution.py:58
  141.3 5.3 %copy-start = (bf16[4096,600]{1,0:T(8,128)(2,1)S(1)}, bf16[4096,600]{1,0:T(8,128)(2,1)}, u32[]{:S(2)}) copy-start(bf16[4096,600]{1,0:T(8,128)(2,1)} %all-gather.2.cloned.1.call-done.owned_ref) | copy-start | bytes 14745604
  144.9 6.2 %collective-permute-start = (f32[44,600]{1,0:T(8,128)S(1)}, f32[44,600]{1,0:T(8,128)S(1)}, u32[]{:S(2)}, u32[]{:S(2)}) collective-permute-start(f32[44,600]{1,0:T(8,128)S(1)} %fusion.2), channel_id=1, source_target_pairs={{0,2},{2,0},{1,3},{3,1},{4,6},{6,4},{5,7},{7,5},{8,10},{10,8},{9,1... | collective-permute-start | bytes 316808 | tf_op jit(solution)/shard_map/ppermute | solution.py:58
Sparse Core Ops, SparseCore 0:
  12.0 101.8 all-gather.1

commit v18 on v12

--- a/solution.py
+++ b/solution.py
@@ -9,7 +9,7 @@
 COLS = ("col", "rep")
 PARTIAL_BYTES_MAX = 0
 LANES = 128
-ROW_BLOCK = 1024
+ROW_BLOCK = 2048
 
 
 def owner_columns(local, col_energy, owners, width):

time: 161 us -> 160 us (level)
  no operation moved by 1% of the time
where the time goes in v18:
time: 160 us; the launch traced here: 159 us
  waiting for transfers between devices  103 us (64%)
  between operations  15.5 us (10%)
  starting transfers between devices  12.9 us (8%)
  local copies, waits for them, and re-layouts  11.7 us (7%)
  matrix products  7.73 us (5%)
  Pallas kernels  5.95 us (4%)
  other arithmetic  2.23 us (1%)
    all_to_all x2, waiting for transfers between devices, coupling_by_columns(): moved = lax.all_to_all(chunk, COLS, split_axis=0, concat_axis=0, tiled=True)  100 us
    all_to_all x2, starting transfers between devices, coupling_by_columns(): moved = lax.all_to_all(chunk, COLS, split_axis=0, concat_axis=0, tiled=True)  9.79 us
    dot_general x2, matrix products, coupling_by_columns(): lax.dot_general(moved.reshape(shards * rows, last - first), owned_all, ((...  7.73 us
    pallas_call x1, Pallas kernels, gamma_rows_last(): pl.pallas_call(gamma_kernel, out_shape=jax.ShapeDtypeStruct((width, 1, ro...  5.95 us
  transfers between devices with their start and end apart: 5, of which 3 were waited for; matrix products, arithmetic and copies ran while one was open for 8% of the time, Pallas kernels for 0%

profile of v18, /device:TPU:0, one launch (start us, length us, event | category | flops | bytes accessed | tf_op | source)
XLA Modules:
  0.0 159.4 jit_solution(3728242315333995884)
XLA Ops:
  6.5 0.0 all-gather.2.cloned.1.call-start
  6.5 1.3 fusion.3
  9.2 1.2 constant_dynamic-slice_fusion.1
  10.4 0.2 copy.13
  10.6 0.2 copy.14
  10.8 1.1 pad_maximum_fusion
  11.9 0.0 all-gather.2.cloned.1.call-update
  11.9 2.6 %reshape_squeeze.3 = bf16[512,8,300]{0,2,1:T(8,128)(2,1)S(1)} reshape(bf16[1,512,2400]{1,2,0:T(8,128)(2,1)} %param.4) | data formatting | bytes 4915200 | tf_op jit(solution)/shard_map/reshape;squeeze | solution.py:36
  14.6 1.5 slice.16
  16.1 6.3 %all-to-all-start = ((bf16[8,512,256]{1,2,0:T(8,128)(2,1)}), bf16[8,512,256]{1,2,0:T(8,128)(2,1)}, u32[]{:S(2)}, u32[]{:S(2)}) async-start(bf16[8,512,256]{1,2,0:T(8,128)(2,1)} %slice.16), calls=%async_computation | async-start | bytes 4194304 | tf_op jit(solution)/shard_map/all_to_all | solution.py:45
  22.4 0.8 slice.17
  23.2 90.5 %all-to-all-done = bf16[8,512,256]{1,2,0:T(8,128)(2,1)} async-done(((bf16[8,512,256]{1,2,0:T(8,128)(2,1)}), bf16[8,512,256]{1,2,0:T(8,128)(2,1)}, u32[]{:S(2)}, u32[]{:S(2)}) %all-to-all-start) | async-done | bytes 2097184 | tf_op jit(solution)/shard_map/all_to_all | solution.py:45
  113.7 2.8 %copy.15 = bf16[8,512,256]{2,1,0:T(8,128)(2,1)S(1)} copy(bf16[8,512,256]{1,2,0:T(8,128)(2,1)} %all-to-all-done) | data formatting | bytes 4194304 | tf_op jit(solution)/shard_map/all_to_all | solution.py:45
  116.6 0.0 all-gather.2.cloned.1.call-done.owned_ref
  116.6 0.0 copy-start
  116.6 4.3 %convolution_bitcast_fusion = f32[256,600]{1,0:T(8,128)S(1)} fusion(bf16[4096,600]{1,0:T(8,128)(2,1)} %all-gather.2.cloned.1.call-done.owned_ref, bf16[4096,256]{1,0:T(8,128)(2,1)S(1)} %bitcast.26), kind=kOutput, calls=%fused_computation | convolution fusion | flops 1258291200 | bytes 7626752 | tf_op jit(solution)/shard_map/dot_general | solution.py:46
  120.9 3.5 %all-to-all-start.1 = ((bf16[8,512,44]{1,2,0:T(8,128)(2,1)}), bf16[8,512,44]{1,2,0:T(8,128)(2,1)S(1)}, u32[]{:S(2)}, u32[]{:S(2)}) async-start(bf16[8,512,44]{1,2,0:T(8,128)(2,1)} %slice.17), calls=%async_computation.1 | async-start | bytes 786432 | tf_op jit(solution)/shard_map/all_to_all | solution.py:45
  125.1 0.2 copy.17
  125.3 1.6 collective-permute-start
  126.9 0.1 fusion.2
  127.0 9.9 %all-to-all-done.1 = bf16[8,512,44]{1,2,0:T(8,128)(2,1)S(1)} async-done(((bf16[8,512,44]{1,2,0:T(8,128)(2,1)}), bf16[8,512,44]{1,2,0:T(8,128)(2,1)S(1)}, u32[]{:S(2)}, u32[]{:S(2)}) %all-to-all-start.1) | async-done | bytes 360480 | tf_op jit(solution)/shard_map/all_to_all | solution.py:45
  136.9 0.2 copy.23
  137.1 0.1 copy.21
  137.3 3.4 %fusion.4 = f32[44,600]{1,0:T(8,128)S(1)} fusion(bf16[4096,44]{0,1:T(8,128)(2,1)S(1)} %bitcast.28, bf16[4096,600]{1,0:T(8,128)(2,1)} %all-gather.2.cloned.1.call-done.owned_ref), kind=kOutput, calls=%fused_computation.12 | convolution fusion | flops 216268800 | bytes 5381248 | tf_op jit(solution)/shard_map/dot_general | solution.py:46
  140.7 1.6 collective-permute-start.1
  142.2 0.1 pad_maximum_fusion.1
  142.3 0.0 collective-permute-done
  142.3 0.2 copy.18
  142.5 0.1 add.35
  142.6 3.0 %collective-permute-done.1 = f32[44,600]{1,0:T(8,128)S(1)} collective-permute-done((f32[44,600]{1,0:T(8,128)S(1)}, f32[44,600]{1,0:T(8,128)S(1)}, u32[]{:S(2)}, u32[]{:S(2)}) %collective-permute-start.1) | collective-permute-done | bytes 105632 | tf_op jit(solution)/shard_map/ppermute | solution.py:57
  145.6 1.0 fusion.1.amp_ref
  146.6 5.9 %shard_map.46 = f32[300,1,4096]{2,1,0:T(1,128)} custom-call(bf16[300,600]{1,0:T(8,128)(2,1)} %fusion.1.amp_ref, bf16[4096,600]{1,0:T(8,128)(2,1)} %all-gather.2.cloned.1.call-done.owned_ref), custom_call_target="tpu_custom_call" | custom-call | tf_op jit(solution)/shard_map/pallas_call | solution.py:71
  (4 shorter events, 0.1 us)
Async XLA Ops:
  6.5 110.1 %all-gather.2.cloned.1.call-start = ((), (), s32[]{:S(2)}) async-start(), calls=%async_computation.2 | async-start | bytes 5898240 | tf_op jit(solution)/shard_map/all_gather | solution.py:91
  16.1 97.6 %all-to-all-start = ((bf16[8,512,256]{1,2,0:T(8,128)(2,1)}), bf16[8,512,256]{1,2,0:T(8,128)(2,1)}, u32[]{:S(2)}, u32[]{:S(2)}) async-start(bf16[8,512,256]{1,2,0:T(8,128)(2,1)} %slice.16), calls=%async_computation | async-start | bytes 4194304 | tf_op jit(solution)/shard_map/all_to_all | solution.py:45
  116.6 8.5 %copy-start = (f32[2400]{0:T(1024)S(1)}, f32[2400]{0:T(1024)}, u32[]{:S(2)}) copy-start(f32[2400]{0:T(1024)} %param.6) | copy-start | bytes 28804
  120.9 15.9 %all-to-all-start.1 = ((bf16[8,512,44]{1,2,0:T(8,128)(2,1)}), bf16[8,512,44]{1,2,0:T(8,128)(2,1)S(1)}, u32[]{:S(2)}, u32[]{:S(2)}) async-start(bf16[8,512,44]{1,2,0:T(8,128)(2,1)} %slice.17), calls=%async_computation.1 | async-start | bytes 786432 | tf_op jit(solution)/shard_map/all_to_all | solution.py:45
  125.3 17.0 %collective-permute-start = (f32[256,600]{0,1:T(8,128)S(1)}, f32[256,600]{0,1:T(8,128)S(1)}, u32[]{:S(2)}, u32[]{:S(2)}) collective-permute-start(f32[256,600]{0,1:T(8,128)S(1)} %copy.17), channel_id=1, source_target_pairs={{0,2},{2,0},{1,3},{3,1},{4,6},{6,4},{5,7},{7,5},{8,10},{10,8},{9,1... | collective-permute-start | bytes 1843208 | tf_op jit(solution)/shard_map/ppermute | solution.py:57
  140.7 4.9 %collective-permute-start.1 = (f32[44,600]{1,0:T(8,128)S(1)}, f32[44,600]{1,0:T(8,128)S(1)}, u32[]{:S(2)}, u32[]{:S(2)}) collective-permute-start(f32[44,600]{1,0:T(8,128)S(1)} %fusion.4), channel_id=1, source_target_pairs={{0,2},{2,0},{1,3},{3,1},{4,6},{6,4},{5,7},{7,5},{8,10},{10,8},{9,1... | collective-permute-start | bytes 316808 | tf_op jit(solution)/shard_map/ppermute | solution.py:57
Sparse Core Ops, SparseCore 0:
  12.1 101.8 all-gather.1

commit v19 on v18

--- a/solution.py
+++ b/solution.py
@@ -48,7 +48,7 @@
             preferred_element_type=jnp.float32,
         )
         pieces.append(exchange_sum(previous, "aux", n_aux))
-    return jnp.concatenate(pieces, axis=0)
+    return pieces
 
 
 def exchange_sum(value, axis, size):
@@ -58,26 +58,51 @@
     return total
 
 
-def gamma_kernel(amp_ref, owned_ref, out_ref):
-    out_ref[:, 0, :] = lax.dot_general(
-        amp_ref[...], owned_ref[...], (((1,), (1,)), ((), ())), preferred_element_type=jnp.float32
-    )
+def gamma_kernel(*refs):
+    n_pieces = (len(refs) - 3) // 2
+    owner_ref, owned_ref, out_ref = refs[-3], refs[-2], refs[-1]
+    first = 0
+    for index in range(n_pieces):
+        coupling_ref, energy_ref = refs[2 * index], refs[2 * index + 1]
+        amplitude = (
+            os_scale * coupling_ref[...] / (energy_ref[...] + owner_ref[...])
+        ).astype(jnp.bfloat16)
+        last = first + coupling_ref.shape[0]
+        out_ref[first:last, 0, :] = lax.dot_general(
+            amplitude, owned_ref[...], (((1,), (1,)), ((), ())),
+            preferred_element_type=jnp.float32,
+        )
+        first = last
 
 
-def gamma_rows_last(amplitude, owned_all):
-    width, depth = amplitude.shape
+def gamma_rows_last(pieces, energy_mine, owner_energy, owned_all):
+    width = energy_mine.shape[0]
+    depth = owner_energy.shape[0]
     rows = owned_all.shape[0]
     block = ROW_BLOCK if rows % ROW_BLOCK == 0 else rows
+    operands = []
+    in_specs = []
+    first = 0
+    for piece in pieces:
+        last = first + piece.shape[0]
+        operands += [piece, energy_mine[first:last, None]]
+        in_specs += [
+            pl.BlockSpec(piece.shape, lambda i: (0, 0)),
+            pl.BlockSpec((last - first, 1), lambda i: (0, 0)),
+        ]
+        first = last
+    operands += [owner_energy[None, :], owned_all]
+    in_specs += [
+        pl.BlockSpec((1, depth), lambda i: (0, 0)),
+        pl.BlockSpec((block, depth), lambda i: (i, 0)),
+    ]
     out = pl.pallas_call(
         gamma_kernel,
         out_shape=jax.ShapeDtypeStruct((width, 1, rows), jnp.float32),
         grid=(rows // block,),
-        in_specs=[
-            pl.BlockSpec((width, depth), lambda i: (0, 0)),
-            pl.BlockSpec((block, depth), lambda i: (i, 0)),
-        ],
+        in_specs=in_specs,
         out_specs=pl.BlockSpec((width, 1, block), lambda i: (0, 0, i)),
-    )(amplitude, owned_all)
+    )(*operands)
     return out.transpose(1, 2, 0)
 
 
@@ -91,12 +116,10 @@
     owned_all = lax.all_gather(owned, COLS, axis=0, tiled=True)
     if by_partials:
         coupling = coupling_by_partials(local, owned, shards, width)
-        coupling = exchange_sum(coupling, "aux", n_aux)
+        pieces = [exchange_sum(coupling, "aux", n_aux)]
     else:
-        coupling = coupling_by_columns(local, owned_all, shards, width, n_aux)
-    denominator = energy_mine[:, None] + owner_energy[None, :]
-    amplitude = (os_scale * coupling / denominator).astype(jnp.bfloat16)
-    return gamma_rows_last(amplitude, owned_all)
+        pieces = coupling_by_columns(local, owned_all, shards, width, n_aux)
+    return gamma_rows_last(pieces, energy_mine, owner_energy, owned_all)
 
 
 def solution(mesh):

time: 160 us -> 161 us (level)
  waiting for transfers between devices: 103 us -> 100 us
  local copies, waits for them, and re-layouts: 11.7 us -> 13.8 us
    ppermute x2, waiting for transfers between devices: 3 us -> 0.04 us  [exchange_sum(): lax.ppermute(value, axis, [(i, (i + step) % size) for i in range(size)])]
    broadcast_in_dim x0 -> x5, local copies, waits for them, and re-layouts: none -> 2.09 us  [the longest x4 1.52 us: gamma_rows_last(): operands += [piece, energy_mine[first:last, None]]]
  transfers between devices with their start and end apart: 5 -> 5, of which waited for: 3 -> 2; matrix products, arithmetic and copies ran while one was open for 8% -> 9% of each run, Pallas kernels for 0% -> 0%
where the time goes in v19:
time: 161 us
  waiting for transfers between devices  100 us (62%)
  between operations  15.5 us (10%)
  local copies, waits for them, and re-layouts  13.8 us (9%)
  starting transfers between devices  12.9 us (8%)
  matrix products  7.73 us (5%)
  Pallas kernels  7.41 us (5%)
  other arithmetic  2.78 us (2%)
    all_to_all x2, waiting for transfers between devices, coupling_by_columns(): moved = lax.all_to_all(chunk, COLS, split_axis=0, concat_axis=0, tiled=True)  100 us
    all_to_all x2, starting transfers between devices, coupling_by_columns(): moved = lax.all_to_all(chunk, COLS, split_axis=0, concat_axis=0, tiled=True)  9.79 us
    dot_general x2, matrix products, coupling_by_columns(): lax.dot_general(moved.reshape(shards * rows, last - first), owned_all, ((...  7.73 us
    pallas_call x1, Pallas kernels, gamma_rows_last(): pl.pallas_call(gamma_kernel, out_shape=jax.ShapeDtypeStruct((width, 1, ro...  7.41 us
  transfers between devices with their start and end apart: 5, of which 2 were waited for; matrix products, arithmetic and copies ran while one was open for 9% of the time, Pallas kernels for 0%

profile of v19, /device:TPU:0, one launch (start us, length us, event | category | flops | bytes accessed | tf_op | source)
XLA Modules:
  0.0 160.5 jit_solution(11342004652920889014)
XLA Ops:
  6.5 1.3 fusion.1
  9.2 1.2 constant_dynamic-slice_fusion.1
  10.4 0.2 copy.16
  10.6 0.2 copy.17
  10.8 1.1 pad_maximum_fusion
  11.9 0.0 all-gather.2.cloned.1.call-update
  11.9 2.6 %reshape_squeeze.3 = bf16[512,8,300]{0,2,1:T(8,128)(2,1)S(1)} reshape(bf16[1,512,2400]{1,2,0:T(8,128)(2,1)} %param.4) | data formatting | bytes 4915200 | tf_op jit(solution)/shard_map/reshape;squeeze | solution.py:36
  14.6 1.5 slice.26
  16.1 6.3 %all-to-all-start = ((bf16[8,512,256]{1,2,0:T(8,128)(2,1)}), bf16[8,512,256]{1,2,0:T(8,128)(2,1)}, u32[]{:S(2)}, u32[]{:S(2)}) async-start(bf16[8,512,256]{1,2,0:T(8,128)(2,1)} %slice.26), calls=%async_computation | async-start | bytes 4194304 | tf_op jit(solution)/shard_map/all_to_all | solution.py:45
  22.4 0.8 slice.28
  23.9 89.8 %all-to-all-done = bf16[8,512,256]{1,2,0:T(8,128)(2,1)} async-done(((bf16[8,512,256]{1,2,0:T(8,128)(2,1)}), bf16[8,512,256]{1,2,0:T(8,128)(2,1)}, u32[]{:S(2)}, u32[]{:S(2)}) %all-to-all-start) | async-done | bytes 2097184 | tf_op jit(solution)/shard_map/all_to_all | solution.py:45
  113.7 2.8 %copy.18 = bf16[8,512,256]{2,1,0:T(8,128)(2,1)S(1)} copy(bf16[8,512,256]{1,2,0:T(8,128)(2,1)} %all-to-all-done) | data formatting | bytes 4194304 | tf_op jit(solution)/shard_map/all_to_all | solution.py:45
  116.6 0.0 all-gather.2.cloned.1.call-done.refs_5_
  116.6 4.3 %convolution_bitcast_fusion = f32[256,600]{1,0:T(8,128)S(1)} fusion(bf16[4096,600]{1,0:T(8,128)(2,1)} %all-gather.2.cloned.1.call-done.refs_5_, bf16[4096,256]{1,0:T(8,128)(2,1)S(1)} %bitcast.30), kind=kOutput, calls=%fused_computation | convolution fusion | flops 1258291200 | bytes 7626752 | tf_op jit(solution)/shard_map/dot_general | solution.py:46
  120.9 3.5 %all-to-all-start.1 = ((bf16[8,512,44]{1,2,0:T(8,128)(2,1)}), bf16[8,512,44]{1,2,0:T(8,128)(2,1)S(1)}, u32[]{:S(2)}, u32[]{:S(2)}) async-start(bf16[8,512,44]{1,2,0:T(8,128)(2,1)} %slice.28), calls=%async_computation.1 | async-start | bytes 786432 | tf_op jit(solution)/shard_map/all_to_all | solution.py:45
  124.4 0.1 fusion
  124.5 0.2 copy.20
  124.8 1.6 collective-permute-start
  126.4 10.5 %all-to-all-done.1 = bf16[8,512,44]{1,2,0:T(8,128)(2,1)S(1)} async-done(((bf16[8,512,44]{1,2,0:T(8,128)(2,1)}), bf16[8,512,44]{1,2,0:T(8,128)(2,1)S(1)}, u32[]{:S(2)}, u32[]{:S(2)}) %all-to-all-start.1) | async-done | bytes 360480 | tf_op jit(solution)/shard_map/all_to_all | solution.py:45
  136.9 0.2 copy.28
  137.1 0.1 copy.26
  137.3 3.4 %fusion.2 = f32[44,600]{1,0:T(8,128)S(1)} fusion(bf16[4096,44]{0,1:T(8,128)(2,1)S(1)} %bitcast.32, bf16[4096,600]{1,0:T(8,128)(2,1)} %all-gather.2.cloned.1.call-done.refs_5_), kind=kOutput, calls=%fused_computation.11 | convolution fusion | flops 216268800 | bytes 5381248 | tf_op jit(solution)/shard_map/dot_general | solution.py:46
  140.7 1.6 collective-permute-start.1
  142.2 0.1 pad_maximum_fusion.1
  142.3 0.6 broadcast_in_dim.13.refs_4_
  142.9 0.7 copy.24.refs_3_
  143.6 0.8 copy.23.refs_1_
  144.4 0.2 copy.21
  144.6 0.9 add.22.refs_0_
  145.6 0.0 collective-permute-done.1
  145.6 0.7 add.25.refs_2_
  146.3 7.4 %shard_map.46 = f32[300,1,4096]{2,1,0:T(1,128)} custom-call(f32[256,600]{1,0:T(8,128)} %add.22.refs_0_, f32[256,1]{1,0:T(8,128)} %copy.23.refs_1_, f32[44,600]{1,0:T(8,128)} %add.25.refs_2_, f32[44,1]{1,0:T(8,128)} %copy.24.refs_3_, f32[1,600]{1,0:T(1,128)} %broadcast_in_dim.13.refs_4_, bf16[4096,600]{1,0:T(8,128)(2,1)} %all-gather.2.cloned.1.call-done.refs_5_), custom_call_target="tpu_custom_call" | custom-call | tf_op jit(solution)/shard_map/pallas_call | solution.py:99
  (9 shorter events, 0.1 us)
Async XLA Ops:
  6.5 110.1 %all-gather.2.cloned.1.call-start = ((), (), s32[]{:S(2)}) async-start(), calls=%async_computation.2 | async-start | bytes 5898240 | tf_op jit(solution)/shard_map/all_gather | solution.py:116
  16.1 97.6 %all-to-all-start = ((bf16[8,512,256]{1,2,0:T(8,128)(2,1)}), bf16[8,512,256]{1,2,0:T(8,128)(2,1)}, u32[]{:S(2)}, u32[]{:S(2)}) async-start(bf16[8,512,256]{1,2,0:T(8,128)(2,1)} %slice.26), calls=%async_computation | async-start | bytes 4194304 | tf_op jit(solution)/shard_map/all_to_all | solution.py:45
  116.6 7.8 %copy-start = (f32[2400]{0:T(1024)S(1)}, f32[2400]{0:T(1024)}, u32[]{:S(2)}) copy-start(f32[2400]{0:T(1024)} %param.6) | copy-start | bytes 28804
  120.9 15.9 %all-to-all-start.1 = ((bf16[8,512,44]{1,2,0:T(8,128)(2,1)}), bf16[8,512,44]{1,2,0:T(8,128)(2,1)S(1)}, u32[]{:S(2)}, u32[]{:S(2)}) async-start(bf16[8,512,44]{1,2,0:T(8,128)(2,1)} %slice.28), calls=%async_computation.1 | async-start | bytes 786432 | tf_op jit(solution)/shard_map/all_to_all | solution.py:45
  124.8 19.6 %collective-permute-start = (f32[256,600]{0,1:T(8,128)S(1)}, f32[256,600]{0,1:T(8,128)S(1)}, u32[]{:S(2)}, u32[]{:S(2)}) collective-permute-start(f32[256,600]{0,1:T(8,128)S(1)} %copy.20), channel_id=1, source_target_pairs={{0,2},{2,0},{1,3},{3,1},{4,6},{6,4},{5,7},{7,5},{8,10},{10,8},{9,1... | collective-permute-start | bytes 1843208 | tf_op jit(solution)/shard_map/ppermute | solution.py:57
  140.7 4.9 %collective-permute-start.1 = (f32[44,600]{1,0:T(8,128)S(1)}, f32[44,600]{1,0:T(8,128)S(1)}, u32[]{:S(2)}, u32[]{:S(2)}) collective-permute-start(f32[44,600]{1,0:T(8,128)S(1)} %fusion.2), channel_id=1, source_target_pairs={{0,2},{2,0},{1,3},{3,1},{4,6},{6,4},{5,7},{7,5},{8,10},{10,8},{9,1... | collective-permute-start | bytes 316808 | tf_op jit(solution)/shard_map/ppermute | solution.py:57
Sparse Core Ops, SparseCore 0:
  12.1 101.8 all-gather.1

commit v20 on v18

--- a/solution.py
+++ b/solution.py
@@ -43,12 +43,34 @@
         if previous is not None:
             chunk, _ = lax.optimization_barrier((chunk, previous))
         moved = lax.all_to_all(chunk, COLS, split_axis=0, concat_axis=0, tiled=True)
-        previous = lax.dot_general(
-            moved.reshape(shards * rows, last - first), owned_all, (((0,), (0,)), ((), ())),
-            preferred_element_type=jnp.float32,
-        )
+        previous = coupling_blocks(moved, owned_all)
         pieces.append(exchange_sum(previous, "aux", n_aux))
     return jnp.concatenate(pieces, axis=0)
+
+
+def coupling_kernel(moved_ref, owned_ref, out_ref):
+    @pl.when(pl.program_id(0) == 0)
+    def _():
+        out_ref[...] = jnp.zeros_like(out_ref)
+
+    out_ref[...] += lax.dot_general(
+        moved_ref[0], owned_ref[...], (((0,), (0,)), ((), ())), preferred_element_type=jnp.float32
+    )
+
+
+def coupling_blocks(moved, owned_all):
+    blocks, rows, width = moved.shape
+    depth = owned_all.shape[1]
+    return pl.pallas_call(
+        coupling_kernel,
+        out_shape=jax.ShapeDtypeStruct((width, depth), jnp.float32),
+        grid=(blocks,),
+        in_specs=[
+            pl.BlockSpec((1, rows, width), lambda i: (i, 0, 0)),
+            pl.BlockSpec((rows, depth), lambda i: (i, 0)),
+        ],
+        out_specs=pl.BlockSpec((width, depth), lambda i: (0, 0)),
+    )(moved, owned_all)
 
 
 def exchange_sum(value, axis, size):

time: 160 us -> 167 us (1.044)
  Pallas kernels: 5.95 us -> 20.4 us
  matrix products: 7.73 us -> 0 us
  local copies, waits for them, and re-layouts: 11.7 us -> 14.3 us
  waiting for transfers between devices: 103 us -> 101 us
    pallas_call x0 -> x2, Pallas kernels: none -> 14.5 us  [coupling_blocks(): pl.pallas_call(coupling_kernel, out_shape=jax.ShapeDtypeStruct((width, de...]
    dot_general x2 -> x0, matrix products: 7.73 us -> none  [coupling_by_columns(): lax.dot_general(moved.reshape(shards * rows, last - first), owned_all, ((...]
    all_to_all x2, waiting for transfers between devices: 100 us -> 97.4 us  [coupling_by_columns(): moved = lax.all_to_all(chunk, COLS, split_axis=0, concat_axis=0, tiled=True)]
    another operation x1 -> x2, local copies, waits for them, and re-layouts: 2.64 us -> 5.41 us  [coupling_by_columns(): blocked = local.reshape(rows, shards, width).transpose(1, 0, 2)]
    all_to_all x2 -> x1, local copies, waits for them, and re-layouts: 3.05 us -> 1.38 us  [coupling_by_columns(): moved = lax.all_to_all(chunk, COLS, split_axis=0, concat_axis=0, tiled=True)]
  transfers between devices with their start and end apart: 5 -> 5, of which waited for: 3 -> 3; matrix products, arithmetic and copies ran while one was open for 8% -> 6% of each run, Pallas kernels for 0% -> 4%
where the time goes in v20:
time: 167 us; the launch traced here: 166 us
  waiting for transfers between devices  101 us (60%)
  Pallas kernels  20.4 us (12%)
  between operations  15.4 us (9%)
  local copies, waits for them, and re-layouts  14.3 us (9%)
  starting transfers between devices  12.8 us (8%)
  other arithmetic  2.33 us (1%)
    all_to_all x2, waiting for transfers between devices, coupling_by_columns(): moved = lax.all_to_all(chunk, COLS, split_axis=0, concat_axis=0, tiled=True)  97.4 us
    pallas_call x2, Pallas kernels, coupling_blocks(): pl.pallas_call(coupling_kernel, out_shape=jax.ShapeDtypeStruct((width, de...  14.5 us
    all_to_all x2, starting transfers between devices, coupling_by_columns(): moved = lax.all_to_all(chunk, COLS, split_axis=0, concat_axis=0, tiled=True)  9.78 us
    pallas_call x1, Pallas kernels, gamma_rows_last(): pl.pallas_call(gamma_kernel, out_shape=jax.ShapeDtypeStruct((width, 1, ro...  5.95 us
    another operation x2, local copies, waits for them, and re-layouts, coupling_by_columns(): blocked = local.reshape(rows, shards, width).transpose(1, 0, 2)  5.41 us
  transfers between devices with their start and end apart: 5, of which 3 were waited for; matrix products, arithmetic and copies ran while one was open for 6% of the time, Pallas kernels for 4%

profile of v20, /device:TPU:0, one launch (start us, length us, event | category | flops | bytes accessed | tf_op | source)
XLA Modules:
  0.0 165.9 jit_solution(15516819676748022872)
XLA Ops:
  6.5 0.0 all-gather.2.cloned.1.call-start
  6.5 1.4 fusion.3
  9.3 1.2 constant_dynamic-slice_fusion.1
  10.5 0.2 copy.12
  10.7 0.2 copy.11
  10.9 1.1 pad_maximum_fusion
  12.1 0.0 all-gather.2.cloned.1.call-update
  12.1 0.0 copy-done.2
  12.1 2.1 %reshape_squeeze.3 = bf16[512,8,300]{0,2,1:T(8,128)(2,1)} reshape(bf16[1,512,2400]{1,2,0:T(8,128)(2,1)S(1)} %copy-done.2) | data formatting | bytes 4915200 | tf_op jit(solution)/shard_map/reshape;squeeze | solution.py:36
  14.2 3.3 %copy.10 = bf16[512,8,300]{2,0,1:T(8,128)(2,1)S(1)} copy(bf16[512,8,300]{0,2,1:T(8,128)(2,1)} %reshape_squeeze.3) | data formatting | bytes 4915200 | tf_op jit(solution)/shard_map/reshape;squeeze | solution.py:36
  17.5 1.5 slice.16
  19.0 6.3 %all-to-all-start = ((bf16[8,512,256]{2,1,0:T(8,128)(2,1)}), bf16[8,512,256]{2,1,0:T(8,128)(2,1)}, u32[]{:S(2)}, u32[]{:S(2)}) async-start(bf16[8,512,256]{2,1,0:T(8,128)(2,1)} %slice.16), calls=%async_computation | async-start | bytes 4194304 | tf_op jit(solution)/shard_map/all_to_all | solution.py:45
  25.3 1.2 slice.17
  26.5 87.5 %all-to-all-done.moved_ref = bf16[8,512,256]{2,1,0:T(8,128)(2,1)} async-done(((bf16[8,512,256]{2,1,0:T(8,128)(2,1)}), bf16[8,512,256]{2,1,0:T(8,128)(2,1)}, u32[]{:S(2)}, u32[]{:S(2)}) %all-to-all-start) | async-done | bytes 2097184 | tf_op jit(solution)/shard_map/all_to_all | solution.py:45
  114.0 7.8 %shard_map.46 = f32[256,600]{1,0:T(8,128)} custom-call(bf16[8,512,256]{2,1,0:T(8,128)(2,1)} %all-to-all-done.moved_ref, bf16[4096,600]{1,0:T(8,128)(2,1)} %all-gather.2.cloned.1.call-done.owned_ref), custom_call_target="tpu_custom_call" | custom-call | tf_op jit(solution)/shard_map/pallas_call | solution.py:64
  121.7 0.0 copy-done.1
  121.8 1.2 copy.15
  123.0 3.5 %all-to-all-start.1 = ((bf16[8,512,44]{1,2,0:T(8,128)(2,1)}), bf16[8,512,44]{1,2,0:T(8,128)(2,1)S(1)}, u32[]{:S(2)}, u32[]{:S(2)}) async-start(bf16[8,512,44]{1,2,0:T(8,128)(2,1)} %copy.15), calls=%async_computation.1 | async-start | bytes 786432 | tf_op jit(solution)/shard_map/all_to_all | solution.py:45
  126.4 0.2 copy.13
  126.7 1.5 collective-permute-start
  128.9 0.1 fusion.2
  129.0 9.9 %all-to-all-done.1 = bf16[8,512,44]{1,2,0:T(8,128)(2,1)S(1)} async-done(((bf16[8,512,44]{1,2,0:T(8,128)(2,1)}), bf16[8,512,44]{1,2,0:T(8,128)(2,1)S(1)}, u32[]{:S(2)}, u32[]{:S(2)}) %all-to-all-start.1) | async-done | bytes 360480 | tf_op jit(solution)/shard_map/all_to_all | solution.py:45
  138.9 1.4 copy.16.moved_ref
  140.3 6.7 %shard_map.47 = f32[44,600]{1,0:T(8,128)} custom-call(bf16[8,512,44]{2,1,0:T(8,128)(2,1)} %copy.16.moved_ref, bf16[4096,600]{1,0:T(8,128)(2,1)} %all-gather.2.cloned.1.call-done.owned_ref), custom_call_target="tpu_custom_call" | custom-call | tf_op jit(solution)/shard_map/pallas_call | solution.py:64
  147.0 1.5 collective-permute-start.1
  148.5 0.1 pad_maximum_fusion.1
  148.5 0.0 collective-permute-done
  148.5 0.2 copy.14
  148.8 0.1 add.35
  148.9 3.2 %collective-permute-done.1 = f32[44,600]{1,0:T(8,128)S(1)} collective-permute-done((f32[44,600]{1,0:T(8,128)}, f32[44,600]{1,0:T(8,128)S(1)}, u32[]{:S(2)}, u32[]{:S(2)}) %collective-permute-start.1) | collective-permute-done | bytes 105632 | tf_op jit(solution)/shard_map/ppermute | solution.py:79
  152.1 1.0 fusion.1.amp_ref
  153.1 6.0 %shard_map.48 = f32[300,1,4096]{2,1,0:T(1,128)} custom-call(bf16[300,600]{1,0:T(8,128)(2,1)} %fusion.1.amp_ref, bf16[4096,600]{1,0:T(8,128)(2,1)} %all-gather.2.cloned.1.call-done.owned_ref), custom_call_target="tpu_custom_call" | custom-call | tf_op jit(solution)/shard_map/pallas_call | solution.py:93
  (11 shorter events, 0.0 us)
Async XLA Ops:
  6.5 5.6 %copy-start.2 = (bf16[1,512,2400]{1,2,0:T(8,128)(2,1)S(1)}, bf16[1,512,2400]{1,2,0:T(8,128)(2,1)}, u32[]{:S(2)}) copy-start(bf16[1,512,2400]{1,2,0:T(8,128)(2,1)} %param.4) | copy-start | bytes 7372804
  6.5 107.4 %all-gather.2.cloned.1.call-start = ((), (), s32[]{:S(2)}) async-start(), calls=%async_computation.2 | async-start | bytes 5898240 | tf_op jit(solution)/shard_map/all_gather | solution.py:113
  19.0 95.0 %all-to-all-start = ((bf16[8,512,256]{2,1,0:T(8,128)(2,1)}), bf16[8,512,256]{2,1,0:T(8,128)(2,1)}, u32[]{:S(2)}, u32[]{:S(2)}) async-start(bf16[8,512,256]{2,1,0:T(8,128)(2,1)} %slice.16), calls=%async_computation | async-start | bytes 4194304 | tf_op jit(solution)/shard_map/all_to_all | solution.py:45
  26.5 95.2 %copy-start.1 = (bf16[8,512,44]{2,1,0:T(8,128)(2,1)S(1)}, bf16[8,512,44]{2,1,0:T(8,128)(2,1)}, u32[]{:S(2)}) copy-start(bf16[8,512,44]{2,1,0:T(8,128)(2,1)} %slice.17) | copy-start | bytes 1081348
  121.7 4.7 %copy-start = (f32[256,600]{1,0:T(8,128)S(1)}, f32[256,600]{1,0:T(8,128)}, u32[]{:S(2)}) copy-start(f32[256,600]{1,0:T(8,128)} %shard_map.46) | copy-start | bytes 1843204
  121.7 7.1 %copy-start.4 = (f32[2400]{0:T(1024)S(1)}, f32[2400]{0:T(1024)}, u32[]{:S(2)}) copy-start(f32[2400]{0:T(1024)} %param.6) | copy-start | bytes 28804
  123.0 15.9 %all-to-all-start.1 = ((bf16[8,512,44]{1,2,0:T(8,128)(2,1)}), bf16[8,512,44]{1,2,0:T(8,128)(2,1)S(1)}, u32[]{:S(2)}, u32[]{:S(2)}) async-start(bf16[8,512,44]{1,2,0:T(8,128)(2,1)} %copy.15), calls=%async_computation.1 | async-start | bytes 786432 | tf_op jit(solution)/shard_map/all_to_all | solution.py:45
  126.7 21.9 %collective-permute-start = (f32[256,600]{0,1:T(8,128)S(1)}, f32[256,600]{0,1:T(8,128)S(1)}, u32[]{:S(2)}, u32[]{:S(2)}) collective-permute-start(f32[256,600]{0,1:T(8,128)S(1)} %copy.13), channel_id=1, source_target_pairs={{0,2},{2,0},{1,3},{3,1},{4,6},{6,4},{5,7},{7,5},{8,10},{10,8},{9,1... | collective-permute-start | bytes 1843208 | tf_op jit(solution)/shard_map/ppermute | solution.py:79
  147.0 5.1 %copy-start.3 = (f32[44,600]{1,0:T(8,128)S(1)}, f32[44,600]{1,0:T(8,128)}, u32[]{:S(2)}) copy-start(f32[44,600]{1,0:T(8,128)} %shard_map.47) | copy-start | bytes 316804
  147.0 5.1 %collective-permute-start.1 = (f32[44,600]{1,0:T(8,128)}, f32[44,600]{1,0:T(8,128)S(1)}, u32[]{:S(2)}, u32[]{:S(2)}) collective-permute-start(f32[44,600]{1,0:T(8,128)} %shard_map.47), channel_id=1, source_target_pairs={{0,2},{2,0},{1,3},{3,1},{4,6},{6,4},{5,7},{7,5},{8,10},{10,8},{9,1... | collective-permute-start | bytes 316808 | tf_op jit(solution)/shard_map/ppermute | solution.py:79
Sparse Core Ops, SparseCore 0:
  12.2 100.9 all-gather.1

commit v21 on v18

--- a/solution.py
+++ b/solution.py
@@ -9,7 +9,7 @@
 COLS = ("col", "rep")
 PARTIAL_BYTES_MAX = 0
 LANES = 128
-ROW_BLOCK = 2048
+ROW_BLOCK = 4096
 
 
 def owner_columns(local, col_energy, owners, width):

time: 160 us -> 162 us (1.012)
  Pallas kernels: 5.95 us -> 7.57 us
    pallas_call x1, Pallas kernels: 5.95 us -> 7.57 us  [gamma_rows_last(): pl.pallas_call(gamma_kernel, out_shape=jax.ShapeDtypeStruct((width, 1, ro...]
where the time goes in v21:
time: 162 us; the launch traced here: 161 us
  waiting for transfers between devices  103 us (64%)
  between operations  15.5 us (10%)
  starting transfers between devices  12.9 us (8%)
  local copies, waits for them, and re-layouts  11.7 us (7%)
  matrix products  7.73 us (5%)
  Pallas kernels  7.57 us (5%)
  other arithmetic  2.23 us (1%)
    all_to_all x2, waiting for transfers between devices, coupling_by_columns(): moved = lax.all_to_all(chunk, COLS, split_axis=0, concat_axis=0, tiled=True)  100 us
    all_to_all x2, starting transfers between devices, coupling_by_columns(): moved = lax.all_to_all(chunk, COLS, split_axis=0, concat_axis=0, tiled=True)  9.79 us
    dot_general x2, matrix products, coupling_by_columns(): lax.dot_general(moved.reshape(shards * rows, last - first), owned_all, ((...  7.73 us
    pallas_call x1, Pallas kernels, gamma_rows_last(): pl.pallas_call(gamma_kernel, out_shape=jax.ShapeDtypeStruct((width, 1, ro...  7.57 us
  transfers between devices with their start and end apart: 5, of which 3 were waited for; matrix products, arithmetic and copies ran while one was open for 8% of the time, Pallas kernels for 0%

profile of v21, /device:TPU:0, one launch (start us, length us, event | category | flops | bytes accessed | tf_op | source)
XLA Modules:
  0.0 161.0 jit_solution(7861873992886398455)
XLA Ops:
  6.5 0.0 all-gather.2.cloned.1.call-start
  6.5 1.3 fusion.3
  9.2 1.2 constant_dynamic-slice_fusion.1
  10.4 0.2 copy.13
  10.6 0.2 copy.14
  10.8 1.1 pad_maximum_fusion
  11.9 0.0 all-gather.2.cloned.1.call-update
  11.9 2.6 %reshape_squeeze.3 = bf16[512,8,300]{0,2,1:T(8,128)(2,1)S(1)} reshape(bf16[1,512,2400]{1,2,0:T(8,128)(2,1)} %param.4) | data formatting | bytes 4915200 | tf_op jit(solution)/shard_map/reshape;squeeze | solution.py:36
  14.6 1.5 slice.16
  16.1 6.3 %all-to-all-start = ((bf16[8,512,256]{1,2,0:T(8,128)(2,1)}), bf16[8,512,256]{1,2,0:T(8,128)(2,1)}, u32[]{:S(2)}, u32[]{:S(2)}) async-start(bf16[8,512,256]{1,2,0:T(8,128)(2,1)} %slice.16), calls=%async_computation | async-start | bytes 4194304 | tf_op jit(solution)/shard_map/all_to_all | solution.py:45
  22.4 0.8 slice.17
  23.2 90.5 %all-to-all-done = bf16[8,512,256]{1,2,0:T(8,128)(2,1)} async-done(((bf16[8,512,256]{1,2,0:T(8,128)(2,1)}), bf16[8,512,256]{1,2,0:T(8,128)(2,1)}, u32[]{:S(2)}, u32[]{:S(2)}) %all-to-all-start) | async-done | bytes 2097184 | tf_op jit(solution)/shard_map/all_to_all | solution.py:45
  113.7 2.8 %copy.15 = bf16[8,512,256]{2,1,0:T(8,128)(2,1)S(1)} copy(bf16[8,512,256]{1,2,0:T(8,128)(2,1)} %all-to-all-done) | data formatting | bytes 4194304 | tf_op jit(solution)/shard_map/all_to_all | solution.py:45
  116.6 0.0 all-gather.2.cloned.1.call-done.owned_ref
  116.6 0.0 copy-start
  116.6 4.3 %convolution_bitcast_fusion = f32[256,600]{1,0:T(8,128)S(1)} fusion(bf16[4096,600]{1,0:T(8,128)(2,1)} %all-gather.2.cloned.1.call-done.owned_ref, bf16[4096,256]{1,0:T(8,128)(2,1)S(1)} %bitcast.26), kind=kOutput, calls=%fused_computation | convolution fusion | flops 1258291200 | bytes 7626752 | tf_op jit(solution)/shard_map/dot_general | solution.py:46
  120.9 3.5 %all-to-all-start.1 = ((bf16[8,512,44]{1,2,0:T(8,128)(2,1)}), bf16[8,512,44]{1,2,0:T(8,128)(2,1)S(1)}, u32[]{:S(2)}, u32[]{:S(2)}) async-start(bf16[8,512,44]{1,2,0:T(8,128)(2,1)} %slice.17), calls=%async_computation.1 | async-start | bytes 786432 | tf_op jit(solution)/shard_map/all_to_all | solution.py:45
  125.1 0.2 copy.17
  125.3 1.6 collective-permute-start
  126.9 0.1 fusion.2
  127.0 9.9 %all-to-all-done.1 = bf16[8,512,44]{1,2,0:T(8,128)(2,1)S(1)} async-done(((bf16[8,512,44]{1,2,0:T(8,128)(2,1)}), bf16[8,512,44]{1,2,0:T(8,128)(2,1)S(1)}, u32[]{:S(2)}, u32[]{:S(2)}) %all-to-all-start.1) | async-done | bytes 360480 | tf_op jit(solution)/shard_map/all_to_all | solution.py:45
  136.9 0.2 copy.23
  137.1 0.1 copy.21
  137.3 3.4 %fusion.4 = f32[44,600]{1,0:T(8,128)S(1)} fusion(bf16[4096,44]{0,1:T(8,128)(2,1)S(1)} %bitcast.28, bf16[4096,600]{1,0:T(8,128)(2,1)} %all-gather.2.cloned.1.call-done.owned_ref), kind=kOutput, calls=%fused_computation.12 | convolution fusion | flops 216268800 | bytes 5381248 | tf_op jit(solution)/shard_map/dot_general | solution.py:46
  140.7 1.6 collective-permute-start.1
  142.2 0.1 pad_maximum_fusion.1
  142.3 0.0 collective-permute-done
  142.3 0.2 copy.18
  142.5 0.1 add.35
  142.6 3.0 %collective-permute-done.1 = f32[44,600]{1,0:T(8,128)S(1)} collective-permute-done((f32[44,600]{1,0:T(8,128)S(1)}, f32[44,600]{1,0:T(8,128)S(1)}, u32[]{:S(2)}, u32[]{:S(2)}) %collective-permute-start.1) | collective-permute-done | bytes 105632 | tf_op jit(solution)/shard_map/ppermute | solution.py:57
  145.6 1.0 fusion.1.amp_ref
  146.6 7.6 %shard_map.46 = f32[300,1,4096]{2,1,0:T(1,128)} custom-call(bf16[300,600]{1,0:T(8,128)(2,1)} %fusion.1.amp_ref, bf16[4096,600]{1,0:T(8,128)(2,1)} %all-gather.2.cloned.1.call-done.owned_ref), custom_call_target="tpu_custom_call" | custom-call | tf_op jit(solution)/shard_map/pallas_call | solution.py:71
  (4 shorter events, 0.1 us)
Async XLA Ops:
  6.5 110.1 %all-gather.2.cloned.1.call-start = ((), (), s32[]{:S(2)}) async-start(), calls=%async_computation.2 | async-start | bytes 5898240 | tf_op jit(solution)/shard_map/all_gather | solution.py:91
  16.1 97.6 %all-to-all-start = ((bf16[8,512,256]{1,2,0:T(8,128)(2,1)}), bf16[8,512,256]{1,2,0:T(8,128)(2,1)}, u32[]{:S(2)}, u32[]{:S(2)}) async-start(bf16[8,512,256]{1,2,0:T(8,128)(2,1)} %slice.16), calls=%async_computation | async-start | bytes 4194304 | tf_op jit(solution)/shard_map/all_to_all | solution.py:45
  116.6 8.5 %copy-start = (f32[2400]{0:T(1024)S(1)}, f32[2400]{0:T(1024)}, u32[]{:S(2)}) copy-start(f32[2400]{0:T(1024)} %param.6) | copy-start | bytes 28804
  120.9 15.9 %all-to-all-start.1 = ((bf16[8,512,44]{1,2,0:T(8,128)(2,1)}), bf16[8,512,44]{1,2,0:T(8,128)(2,1)S(1)}, u32[]{:S(2)}, u32[]{:S(2)}) async-start(bf16[8,512,44]{1,2,0:T(8,128)(2,1)} %slice.17), calls=%async_computation.1 | async-start | bytes 786432 | tf_op jit(solution)/shard_map/all_to_all | solution.py:45
  125.3 17.0 %collective-permute-start = (f32[256,600]{0,1:T(8,128)S(1)}, f32[256,600]{0,1:T(8,128)S(1)}, u32[]{:S(2)}, u32[]{:S(2)}) collective-permute-start(f32[256,600]{0,1:T(8,128)S(1)} %copy.17), channel_id=1, source_target_pairs={{0,2},{2,0},{1,3},{3,1},{4,6},{6,4},{5,7},{7,5},{8,10},{10,8},{9,1... | collective-permute-start | bytes 1843208 | tf_op jit(solution)/shard_map/ppermute | solution.py:57
  140.7 4.9 %collective-permute-start.1 = (f32[44,600]{1,0:T(8,128)S(1)}, f32[44,600]{1,0:T(8,128)S(1)}, u32[]{:S(2)}, u32[]{:S(2)}) collective-permute-start(f32[44,600]{1,0:T(8,128)S(1)} %fusion.4), channel_id=1, source_target_pairs={{0,2},{2,0},{1,3},{3,1},{4,6},{6,4},{5,7},{7,5},{8,10},{10,8},{9,1... | collective-permute-start | bytes 316808 | tf_op jit(solution)/shard_map/ppermute | solution.py:57
Sparse Core Ops, SparseCore 0:
  12.1 101.8 all-gather.1
